TPU v7x, 128 devices: a whole 4x4x4 slice. The times are simulated.
128 devices in a mesh: seq: 16 (over z, x), exp: 8 (over y, core).
Axes of the slice: x: 4, y: 4, z: 4, core: 2. Of those that a mesh axis runs over, the one named last changes fastest.
Arguments:
- residual_in: bfloat16 [8, 4096, 2048], P('exp', 'seq'), may hold values from -6 to 6
- query_matrix: bfloat16 [8, 4096, 2048], P('exp', 'seq'), may hold values from -6 to 6
- key_vectors: bfloat16 [8, 4096, 2048], P('exp', 'seq'), may hold values from -6 to 6
- value_vectors: bfloat16 [8, 4096, 2048], P('exp', 'seq'), may hold values from -6 to 6
- head_gain: float32 [2048], replicated, may hold values from 0.5 to 1.5
- norm_gain: float32 [2048], replicated, may hold values from 0.5 to 1.5
- expert_ids: int32 [8, 4096, 4], P('exp', 'seq'), may hold values from 0 to 7, all different within a row; in each aligned block of 256 rows (0 to 255, 256 to 511, ..., all dimensions but the last counted through in order) at most 192 rows name the same one
- gate_probs: float32 [8, 4096, 4], P('exp', 'seq'), may hold values from 0.25 to 1
- w_gate: bfloat16 [8, 2048, 1408], P('exp'), may hold values from -0.125 to 0.125
- w_up: bfloat16 [8, 2048, 1408], P('exp'), may hold values from -0.125 to 0.125
- w_down: bfloat16 [8, 1408, 2048], P('exp'), may hold values from -0.15625 to 0.15625
Outputs:
- layer_out: bfloat16 [8, 4096, 2048], P('exp', 'seq')
Inputs may be any that keep to these rules, and one draw needn't show every extreme that they name: `expert_ids`: the 4 experts of one position differ; among the 256 positions of one device, no expert is named by more than 192 routes.
All inputs are finite; a program needn't handle non-finite values.
Results may differ from a plain program's by a relative error of at most 0.013.
Values may be sent and summed in bfloat16 or wider, within the bound.
No kernel may reach another device: no remote copies, remote signals or barrier semaphores. Data moves between devices by JAX's collectives and lax.ppermute only.
A program may use at most 128 MiB of HBM per device.

v0:
```python
import jax
import jax.numpy as jnp
from jax import lax
from jax.sharding import PartitionSpec as P

D = 2048
HEADS = 16
HD = 128
TOP = 4
EXPERTS = 8
CAP = 192


def on_device(
    residual_in,
    query_matrix,
    key_vectors,
    value_vectors,
    head_gain,
    norm_gain,
    expert_ids,
    gate_probs,
    w_gate,
    w_up,
    w_down,
):
    positions = residual_in.shape[1]
    queries = query_matrix[0].reshape(positions, HEADS, HD)
    key_rows = key_vectors[0].reshape(positions, HEADS, HD)
    value_rows = value_vectors[0].reshape(positions, HEADS, HD)
    state = jnp.einsum("thd,the->hde", key_rows, value_rows, preferred_element_type=jnp.float32)
    my_index = lax.axis_index("seq")
    piece = lax.all_gather(state[None], "seq", axis=0, tiled=True)
    owners = jnp.arange(piece.shape[0], dtype=jnp.int32)
    earlier = owners < my_index
    prefix = jnp.sum(jnp.where(earlier[:, None, None, None], piece, 0.0), axis=0)
    causal = jnp.tril(jnp.ones((positions, positions), dtype=bool))
    scores = jnp.einsum("thd,uhd->htu", queries, key_rows, preferred_element_type=jnp.float32)
    weights = jnp.where(causal[None], scores, 0.0).astype(jnp.bfloat16)
    inner = jnp.einsum("htu,uhd->thd", weights, value_rows, preferred_element_type=jnp.float32)
    outer_product = jnp.einsum(
        "thd,hde->the", queries, prefix.astype(jnp.bfloat16), preferred_element_type=jnp.float32
    )
    mixed = inner + outer_product
    mean_square = jnp.mean(mixed * mixed, axis=-1, keepdims=True)
    attn = (mixed * lax.rsqrt(mean_square + 1e-06)).reshape(positions, D) * head_gain
    resid_float = (
        (residual_in[0].astype(jnp.float32) + attn).astype(jnp.bfloat16).astype(jnp.float32)
    )
    row_square = jnp.mean(resid_float * resid_float, axis=-1, keepdims=True)
    normed = (resid_float * lax.rsqrt(row_square + 1e-06) * norm_gain).astype(jnp.bfloat16)
    route_ids = expert_ids[0].reshape(-1)
    route_gates = gate_probs[0]
    expert_indicator = (route_ids[:, None] == jnp.arange(EXPERTS, dtype=jnp.int32)[None, :]).astype(
        jnp.int32
    )
    slots = jnp.sum(
        (jnp.cumsum(expert_indicator, axis=0) - expert_indicator) * expert_indicator, axis=1
    )
    target = route_ids * CAP + slots
    token_of = jnp.arange(positions * TOP, dtype=jnp.int32) // TOP
    outgoing = (
        jnp.zeros((EXPERTS * CAP, D), jnp.bfloat16)
        .at[target]
        .set(normed[token_of])
        .reshape(EXPERTS, CAP, D)
    )
    local_count = w_gate.shape[0]
    groups = EXPERTS // local_count
    block = lax.all_to_all(outgoing, "exp", split_axis=0, concat_axis=0, tiled=True)
    count = block.shape[1]
    grouped = block.reshape(groups, local_count, count, D)
    gate_part = jnp.einsum("gend,edf->genf", grouped, w_gate, preferred_element_type=jnp.float32)
    up_part = jnp.einsum("gend,edf->genf", grouped, w_up, preferred_element_type=jnp.float32)
    hidden = (jax.nn.silu(gate_part) * up_part).astype(jnp.bfloat16)
    result = jnp.einsum("genf,efd->gend", hidden, w_down, preferred_element_type=jnp.float32)
    result = result.astype(jnp.bfloat16).reshape(EXPERTS, count, D)
    returned = lax.all_to_all(result, "exp", split_axis=0, concat_axis=0, tiled=True)
    picked = returned.reshape(EXPERTS * CAP, D)[target].reshape(positions, TOP, D)
    combined = jnp.sum(picked.astype(jnp.float32) * route_gates[:, :, None], axis=1)
    return (resid_float + combined).astype(jnp.bfloat16)[None]


def solution(mesh):
    in_specs = (
        P("exp", "seq", None),
        P("exp", "seq", None),
        P("exp", "seq", None),
        P("exp", "seq", None),
        P(),
        P(),
        P("exp", "seq", None),
        P("exp", "seq", None),
        P("exp", None, None),
        P("exp", None, None),
        P("exp", None, None),
    )
    out_specs = P("exp", "seq", None)
    return jax.shard_map(
        on_device, mesh=mesh, in_specs=in_specs, out_specs=out_specs, check_vma=False
    )
```

profile of v0, /device:TPU:1, one launch (start us, length us, event | category | flops | bytes accessed | tf_op | source)
XLA Modules:
  0.0 405.5 jit_solution(9483026792404834334)
XLA Ops:
  6.5 0.0 copy-start.5
  6.5 0.0 all-gather.3.cloned.1.call-start
  6.5 1.5 copy.43
  8.0 1.5 copy.45
  9.5 1.4 fusion.30
  10.9 0.0 all-gather.3.cloned.1.call-update
  11.0 0.0 copy-done.5
  11.0 0.1 copy.38
  11.1 0.1 eq.29
  11.2 0.1 eq.25
  11.4 1.5 copy.44
  12.8 2.3 reduce-window.6
  15.1 0.3 slice_reduce_fusion
  15.4 0.2 reduce-window.9
  15.5 0.1 copy.37
  15.7 0.1 mul.92
  15.9 0.1 add_bitcast_fusion
  16.0 2.7 fusion.28
  18.7 106.7 %all-gather.3.cloned.1.call-done = f32[256,128,128]{2,1,0:T(8,128)} async-done(((f32[16,128,128]{2,1,0:T(8,128)}), f32[256,128,128]{2,1,0:T(8,128)}) %all-gather.3.cloned.1.call-update) | async-done | bytes 16777232 | tf_op jit(solution)/shard_map/all_gather | solution.py:33
  125.5 0.0 copy-start.3
  125.5 8.9 %select_reduce_fusion = bf16[16,128,128]{2,1,0:T(8,128)(2,1)} fusion(f32[16,16,128,128]{3,2,1,0:T(8,128)} %bitcast.112, pred[16]{0:T(512)(128)(4,1)S(1)} %iota_compare_fusion.3), kind=kLoop, calls=%fused_computation.3 | loop fusion | flops 8126464 | bytes 17301520 | tf_op jit(solution)/shard_map/reduce_sum | solution.py:36
  134.4 0.0 copy-done.3
  134.4 1.6 multiply_reduce_fusion.1
  136.1 0.0 copy-start.2
  136.1 0.0 copy-start.4
  136.1 0.2 broadcast_multiply_fusion
  136.3 0.0 copy-start.6
  136.3 1.9 copy.40
  138.2 0.0 copy-done.2
  138.2 0.0 copy-done.4
  138.2 2.1 fusion.24
  140.3 0.0 copy-done.6
  140.3 1.3 fusion.26
  141.6 23.1 %scatter_custom_fusion = bf16[1536,2048]{1,0:T(8,128)(2,1)} fusion(s32[1024]{0:T(1024)S(1)} %bitcast.122, bf16[256,2048]{1,0:T(8,128)(2,1)} %fusion.26, s32[1024]{0:T(1024)S(1)} %broadcast_clamp_fusion.1, bf16[]{:T(256)} %constant.44.clone.1), kind=kCustom, calls=%fused_computation.20 | custom fusion | bytes 6291968 | tf_op jit(solution)/shard_map/scatter | solution.py:65
  164.8 76.4 %all_to_all.10 = bf16[8,192,2048]{2,1,0:T(8,128)(2,1)S(1)} all-to-all(bf16[8,192,2048]{2,1,0:T(8,128)(2,1)} %bitcast.109), channel_id=1, replica_groups=mesh['seq'=16,'exp'=8] {'exp'}, dimensions={0} | all-to-all | bytes 12582912 | tf_op jit(solution)/shard_map/all_to_all | solution.py:70
  241.2 0.0 copy-start.1
  241.2 2.6 copy-done.1
  243.7 13.4 %fusion.6 = f32[8,192,1408]{2,1,0:T(8,128)} fusion(bf16[8,192,2048]{2,1,0:T(8,128)(2,1)S(1)} %all_to_all.10, bf16[1,2048,1408]{2,1,0:T(8,128)(2,1)} %param.20), kind=kOutput, calls=%fused_computation.14 | convolution fusion | flops 8858370048 | bytes 20709376 | tf_op jit(solution)/shard_map/gend,edf->genf/dot_general | solution.py:74
  257.1 28.7 %fusion.9 = bf16[8,192,2048]{2,1,0:T(8,128)(2,1)} fusion(bf16[1,1408,2048]{2,1,0:T(8,128)(2,1)} %param.21, f32[8,192,1408]{2,1,0:T(8,128)} %fusion.6, bf16[8,192,2048]{2,1,0:T(8,128)(2,1)} %copy-done.1, bf16[1,2048,1408]{2,1,0:T(8,128)(2,1)} %param.19), kind=kOutput, calls=%fused_computation.17 | convolution fusion | flops 17732861952 | bytes 32768000 | tf_op jit(solution)/shard_map/genf,efd->gend/dot_general | solution.py:76
  285.8 0.0 copy-start.7
  285.8 6.0 %all-to-all-start.1 = ((bf16[8,192,2048]{2,1,0:T(8,128)(2,1)}), bf16[8,192,2048]{2,1,0:T(8,128)(2,1)}, u32[]{:S(2)}, u32[]{:S(2)}) async-start(bf16[8,192,2048]{2,1,0:T(8,128)(2,1)} %fusion.9), calls=%async_computation.1 | async-start | bytes 12582912 | tf_op jit(solution)/shard_map/all_to_all | solution.py:78
  291.9 0.0 copy-done.7
  291.9 0.1 copy.41
  292.0 1.8 copy.36
  293.8 69.2 %all-to-all-done.1 = bf16[8,192,2048]{2,1,0:T(8,128)(2,1)} async-done(((bf16[8,192,2048]{2,1,0:T(8,128)(2,1)}), bf16[8,192,2048]{2,1,0:T(8,128)(2,1)}, u32[]{:S(2)}, u32[]{:S(2)}) %all-to-all-start.1) | async-done | bytes 6291488 | tf_op jit(solution)/shard_map/all_to_all | solution.py:78
  363.1 12.4 %gather_fusion = bf16[1024,2048]{1,0:T(8,128)(2,1)} fusion(bf16[1536,2048]{1,0:T(8,128)(2,1)} %bitcast.26, s32[1024]{0:T(1024)S(1)} %broadcast_clamp_fusion), kind=kCustom, calls=%fused_computation.1 | custom fusion | bytes 8392704 | tf_op jit(solution)/shard_map/gather | solution.py:79
  375.5 8.3 %reshape.198 = f32[256,4,2048]{2,1,0:T(4,128)} reshape(bf16[1024,2048]{1,0:T(8,128)(2,1)} %gather_fusion) | data formatting | bytes 12582912 | tf_op jit(solution)/shard_map/convert_element_type | solution.py:80
  383.8 0.0 copy-start
  383.8 11.5 %multiply_reduce_fusion = f32[256,2048]{1,0:T(8,128)} fusion(f32[256,4,2048]{2,1,0:T(4,128)} %reshape.198, f32[256,4]{1,0:T(8,128)S(1)} %copy.41), kind=kLoop, calls=%fused_computation.11 | loop fusion | flops 3670016 | bytes 10489856 | tf_op jit(solution)/shard_map/reduce_sum | solution.py:80
  395.3 0.0 copy-done
  395.3 3.1 fusion.27
  (11 shorter events, 0.1 us)
Async XLA Ops:
  6.5 4.4 %copy-start.5 = (s32[1,256,4]{1,2,0:T(4,128)S(1)}, s32[1,256,4]{1,2,0:T(4,128)}, u32[]{:S(2)}) copy-start(s32[1,256,4]{1,2,0:T(4,128)} %param.17) | copy-start | bytes 12292
  6.5 119.0 %all-gather.3.cloned.1.call-start = ((), (), s32[]{:S(2)}) async-start(), calls=%async_computation.2 | async-start | bytes 17825792 | tf_op jit(solution)/shard_map/all_gather | solution.py:33
  125.5 9.0 %copy-start.3 = (f32[16,256,128]{1,2,0:T(8,128)S(1)}, f32[16,256,128]{1,2,0:T(8,128)}, u32[]{:S(2)}) copy-start(f32[16,256,128]{1,2,0:T(8,128)} %fusion.28) | copy-start | bytes 6291460
  136.1 2.1 copy-start.2
  136.1 2.1 copy-start.4
  136.3 4.0 copy-start.6
  241.2 2.6 copy-start.1
  285.8 6.0 %copy-start.7 = (f32[1,256,4]{1,2,0:T(4,128)S(1)}, f32[1,256,4]{1,2,0:T(4,128)}, u32[]{:S(2)}) copy-start(f32[1,256,4]{1,2,0:T(4,128)} %param.18) | copy-start | bytes 12292
  285.8 77.3 %all-to-all-start.1 = ((bf16[8,192,2048]{2,1,0:T(8,128)(2,1)}), bf16[8,192,2048]{2,1,0:T(8,128)(2,1)}, u32[]{:S(2)}, u32[]{:S(2)}) async-start(bf16[8,192,2048]{2,1,0:T(8,128)(2,1)} %fusion.9), calls=%async_computation.1 | async-start | bytes 12582912 | tf_op jit(solution)/shard_map/all_to_all | solution.py:78
  383.8 11.5 %copy-start = (f32[1,256,2048]{2,1,0:T(8,128)S(1)}, f32[1,256,2048]{2,1,0:T(8,128)}, u32[]{:S(2)}) copy-start(f32[1,256,2048]{2,1,0:T(8,128)} %copy.36) | copy-start | bytes 6291460
Sparse Core Ops, SparseCore 0:
  11.1 114.3 all-gather.2
where the time goes:
time: 412 us; the launch traced here: 405 us
  waiting for transfers between devices  176 us (43%)
  blocking collectives  76.4 us (19%)
  local copies, waits for them, and re-layouts  55.6 us (13%)
  matrix products  47.8 us (12%)
  other arithmetic  29.7 us (7%)
  between operations  13.8 us (3%)
  starting transfers between devices  6.04 us (1%)
    all_gather x1, waiting for transfers between devices, on_device(): piece = lax.all_gather(state[None], 'seq', axis=0, tiled=True)  107 us
    all_to_all x1, blocking collectives, on_device(): lax.all_to_all(outgoing, 'exp', split_axis=0, concat_axis=0, tiled=True)  76.4 us
    all_to_all x1, waiting for transfers between devices, on_device(): lax.all_to_all(result, 'exp', split_axis=0, concat_axis=0, tiled=True)  69.2 us
    dot_general x1, matrix products, on_device(): jnp.einsum('genf,efd->gend', hidden, w_down, preferred_element_type=jnp.f...  28.7 us
    scatter x1, local copies, waits for them, and re-layouts, on_device(): outgoing = jnp.zeros((EXPERTS * CAP, D), jnp.bfloat16).at[target].set(nor...  23.1 us
    dot_general x1, matrix products, on_device(): jnp.einsum('gend,edf->genf', grouped, w_up, preferred_element_type=jnp.fl...  13.4 us
    gather x1, local copies, waits for them, and re-layouts, on_device(): returned.reshape(EXPERTS * CAP, D)[target].reshape(positions, TOP, D)  12.4 us
    reduce_sum x1, other arithmetic, on_device(): jnp.sum(picked.astype(jnp.float32) * route_gates[:, :, None], axis=1)  11.5 us
  transfers between devices with their start and end apart: 2, of which 2 were waited for; matrix products, arithmetic and copies ran while one was open for 2% of the time, Pallas kernels for 0%

commit v1 on v0

v1 whole, which is shorter than its diff:
```python
import jax
import jax.numpy as jnp
from jax import lax
from jax.sharding import PartitionSpec as P

D = 2048
HEADS = 16
HD = 128
TOP = 4
EXPERTS = 8


def block_prefix(state):
    blocks = lax.axis_size("seq")
    pieces = state.reshape(blocks, -1)
    gathered = lax.all_to_all(pieces, "seq", split_axis=0, concat_axis=0, tiled=True)
    running = jnp.zeros_like(gathered[0])
    sums = []
    for j in range(blocks):
        sums.append(running)
        running = running + gathered[j]
    prefixes = jnp.stack(sums).astype(jnp.bfloat16)
    mine = lax.all_to_all(prefixes, "seq", split_axis=0, concat_axis=0, tiled=True)
    return mine.reshape(state.shape)


def on_device(
    residual_in,
    query_matrix,
    key_vectors,
    value_vectors,
    head_gain,
    norm_gain,
    expert_ids,
    gate_probs,
    w_gate,
    w_up,
    w_down,
):
    positions = residual_in.shape[1]
    queries = query_matrix[0].reshape(positions, HEADS, HD)
    key_rows = key_vectors[0].reshape(positions, HEADS, HD)
    value_rows = value_vectors[0].reshape(positions, HEADS, HD)
    state = jnp.einsum("thd,the->hde", key_rows, value_rows, preferred_element_type=jnp.float32)
    prefix = block_prefix(state)
    causal = jnp.tril(jnp.ones((positions, positions), dtype=bool))
    scores = jnp.einsum("thd,uhd->htu", queries, key_rows, preferred_element_type=jnp.float32)
    weights = jnp.where(causal[None], scores, 0.0).astype(jnp.bfloat16)
    inner = jnp.einsum("htu,uhd->thd", weights, value_rows, preferred_element_type=jnp.float32)
    outer_product = jnp.einsum(
        "thd,hde->the", queries, prefix, preferred_element_type=jnp.float32
    )
    mixed = inner + outer_product
    mean_square = jnp.mean(mixed * mixed, axis=-1, keepdims=True)
    attn = (mixed * lax.rsqrt(mean_square + 1e-06)).reshape(positions, D) * head_gain
    resid_float = (
        (residual_in[0].astype(jnp.float32) + attn).astype(jnp.bfloat16).astype(jnp.float32)
    )
    row_square = jnp.mean(resid_float * resid_float, axis=-1, keepdims=True)
    normed = (resid_float * lax.rsqrt(row_square + 1e-06) * norm_gain).astype(jnp.bfloat16)

    route_ids = expert_ids[0]
    route_gates = gate_probs[0]
    experts = jnp.arange(EXPERTS, dtype=jnp.int32)
    table = jnp.sum(
        jnp.where(route_ids[:, :, None] == experts[None, None, :], route_gates[:, :, None], 0.0),
        axis=1,
    )
    local_count = w_gate.shape[0]
    rows = lax.all_gather(normed, "exp", axis=0, tiled=True)
    all_table = lax.all_gather(table, "exp", axis=0, tiled=True)
    first = lax.axis_index("exp") * local_count
    local_weights = lax.dynamic_slice_in_dim(all_table, first, local_count, axis=1)
    gate_part = jnp.einsum("nd,edf->enf", rows, w_gate, preferred_element_type=jnp.float32)
    up_part = jnp.einsum("nd,edf->enf", rows, w_up, preferred_element_type=jnp.float32)
    hidden = (jax.nn.silu(gate_part) * up_part).astype(jnp.bfloat16)
    result = jnp.einsum("enf,efd->end", hidden, w_down, preferred_element_type=jnp.float32)
    result = result.astype(jnp.bfloat16).astype(jnp.float32)
    contrib = jnp.sum(result * local_weights.T[:, :, None], axis=0).astype(jnp.bfloat16)
    combined = lax.psum_scatter(contrib, "exp", scatter_dimension=0, tiled=True)
    return (resid_float + combined.astype(jnp.float32)).astype(jnp.bfloat16)[None]


def solution(mesh):
    in_specs = (
        P("exp", "seq", None),
        P("exp", "seq", None),
        P("exp", "seq", None),
        P("exp", "seq", None),
        P(),
        P(),
        P("exp", "seq", None),
        P("exp", "seq", None),
        P("exp", None, None),
        P("exp", None, None),
        P("exp", None, None),
    )
    out_specs = P("exp", "seq", None)
    return jax.shard_map(
        on_device, mesh=mesh, in_specs=in_specs, out_specs=out_specs, check_vma=False
    )
```

time: 412 us -> 248 us (0.60); the launches traced: 405 us -> 247 us
  waiting for transfers between devices: 176 us -> 106 us
  blocking collectives: 76.4 us -> 16.4 us
  local copies, waits for them, and re-layouts: 55.6 us -> 11.7 us
  matrix products: 47.8 us -> 60.9 us
  starting transfers between devices: 6.04 us -> 12.9 us
  other arithmetic: 29.7 us -> 25.4 us
    all_to_all x1 -> x0, blocking collectives: 76.4 us -> none  [on_device(): lax.all_to_all(outgoing, 'exp', split_axis=0, concat_axis=0, tiled=True)]
    all_gather x1, waiting for transfers between devices: 107 us -> 34.1 us  [on_device(): rows = lax.all_gather(normed, 'exp', axis=0, tiled=True)]
    reduce_scatter x0 -> x1, waiting for transfers between devices: none -> 51.8 us  [on_device(): combined = lax.psum_scatter(contrib, 'exp', scatter_dimension=0, tiled=True)]
    all_to_all x1 -> x2, waiting for transfers between devices: 69.2 us -> 20.3 us  [the longest x1 15.4 us: block_prefix(): lax.all_to_all(pieces, 'seq', split_axis=0, concat_axis=0, tiled=True)]
    scatter x1 -> x0, local copies, waits for them, and re-layouts: 23.1 us -> none  [on_device(): outgoing = jnp.zeros((EXPERTS * CAP, D), jnp.bfloat16).at[target].set(nor...]
    reduce_sum x3 -> x1, other arithmetic: 20.5 us -> 0.01 us  [on_device(): jnp.sum(jnp.where(route_ids[:, :, None] == experts[None, None, :], route_...]
    all_gather x0 -> x1, blocking collectives: none -> 16.4 us  [on_device(): all_table = lax.all_gather(table, 'exp', axis=0, tiled=True)]
    dot_general x3, matrix products: 43.7 us -> 56.8 us  [the longest x1 36 us: on_device(): jnp.einsum('enf,efd->end', hidden, w_down, preferred_element_type=jnp.flo...]
  transfers between devices with their start and end apart: 2 -> 4, of which waited for: 2 -> 4; matrix products, arithmetic and copies ran while one was open for 2% -> 2% of each run, Pallas kernels for 0% -> 0%
where the time goes in v1:
time: 248 us; the launch traced here: 247 us
  waiting for transfers between devices  106 us (43%)
  matrix products  60.9 us (25%)
  other arithmetic  25.4 us (10%)
  blocking collectives  16.4 us (7%)
  between operations  13.6 us (5%)
  starting transfers between devices  12.9 us (5%)
  local copies, waits for them, and re-layouts  11.7 us (5%)
    reduce_scatter x1, waiting for transfers between devices, on_device(): combined = lax.psum_scatter(contrib, 'exp', scatter_dimension=0, tiled=True)  51.8 us
    dot_general x1, matrix products, on_device(): jnp.einsum('enf,efd->end', hidden, w_down, preferred_element_type=jnp.flo...  36 us
    all_gather x1, waiting for transfers between devices, on_device(): rows = lax.all_gather(normed, 'exp', axis=0, tiled=True)  34.1 us
    dot_general x1, matrix products, on_device(): jnp.einsum('nd,edf->enf', rows, w_gate, preferred_element_type=jnp.float32)  18.6 us
    all_gather x1, blocking collectives, on_device(): all_table = lax.all_gather(table, 'exp', axis=0, tiled=True)  16.4 us
    all_to_all x1, waiting for transfers between devices, block_prefix(): lax.all_to_all(pieces, 'seq', split_axis=0, concat_axis=0, tiled=True)  15.4 us
    unnamed x13, other arithmetic  9.37 us
    all_to_all x1, starting transfers between devices, block_prefix(): lax.all_to_all(pieces, 'seq', split_axis=0, concat_axis=0, tiled=True)  8.42 us
  transfers between devices with their start and end apart: 4, of which 4 were waited for; matrix products, arithmetic and copies ran while one was open for 2% of the time, Pallas kernels for 0%

profile of v1, /device:TPU:1, one launch (start us, length us, event | category | flops | bytes accessed | tf_op | source)
XLA Modules:
  0.0 247.2 jit_solution(10188754233409415296)
XLA Ops:
  6.5 1.5 copy.48
  8.0 1.5 copy.50
  9.5 1.4 fusion.19
  10.9 8.4 %all-to-all-start = ((f32[16,1,16384]{2,1,0:T(1,128)}), f32[16,1,16384]{2,1,0:T(1,128)S(1)}, u32[]{:S(2)}, u32[]{:S(2)}) async-start(f32[16,1,16384]{2,1,0:T(1,128)} %bitcast.81), calls=%async_computation | async-start | bytes 2097152 | tf_op jit(solution)/shard_map/all_to_all | solution.py:16
  19.3 0.7 constant_dynamic-update-slice_fusion
  20.0 15.4 %all-to-all-done = f32[16,1,16384]{2,1,0:T(1,128)S(1)} async-done(((f32[16,1,16384]{2,1,0:T(1,128)}), f32[16,1,16384]{2,1,0:T(1,128)S(1)}, u32[]{:S(2)}, u32[]{:S(2)}) %all-to-all-start) | async-done | bytes 1048608 | tf_op jit(solution)/shard_map/all_to_all | solution.py:16
  35.4 0.7 convert_dynamic-update-slice_fusion.13
  36.1 0.7 convert_dynamic-update-slice_fusion.12
  36.8 0.7 convert_dynamic-update-slice_fusion.11
  37.5 0.8 convert_dynamic-update-slice_fusion.10
  38.2 0.7 convert_dynamic-update-slice_fusion.9
  38.9 0.7 convert_dynamic-update-slice_fusion.8
  39.7 0.7 convert_dynamic-update-slice_fusion.7
  40.4 0.7 convert_dynamic-update-slice_fusion.6
  41.1 0.7 convert_dynamic-update-slice_fusion.5
  41.8 0.7 convert_dynamic-update-slice_fusion.4
  42.6 0.7 convert_dynamic-update-slice_fusion.3
  43.3 0.7 convert_dynamic-update-slice_fusion.2
  44.0 0.7 convert_dynamic-update-slice_fusion.1
  44.7 0.7 convert_dynamic-update-slice_fusion
  45.4 0.7 fusion.25
  46.2 0.5 broadcast.38
  46.7 4.9 %reduce.1 = bf16[16,16384]{1,0:T(8,128)(2,1)S(1)} reduce(bf16[16,1,16384]{2,1,0:T(2,128)(2,1)} %fusion.25, bf16[]{:T(256)} %broadcast.38), dimensions={1}, to_apply=%fusion.25.reduce_sub_computation | reduce | bytes 1048578 | tf_op jit(solution)/shard_map/stack | solution.py:22
  51.6 1.2 reshape.397
  52.8 4.3 %all-to-all-start.1 = ((bf16[16,2,8192]{2,1,0:T(2,128)(2,1)}), bf16[16,2,8192]{2,1,0:T(2,128)(2,1)}, u32[]{:S(2)}, u32[]{:S(2)}) async-start(bf16[16,2,8192]{2,1,0:T(2,128)(2,1)} %reshape.397), calls=%async_computation.1 | async-start | bytes 1048576 | tf_op jit(solution)/shard_map/all_to_all | solution.py:23
  57.1 0.2 all-gather.2.cloned.1.call-start
  57.3 1.5 copy.49
  58.8 2.7 %fusion.16 = f32[16,256,128]{1,2,0:T(8,128)} fusion(bf16[256,16,128]{0,2,1:T(8,128)(2,1)S(1)} %bitcast.78, pred[256,256]{1,0:T(8,128)(4,1)S(1)} %iota_compare_fusion, bf16[256,16,128]{2,1,0:T(8,128)(2,1)S(1)} %bitcast.80, bf16[256,16,128]{2,1,0:T(8,128)(2,1)S(1)} %bitcast.82), kind=kOutput, calls=%fused_computation.26 | convolution fusion | flops 538968064 | bytes 5308416 | tf_op jit(solution)/shard_map/htu,uhd->thd/dot_general | solution.py:49
  61.5 5.0 %all-to-all-done.1 = bf16[16,2,8192]{2,1,0:T(2,128)(2,1)} async-done(((bf16[16,2,8192]{2,1,0:T(2,128)(2,1)}), bf16[16,2,8192]{2,1,0:T(2,128)(2,1)}, u32[]{:S(2)}, u32[]{:S(2)}) %all-to-all-start.1) | async-done | bytes 524320 | tf_op jit(solution)/shard_map/all_to_all | solution.py:23
  66.4 2.2 reshape.398
  68.7 3.1 %reduce = bf16[16,16384]{1,0:T(8,128)(2,1)S(1)} reduce(bf16[16,1,16384]{2,1,0:T(2,128)(2,1)S(1)} %reshape.398, bf16[]{:T(256)} %constant.37), dimensions={1}, to_apply=%all_to_all.12.reduce_sub_computation | reduce | bytes 1048578 | tf_op jit(solution)/shard_map/all_to_all | solution.py:23
  71.8 0.1 copy.51
  71.9 0.0 copy-start
  71.9 2.2 multiply_reduce_fusion
  74.1 0.0 copy-start.1
  74.1 1.6 broadcast_multiply_fusion
  75.7 0.0 copy-start.2
  75.7 0.0 copy-start.3
  75.7 1.9 copy.46
  77.7 0.0 copy-done
  77.7 1.7 fusion.11
  79.4 0.0 copy-done.1
  79.4 1.3 fusion.13
  80.7 0.0 all-gather.2.cloned.1.call-update
  80.7 0.0 reduce-scatter.2.cloned.1.call-start
  80.8 0.0 copy-done.2
  80.8 0.0 copy-done.3
  80.8 16.4 %all_gather.7 = f32[2048,8]{0,1:T(8,128)S(1)} all-gather(f32[256,8]{0,1:T(8,128)S(1)} %select_reduce_fusion), channel_id=1, replica_groups=mesh['seq'=16,'exp'=8] {'exp'}, dimensions={0}, use_global_device_ids=true | all-gather | bytes 73728 | tf_op jit(solution)/shard_map/all_gather | solution.py:71
  97.3 34.1 %all-gather.2.cloned.1.call-done = bf16[2048,2048]{1,0:T(8,128)(2,1)} async-done(((bf16[256,2048]{1,0:T(8,128)(2,1)}), bf16[2048,2048]{1,0:T(8,128)(2,1)}) %all-gather.2.cloned.1.call-update) | async-done | bytes 8388624 | tf_op jit(solution)/shard_map/all_gather | solution.py:70
  131.3 18.6 %fusion.8 = f32[2048,1408]{1,0:T(8,128)} fusion(bf16[2048,2048]{1,0:T(8,128)(2,1)} %all-gather.2.cloned.1.call-done, bf16[1,2048,1408]{2,1,0:T(8,128)(2,1)} %param.19), kind=kOutput, calls=%fused_computation.11 | convolution fusion | flops 11811160064 | bytes 25690112 | tf_op jit(solution)/shard_map/nd,edf->enf/dot_general | solution.py:74
  149.9 36.0 %multiply_convert_fusion = bf16[2048,2048]{1,0:T(8,128)(2,1)} fusion(f32[2048]{0:T(1024)S(1)} %bitcast.88, bf16[1,1408,2048]{2,1,0:T(8,128)(2,1)} %param.21, bf16[2048,2048]{1,0:T(8,128)(2,1)} %all-gather.2.cloned.1.call-done, f32[2048,1408]{1,0:T(8,128)} %fusion.8, bf16[1,2048,1408]{2,1,0:T(8,128)(2,1)} %param.20), kind=kOutput, calls=%fused_computation | convolution fusion | flops 23656398848 | bytes 39854080 | tf_op jit(solution)/shard_map/enf,efd->end/dot_general | solution.py:77
  186.0 0.0 reduce-scatter.2.cloned.1.call-update
  186.0 51.8 %reduce-scatter.2.cloned.1.call-done = bf16[256,2048]{1,0:T(8,128)(2,1)} async-done(((bf16[2048,2048]{1,0:T(8,128)(2,1)}), bf16[256,2048]{1,0:T(8,128)(2,1)}) %reduce-scatter.2.cloned.1.call-update) | async-done | bytes 1048592 | tf_op jit(solution)/shard_map/reduce_scatter | solution.py:80
  237.8 2.6 %fusion.17 = bf16[1,256,2048]{2,1,0:T(8,128)(2,1)} fusion(bf16[256,2048]{1,0:T(8,128)(2,1)} %reduce-scatter.2.cloned.1.call-done, bf16[256,2048]{1,0:T(8,128)(2,1)S(1)} %get-tuple-element.6), kind=kLoop, calls=%fused_computation.27 | loop fusion | flops 2097152 | bytes 3145728 | tf_op jit(solution)/shard_map/broadcast_in_dim | solution.py:81
  (5 shorter events, 0.1 us)
Async XLA Ops:
  10.9 24.5 %all-to-all-start = ((f32[16,1,16384]{2,1,0:T(1,128)}), f32[16,1,16384]{2,1,0:T(1,128)S(1)}, u32[]{:S(2)}, u32[]{:S(2)}) async-start(f32[16,1,16384]{2,1,0:T(1,128)} %bitcast.81), calls=%async_computation | async-start | bytes 2097152 | tf_op jit(solution)/shard_map/all_to_all | solution.py:16
  52.8 13.6 %all-to-all-start.1 = ((bf16[16,2,8192]{2,1,0:T(2,128)(2,1)}), bf16[16,2,8192]{2,1,0:T(2,128)(2,1)}, u32[]{:S(2)}, u32[]{:S(2)}) async-start(bf16[16,2,8192]{2,1,0:T(2,128)(2,1)} %reshape.397), calls=%async_computation.1 | async-start | bytes 1048576 | tf_op jit(solution)/shard_map/all_to_all | solution.py:23
  57.1 74.3 %all-gather.2.cloned.1.call-start = ((), (), s32[]{:S(2)}) async-start(), calls=%async_computation.3 | async-start | bytes 9437184 | tf_op jit(solution)/shard_map/all_gather | solution.py:70
  71.9 5.8 %copy-start = (f32[2048]{0:T(1024)S(1)}, f32[2048]{0:T(1024)}, u32[]{:S(2)}) copy-start(f32[2048]{0:T(1024)} %param.15) | copy-start | bytes 24580
  74.1 5.3 %copy-start.1 = (f32[2048]{0:T(1024)S(1)}, f32[2048]{0:T(1024)}, u32[]{:S(2)}) copy-start(f32[2048]{0:T(1024)} %param.16) | copy-start | bytes 24580
  75.7 5.1 %copy-start.2 = (f32[1,256,4]{1,2,0:T(4,128)S(1)}, f32[1,256,4]{1,2,0:T(4,128)}, u32[]{:S(2)}) copy-start(f32[1,256,4]{1,2,0:T(4,128)} %param.18) | copy-start | bytes 12292
  75.7 5.1 %copy-start.3 = (s32[1,256,4]{1,2,0:T(4,128)S(1)}, s32[1,256,4]{1,2,0:T(4,128)}, u32[]{:S(2)}) copy-start(s32[1,256,4]{1,2,0:T(4,128)} %param.17) | copy-start | bytes 12292
  80.7 157.0 %reduce-scatter.2.cloned.1.call-start = ((), (), s32[]{:S(2)}) async-start(), calls=%async_computation.4 | async-start | bytes 9437184 | tf_op jit(solution)/shard_map/reduce_scatter | solution.py:80
Sparse Core Ops, SparseCore 0:
  80.9 50.4 all-gather.1
  186.1 51.6 reduce-scatter.1

commit v2 on v1

--- a/solution.py
+++ b/solution.py
@@ -8,18 +8,15 @@
 HD = 128
 TOP = 4
 EXPERTS = 8
+CHUNKS = 2
 
 
 def block_prefix(state):
     blocks = lax.axis_size("seq")
     pieces = state.reshape(blocks, -1)
     gathered = lax.all_to_all(pieces, "seq", split_axis=0, concat_axis=0, tiled=True)
-    running = jnp.zeros_like(gathered[0])
-    sums = []
-    for j in range(blocks):
-        sums.append(running)
-        running = running + gathered[j]
-    prefixes = jnp.stack(sums).astype(jnp.bfloat16)
+    shifted = jnp.concatenate([jnp.zeros_like(gathered[:1]), gathered[:-1]], axis=0)
+    prefixes = lax.cumsum(shifted, axis=0).astype(jnp.bfloat16)
     mine = lax.all_to_all(prefixes, "seq", split_axis=0, concat_axis=0, tiled=True)
     return mine.reshape(state.shape)
 
@@ -66,18 +63,27 @@
         jnp.where(route_ids[:, :, None] == experts[None, None, :], route_gates[:, :, None], 0.0),
         axis=1,
     )
+    groups = lax.axis_size("exp")
+    me = lax.axis_index("exp")
+    slots = jnp.where((jnp.arange(groups) == me)[:, None, None], table[None], 0.0)
+    all_table = lax.psum(slots, "exp")
     local_count = w_gate.shape[0]
-    rows = lax.all_gather(normed, "exp", axis=0, tiled=True)
-    all_table = lax.all_gather(table, "exp", axis=0, tiled=True)
-    first = lax.axis_index("exp") * local_count
-    local_weights = lax.dynamic_slice_in_dim(all_table, first, local_count, axis=1)
-    gate_part = jnp.einsum("nd,edf->enf", rows, w_gate, preferred_element_type=jnp.float32)
-    up_part = jnp.einsum("nd,edf->enf", rows, w_up, preferred_element_type=jnp.float32)
-    hidden = (jax.nn.silu(gate_part) * up_part).astype(jnp.bfloat16)
-    result = jnp.einsum("enf,efd->end", hidden, w_down, preferred_element_type=jnp.float32)
-    result = result.astype(jnp.bfloat16).astype(jnp.float32)
-    contrib = jnp.sum(result * local_weights.T[:, :, None], axis=0).astype(jnp.bfloat16)
-    combined = lax.psum_scatter(contrib, "exp", scatter_dimension=0, tiled=True)
+    local_weights = lax.dynamic_slice_in_dim(all_table, me * local_count, local_count, axis=2)
+
+    chunk = positions // CHUNKS
+    outs = []
+    for c in range(CHUNKS):
+        part = normed[c * chunk:(c + 1) * chunk]
+        rows = lax.all_gather(part, "exp", axis=0, tiled=True)
+        weight = local_weights[:, c * chunk:(c + 1) * chunk].reshape(groups * chunk, local_count)
+        gate_part = jnp.einsum("nd,edf->enf", rows, w_gate, preferred_element_type=jnp.float32)
+        up_part = jnp.einsum("nd,edf->enf", rows, w_up, preferred_element_type=jnp.float32)
+        hidden = (jax.nn.silu(gate_part) * up_part).astype(jnp.bfloat16)
+        result = jnp.einsum("enf,efd->end", hidden, w_down, preferred_element_type=jnp.float32)
+        result = result.astype(jnp.bfloat16).astype(jnp.float32)
+        contrib = jnp.sum(result * weight.T[:, :, None], axis=0).astype(jnp.bfloat16)
+        outs.append(lax.psum_scatter(contrib, "exp", scatter_dimension=0, tiled=True))
+    combined = jnp.concatenate(outs, axis=0)
     return (resid_float + combined.astype(jnp.float32)).astype(jnp.bfloat16)[None]
 
 

time: 248 us -> 271 us (1.093)
  waiting for transfers between devices: 106 us -> 138 us
  blocking collectives: 16.4 us -> 0 us
  matrix products: 60.9 us -> 72.1 us
  other arithmetic: 25.4 us -> 16.2 us
  local copies, waits for them, and re-layouts: 11.7 us -> 15 us
    psum x0 -> x1, waiting for transfers between devices: none -> 40.4 us  [on_device(): all_table = lax.psum(slots, 'exp')]
    all_gather x1 -> x0, blocking collectives: 16.4 us -> none  [on_device(): all_table = lax.all_gather(table, 'exp', axis=0, tiled=True)]
    reduce_scatter x1 -> x2, waiting for transfers between devices: 51.8 us -> 41.2 us  [on_device(): lax.psum_scatter(contrib, 'exp', scatter_dimension=0, tiled=True)]
    unnamed x13 -> x0, other arithmetic: 9.37 us -> none
    dot_general x1 -> x2, matrix products: 36 us -> 42.3 us  [on_device(): jnp.einsum('enf,efd->end', hidden, w_down, preferred_element_type=jnp.flo...]
    dot_general x1 -> x2, matrix products: 18.6 us -> 23.5 us  [on_device(): jnp.einsum('nd,edf->enf', rows, w_up, preferred_element_type=jnp.float32)]
    convert_element_type x0 -> x1, other arithmetic: none -> 3.25 us  [on_device(): (resid_float + combined.astype(jnp.float32)).astype(jnp.bfloat16)[None]]
    all_gather x1 -> x2, waiting for transfers between devices: 34.1 us -> 35.2 us  [on_device(): rows = lax.all_gather(part, 'exp', axis=0, tiled=True)]
  transfers between devices with their start and end apart: 4 -> 7, of which waited for: 4 -> 7; matrix products, arithmetic and copies ran while one was open for 2% -> 32% of each run, Pallas kernels for 0% -> 0%
where the time goes in v2:
time: 271 us; the launch traced here: 268 us
  waiting for transfers between devices  138 us (51%)
  matrix products  72.1 us (27%)
  other arithmetic  16.2 us (6%)
  local copies, waits for them, and re-layouts  15 us (6%)
  starting transfers between devices  13.6 us (5%)
  between operations  13.4 us (5%)
    dot_general x2, matrix products, on_device(): jnp.einsum('enf,efd->end', hidden, w_down, preferred_element_type=jnp.flo...  42.3 us
    reduce_scatter x2, waiting for transfers between devices, on_device(): lax.psum_scatter(contrib, 'exp', scatter_dimension=0, tiled=True)  41.2 us
    psum x1, waiting for transfers between devices, on_device(): all_table = lax.psum(slots, 'exp')  40.4 us
    all_gather x2, waiting for transfers between devices, on_device(): rows = lax.all_gather(part, 'exp', axis=0, tiled=True)  35.2 us
    dot_general x2, matrix products, on_device(): jnp.einsum('nd,edf->enf', rows, w_up, preferred_element_type=jnp.float32)  23.5 us
    all_to_all x1, waiting for transfers between devices, block_prefix(): lax.all_to_all(pieces, 'seq', split_axis=0, concat_axis=0, tiled=True)  16 us
    all_to_all x1, starting transfers between devices, block_prefix(): lax.all_to_all(pieces, 'seq', split_axis=0, concat_axis=0, tiled=True)  8.47 us
    unnamed x15, local copies, waits for them, and re-layouts  7.48 us
  transfers between devices with their start and end apart: 7, of which 7 were waited for; matrix products, arithmetic and copies ran while one was open for 32% of the time, Pallas kernels for 0%

profile of v2, /device:TPU:1, one launch (start us, length us, event | category | flops | bytes accessed | tf_op | source)
XLA Modules:
  0.0 268.0 jit_solution(8376810459908882183)
XLA Ops:
  6.5 1.5 copy.42
  8.0 0.0 copy-start.3
  8.0 0.0 copy-start.4
  8.0 1.5 copy.44
  9.5 1.4 fusion.49
  10.9 8.5 %all-to-all-start = ((f32[16,1,16384]{2,1,0:T(1,128)}), f32[16,1,16384]{2,1,0:T(1,128)}, u32[]{:S(2)}, u32[]{:S(2)}) async-start(f32[16,1,16384]{2,1,0:T(1,128)} %bitcast.1), calls=%async_computation | async-start | bytes 2097152 | tf_op jit(solution)/shard_map/all_to_all | solution.py:17
  19.4 0.0 copy-done.3
  19.5 0.0 copy-done.4
  19.5 16.0 %all-to-all-done = f32[16,1,16384]{2,1,0:T(1,128)} async-done(((f32[16,1,16384]{2,1,0:T(1,128)}), f32[16,1,16384]{2,1,0:T(1,128)}, u32[]{:S(2)}, u32[]{:S(2)}) %all-to-all-start) | async-done | bytes 1048608 | tf_op jit(solution)/shard_map/all_to_all | solution.py:17
  35.5 1.9 reduce-window_convert_fusion
  37.4 0.5 broadcast.59
  38.0 4.6 %reduce.1 = bf16[16,16384]{1,0:T(8,128)(2,1)} reduce(bf16[16,1,16384]{2,1,0:T(2,128)(2,1)S(1)} %reduce-window_convert_fusion, bf16[]{:T(256)} %broadcast.59), dimensions={1}, to_apply=%reduce-window_convert_fusion.reduce_sub_computation | reduce | bytes 1048578 | tf_op jit(solution)/shard_map/block_prefix/reduce_window_sum | solution.py:19
  42.5 2.2 reshape.169
  44.8 4.3 %all-to-all-start.1 = ((bf16[16,2,8192]{2,1,0:T(2,128)(2,1)}), bf16[16,2,8192]{2,1,0:T(2,128)(2,1)}, u32[]{:S(2)}, u32[]{:S(2)}) async-start(bf16[16,2,8192]{2,1,0:T(2,128)(2,1)} %reshape.169), calls=%async_computation.1 | async-start | bytes 1048576 | tf_op jit(solution)/shard_map/all_to_all | solution.py:20
  49.0 0.0 all-reduce.2.cloned.1.call-start
  49.1 0.7 broadcast_select_fusion
  49.8 0.0 all-reduce.2.cloned.1.call-update
  49.8 0.2 all-gather.3.cloned.1.call-start
  50.0 1.5 copy.43
  51.5 2.7 %fusion.46 = f32[16,256,128]{1,2,0:T(8,128)} fusion(bf16[256,16,128]{0,2,1:T(8,128)(2,1)S(1)} %bitcast.146, pred[256,256]{1,0:T(8,128)(4,1)S(1)} %iota_compare_fusion, bf16[256,16,128]{2,1,0:T(8,128)(2,1)S(1)} %bitcast.148, bf16[256,16,128]{2,1,0:T(8,128)(2,1)S(1)} %bitcast.149), kind=kOutput, calls=%fused_computation.47 | convolution fusion | flops 538968064 | bytes 5308416 | tf_op jit(solution)/shard_map/htu,uhd->thd/dot_general | solution.py:46
  54.2 4.2 %all-to-all-done.1 = bf16[16,2,8192]{2,1,0:T(2,128)(2,1)} async-done(((bf16[16,2,8192]{2,1,0:T(2,128)(2,1)}), bf16[16,2,8192]{2,1,0:T(2,128)(2,1)}, u32[]{:S(2)}, u32[]{:S(2)}) %all-to-all-start.1) | async-done | bytes 524320 | tf_op jit(solution)/shard_map/all_to_all | solution.py:20
  58.4 2.2 reshape.170
  60.6 3.1 %reduce = bf16[16,16384]{1,0:T(8,128)(2,1)S(1)} reduce(bf16[16,1,16384]{2,1,0:T(2,128)(2,1)S(1)} %reshape.170, bf16[]{:T(256)} %constant.38), dimensions={1}, to_apply=%all_to_all.12.reduce_sub_computation | reduce | bytes 1048578 | tf_op jit(solution)/shard_map/all_to_all | solution.py:20
  63.8 0.1 copy.45
  63.9 2.2 multiply_reduce_fusion
  66.1 0.0 copy-start
  66.1 0.0 copy-start.1
  66.1 0.2 broadcast_multiply_fusion
  66.3 0.0 copy-start.2
  66.3 1.9 copy.40
  68.2 0.0 copy-done
  68.2 0.0 copy-done.1
  68.2 2.1 fusion.43
  70.3 0.0 copy-done.2
  70.3 0.3 fusion.45
  70.6 1.1 fusion.58
  71.7 0.0 all-gather.3.cloned.1.call-update
  71.7 0.0 all-gather.5.cloned.1.call-start
  71.8 0.7 all-gather.5.cloned.1.call-update
  72.5 0.3 reduce-scatter.3.cloned.1.call-start
  72.8 40.4 %all-reduce.2.cloned.1.call-done = f32[8,256,8]{1,0,2:T(8,128)} async-done(((f32[8,256,8]{1,0,2:T(8,128)}), f32[8,256,8]{1,0,2:T(8,128)}) %all-reduce.2.cloned.1.call-update) | async-done | bytes 65552 | tf_op jit(solution)/shard_map/psum | solution.py:69
  113.1 0.7 dynamic-slice_bitcast_fusion.1
  113.8 34.7 %all-gather.3.cloned.1.call-done = bf16[1024,2048]{1,0:T(8,128)(2,1)} async-done(((bf16[128,2048]{1,0:T(8,128)(2,1)}), bf16[1024,2048]{1,0:T(8,128)(2,1)}) %all-gather.3.cloned.1.call-update) | async-done | bytes 4194320 | tf_op jit(solution)/shard_map/all_gather | solution.py:77
  148.5 11.7 %fusion.11 = f32[1024,1408]{1,0:T(8,128)} fusion(bf16[1024,2048]{1,0:T(8,128)(2,1)} %all-gather.3.cloned.1.call-done, bf16[1,2048,1408]{2,1,0:T(8,128)(2,1)} %param.20), kind=kOutput, calls=%fused_computation.18 | convolution fusion | flops 5905580032 | bytes 15728640 | tf_op jit(solution)/shard_map/nd,edf->enf/dot_general | solution.py:80
  160.3 21.2 %multiply_convert_fusion.1 = bf16[1024,2048]{1,0:T(8,128)(2,1)} fusion(f32[1024]{0:T(1024)S(1)} %get-tuple-element.9, bf16[1,1408,2048]{2,1,0:T(8,128)(2,1)} %param.21, f32[1024,1408]{1,0:T(8,128)} %fusion.11, bf16[1024,2048]{1,0:T(8,128)(2,1)} %all-gather.3.cloned.1.call-done, bf16[1,2048,1408]{2,1,0:T(8,128)(2,1)} %param.19), kind=kOutput, calls=%fused_computation.2 | convolution fusion | flops 11828199424 | bytes 25694208 | tf_op jit(solution)/shard_map/enf,efd->end/dot_general | solution.py:82
  181.5 0.0 reduce-scatter.3.cloned.1.call-update
  181.5 0.3 reduce-scatter.5.cloned.1.call-start
  181.8 0.5 all-gather.5.cloned.1.call-done
  182.3 11.7 %fusion.9 = f32[1024,1408]{1,0:T(8,128)} fusion(bf16[1024,2048]{1,0:T(8,128)(2,1)} %all-gather.5.cloned.1.call-done, bf16[1,2048,1408]{2,1,0:T(8,128)(2,1)} %param.20), kind=kOutput, calls=%fused_computation.16 | convolution fusion | flops 5905580032 | bytes 15728640 | tf_op jit(solution)/shard_map/nd,edf->enf/dot_general | solution.py:80
  194.0 21.1 %multiply_convert_fusion = bf16[1024,2048]{1,0:T(8,128)(2,1)} fusion(f32[1024]{0:T(1024)S(1)} %get-tuple-element.10, bf16[1,1408,2048]{2,1,0:T(8,128)(2,1)} %param.21, f32[1024,1408]{1,0:T(8,128)} %fusion.9, bf16[1024,2048]{1,0:T(8,128)(2,1)} %all-gather.5.cloned.1.call-done, bf16[1,2048,1408]{2,1,0:T(8,128)(2,1)} %param.19), kind=kOutput, calls=%fused_computation.1 | convolution fusion | flops 11828199424 | bytes 25694208 | tf_op jit(solution)/shard_map/enf,efd->end/dot_general | solution.py:82
  215.2 0.0 reduce-scatter.5.cloned.1.call-update
  215.2 1.9 copy.39
  217.0 2.2 reduce-scatter.3.cloned.1.call-done
  219.2 39.0 %reduce-scatter.5.cloned.1.call-done = bf16[128,2048]{1,0:T(8,128)(2,1)} async-done(((bf16[1024,2048]{1,0:T(8,128)(2,1)}), bf16[128,2048]{1,0:T(8,128)(2,1)}) %reduce-scatter.5.cloned.1.call-update) | async-done | bytes 524304 | tf_op jit(solution)/shard_map/reduce_scatter | solution.py:85
  258.2 3.3 %add_convert_fusion = bf16[1,256,2048]{2,1,0:T(8,128)(2,1)} fusion(f32[1,256,2048]{2,1,0:T(8,128)} %copy.39, bf16[1,256,2048]{2,1,0:T(8,128)(2,1)S(1)} %copy-done, bf16[1,128,2048]{2,1,0:T(8,128)(2,1)} %bitcast.156, bf16[1,128,2048]{2,1,0:T(8,128)(2,1)} %bitcast.155, f32[2048]{0:T(1024)S(1)} %copy-done.1), kind=kLoop, calls=%fused_computation.45 | loop fusion | flops 5767168 | bytes 5251072 | tf_op jit(solution)/shard_map/convert_element_type | solution.py:87
  (5 shorter events, 0.1 us)
Async XLA Ops:
  8.0 11.4 %copy-start.3 = (f32[1,256,4]{1,2,0:T(4,128)S(1)}, f32[1,256,4]{1,2,0:T(4,128)}, u32[]{:S(2)}) copy-start(f32[1,256,4]{1,2,0:T(4,128)} %param.18) | copy-start | bytes 12292
  8.0 11.4 %copy-start.4 = (s32[1,256,4]{1,2,0:T(4,128)S(1)}, s32[1,256,4]{1,2,0:T(4,128)}, u32[]{:S(2)}) copy-start(s32[1,256,4]{1,2,0:T(4,128)} %param.17) | copy-start | bytes 12292
  10.9 24.6 %all-to-all-start = ((f32[16,1,16384]{2,1,0:T(1,128)}), f32[16,1,16384]{2,1,0:T(1,128)}, u32[]{:S(2)}, u32[]{:S(2)}) async-start(f32[16,1,16384]{2,1,0:T(1,128)} %bitcast.1), calls=%async_computation | async-start | bytes 2097152 | tf_op jit(solution)/shard_map/all_to_all | solution.py:17
  44.8 13.6 %all-to-all-start.1 = ((bf16[16,2,8192]{2,1,0:T(2,128)(2,1)}), bf16[16,2,8192]{2,1,0:T(2,128)(2,1)}, u32[]{:S(2)}, u32[]{:S(2)}) async-start(bf16[16,2,8192]{2,1,0:T(2,128)(2,1)} %reshape.169), calls=%async_computation.1 | async-start | bytes 1048576 | tf_op jit(solution)/shard_map/all_to_all | solution.py:20
  49.0 64.1 %all-reduce.2.cloned.1.call-start = ((), (), s32[]{:S(2)}) async-start(), calls=%async_computation.5 | async-start | bytes 131072 | tf_op jit(solution)/shard_map/psum | solution.py:69
  49.8 98.7 %all-gather.3.cloned.1.call-start = ((), (), s32[]{:S(2)}) async-start(), calls=%async_computation.4 | async-start | bytes 4718592 | tf_op jit(solution)/shard_map/all_gather | solution.py:77
  66.1 2.1 copy-start
  66.1 2.1 copy-start.1
  66.3 4.0 %copy-start.2 = (f32[2048]{0:T(1024)S(1)}, f32[2048]{0:T(1024)}, u32[]{:S(2)}) copy-start(f32[2048]{0:T(1024)} %param.16) | copy-start | bytes 24580
  71.7 110.6 %all-gather.5.cloned.1.call-start = ((), (), s32[]{:S(2)}) async-start(), calls=%async_computation.7 | async-start | bytes 4718592 | tf_op jit(solution)/shard_map/all_gather | solution.py:77
  72.5 146.7 %reduce-scatter.3.cloned.1.call-start = ((), (), s32[]{:S(2)}) async-start(), calls=%async_computation.6 | async-start | bytes 4718592 | tf_op jit(solution)/shard_map/reduce_scatter | solution.py:85
  181.5 76.7 %reduce-scatter.5.cloned.1.call-start = ((), (), s32[]{:S(2)}) async-start(), calls=%async_computation.8 | async-start | bytes 4718592 | tf_op jit(solution)/shard_map/reduce_scatter | solution.py:85
Sparse Core Ops, SparseCore 0:
  52.2 60.9 all-reduce.1
  114.9 33.6 all-gather.2
  150.3 31.9 all-gather.4
  184.6 34.6 reduce-scatter.2
  221.5 36.7 reduce-scatter.4

commit v3 on v2

--- a/solution.py
+++ b/solution.py
@@ -65,17 +65,22 @@
     )
     groups = lax.axis_size("exp")
     me = lax.axis_index("exp")
-    slots = jnp.where((jnp.arange(groups) == me)[:, None, None], table[None], 0.0)
-    all_table = lax.psum(slots, "exp")
     local_count = w_gate.shape[0]
-    local_weights = lax.dynamic_slice_in_dim(all_table, me * local_count, local_count, axis=2)
+    high = table.astype(jnp.bfloat16)
+    rest = table - high.astype(jnp.float32)
+    middle = rest.astype(jnp.bfloat16)
+    low = (rest - middle.astype(jnp.float32)).astype(jnp.bfloat16)
+    pad = jnp.zeros((positions, 128 - 3 * EXPERTS), jnp.bfloat16)
+    payload = jnp.concatenate([normed, high, middle, low, pad], axis=1)
 
     chunk = positions // CHUNKS
     outs = []
     for c in range(CHUNKS):
-        part = normed[c * chunk:(c + 1) * chunk]
-        rows = lax.all_gather(part, "exp", axis=0, tiled=True)
-        weight = local_weights[:, c * chunk:(c + 1) * chunk].reshape(groups * chunk, local_count)
+        gathered = lax.all_gather(payload[c * chunk:(c + 1) * chunk], "exp", axis=0, tiled=True)
+        rows = gathered[:, :D]
+        code = gathered[:, D:D + 3 * EXPERTS].astype(jnp.float32)
+        code = lax.dynamic_slice_in_dim(code.reshape(-1, 3, EXPERTS), me * local_count, local_count, axis=2)
+        weight = code[:, 0] + code[:, 1] + code[:, 2]
         gate_part = jnp.einsum("nd,edf->enf", rows, w_gate, preferred_element_type=jnp.float32)
         up_part = jnp.einsum("nd,edf->enf", rows, w_up, preferred_element_type=jnp.float32)
         hidden = (jax.nn.silu(gate_part) * up_part).astype(jnp.bfloat16)

time: 271 us -> 272 us (level)
  blocking collectives: 0 us -> 24.3 us
  waiting for transfers between devices: 138 us -> 117 us
  starting transfers between devices: 13.6 us -> 5.06 us
  local copies, waits for them, and re-layouts: 15 us -> 22.1 us
  other arithmetic: 16.2 us -> 13.4 us
    reduce_scatter x2 -> x0, waiting for transfers between devices: 41.2 us -> none  [on_device(): lax.psum_scatter(contrib, 'exp', scatter_dimension=0, tiled=True)]
    all_gather x2, waiting for transfers between devices: 35.2 us -> 76.3 us  [on_device(): lax.all_gather(payload[c * chunk:(c + 1) * chunk], 'exp', axis=0, tiled=T...]
    psum x1 -> x0, waiting for transfers between devices: 40.4 us -> none  [on_device(): all_table = lax.psum(slots, 'exp')]
    unnamed x5 -> x6, waiting for transfers between devices: 0.75 us -> 39.5 us
    all_to_all x0 -> x1, blocking collectives: none -> 24.3 us  [block_prefix(): lax.all_to_all(pieces, 'seq', split_axis=0, concat_axis=0, tiled=True)]
    all_to_all x1 -> x0, waiting for transfers between devices: 16 us -> none  [block_prefix(): lax.all_to_all(pieces, 'seq', split_axis=0, concat_axis=0, tiled=True)]
    unnamed x15 -> x20, local copies, waits for them, and re-layouts: 7.48 us -> 16.7 us
    all_to_all x1 -> x0, starting transfers between devices: 8.47 us -> none  [block_prefix(): lax.all_to_all(pieces, 'seq', split_axis=0, concat_axis=0, tiled=True)]
  transfers between devices with their start and end apart: 7 -> 5, of which waited for: 7 -> 5; matrix products, arithmetic and copies ran while one was open for 32% -> 17% of each run, Pallas kernels for 0% -> 0%
where the time goes in v3:
time: 272 us; the launch traced here: 269 us
  waiting for transfers between devices  117 us (43%)
  matrix products  73.6 us (27%)
  blocking collectives  24.3 us (9%)
  local copies, waits for them, and re-layouts  22.1 us (8%)
  other arithmetic  13.4 us (5%)
  between operations  13.4 us (5%)
  starting transfers between devices  5.06 us (2%)
    all_gather x2, waiting for transfers between devices, on_device(): lax.all_gather(payload[c * chunk:(c + 1) * chunk], 'exp', axis=0, tiled=T...  76.3 us
    dot_general x2, matrix products, on_device(): jnp.einsum('enf,efd->end', hidden, w_down, preferred_element_type=jnp.flo...  43.3 us
    unnamed x6, waiting for transfers between devices  39.5 us
    all_to_all x1, blocking collectives, block_prefix(): lax.all_to_all(pieces, 'seq', split_axis=0, concat_axis=0, tiled=True)  24.3 us
    dot_general x2, matrix products, on_device(): jnp.einsum('nd,edf->enf', rows, w_up, preferred_element_type=jnp.float32)  23.7 us
    unnamed x20, local copies, waits for them, and re-layouts  16.7 us
  transfers between devices with their start and end apart: 5, of which 5 were waited for; matrix products, arithmetic and copies ran while one was open for 17% of the time, Pallas kernels for 0%

profile of v3, /device:TPU:1, one launch (start us, length us, event | category | flops | bytes accessed | tf_op | source)
XLA Modules:
  0.0 269.0 jit_solution(12462219032883238043)
XLA Ops:
  6.5 1.5 copy.77
  8.0 1.5 copy.79
  9.5 0.5 fusion.62
  9.9 0.0 copy-start.3
  10.0 0.0 copy-start.4
  10.0 24.3 %all_to_all.15 = f32[16,1,16384]{2,1,0:T(1,128)S(1)} all-to-all(f32[16,1,16384]{2,1,0:T(1,128)S(1)} %bitcast.158), channel_id=1, replica_groups=mesh['seq'=16,'exp'=8] {'seq'}, dimensions={0} | all-to-all | bytes 2097152 | tf_op jit(solution)/shard_map/all_to_all | solution.py:17
  34.2 0.7 reduce-window_convert_fusion
  34.9 0.6 broadcast.54
  35.5 4.6 %reduce.1 = bf16[16,16384]{1,0:T(8,128)(2,1)} reduce(bf16[16,1,16384]{2,1,0:T(2,128)(2,1)S(1)} %reduce-window_convert_fusion, bf16[]{:T(256)} %broadcast.54), dimensions={1}, to_apply=%reduce-window_convert_fusion.reduce_sub_computation | reduce | bytes 1048578 | tf_op jit(solution)/shard_map/block_prefix/reduce_window_sum | solution.py:19
  40.2 2.2 reshape.234
  42.4 4.2 %all-to-all-start.1 = ((bf16[16,2,8192]{2,1,0:T(2,128)(2,1)}), bf16[16,2,8192]{2,1,0:T(2,128)(2,1)}, u32[]{:S(2)}, u32[]{:S(2)}) async-start(bf16[16,2,8192]{2,1,0:T(2,128)(2,1)} %reshape.234), calls=%async_computation.1 | async-start | bytes 1048576 | tf_op jit(solution)/shard_map/all_to_all | solution.py:20
  46.6 0.2 all-gather.5.cloned.1.call-start
  46.9 0.0 copy-done.3
  46.9 0.0 copy-done.4
  46.9 1.5 copy.60
  48.4 2.4 copy.78
  50.9 3.9 %fusion.58 = f32[16,256,128]{1,2,0:T(8,128)} fusion(bf16[256,16,128]{0,2,1:T(8,128)(2,1)S(1)} %bitcast.155, pred[256,256]{1,0:T(8,128)(4,1)S(1)} %iota_compare_fusion, bf16[256,16,128]{2,1,0:T(8,128)(2,1)S(1)} %bitcast.157, bf16[256,16,128]{2,1,0:T(8,128)(2,1)} %bitcast.159), kind=kOutput, calls=%fused_computation.53 | convolution fusion | flops 538968064 | bytes 5308416 | tf_op jit(solution)/shard_map/htu,uhd->thd/dot_general | solution.py:46
  54.8 0.0 copy-start
  54.8 1.5 all-to-all-done.1
  56.3 2.2 reshape.235
  58.5 3.9 %reduce = bf16[16,16384]{1,0:T(8,128)(2,1)} reduce(bf16[16,1,16384]{2,1,0:T(2,128)(2,1)S(1)} %reshape.235, bf16[]{:T(256)} %constant.40), dimensions={1}, to_apply=%all_to_all.12.reduce_sub_computation | reduce | bytes 1048578 | tf_op jit(solution)/shard_map/all_to_all | solution.py:20
  62.4 1.1 copy.80
  63.6 0.0 copy-done
  63.6 0.0 copy-start.1
  63.6 2.2 multiply_reduce_fusion
  65.8 0.0 copy-start.2
  65.8 0.2 broadcast_multiply_fusion
  66.0 0.0 copy-done.1
  66.1 0.5 fusion.55
  66.5 0.0 copy-done.2
  66.5 0.3 fusion.59
  66.9 1.1 fusion.72
  68.0 0.0 all-gather.5.cloned.1.call-update
  68.0 0.0 all-gather.3.cloned.1.call-start
  68.1 0.7 all-gather.3.cloned.1.call-update
  68.8 0.3 reduce-scatter.9.cloned.1.call-start
  69.0 37.8 %all-gather.5.cloned.1.call-done = bf16[1024,2176]{0,1:T(8,128)(2,1)} async-done(((bf16[128,2176]{0,1:T(8,128)(2,1)}), bf16[1024,2176]{0,1:T(8,128)(2,1)}) %all-gather.5.cloned.1.call-update) | async-done | bytes 4456464 | tf_op jit(solution)/shard_map/all_gather | solution.py:79
  106.8 0.8 slice_bitcast_fusion
  107.6 38.5 %all-gather.3.cloned.1.call-done = bf16[1024,2176]{0,1:T(8,128)(2,1)} async-done(((bf16[128,2176]{0,1:T(8,128)(2,1)}), bf16[1024,2176]{0,1:T(8,128)(2,1)}) %all-gather.3.cloned.1.call-update) | async-done | bytes 4456464 | tf_op jit(solution)/shard_map/all_gather | solution.py:79
  146.1 0.8 slice_bitcast_fusion.1
  147.0 11.8 %fusion.9 = f32[1024,1408]{1,0:T(8,128)} fusion(bf16[1,2048,1408]{2,1,0:T(8,128)(2,1)} %param.20, bf16[1024,2176]{0,1:T(8,128)(2,1)} %all-gather.5.cloned.1.call-done), kind=kOutput, calls=%fused_computation.16 | convolution fusion | flops 5905580032 | bytes 15728640 | tf_op jit(solution)/shard_map/nd,edf->enf/dot_general | solution.py:85
  158.8 21.5 %multiply_convert_fusion = bf16[1024,2048]{1,0:T(8,128)(2,1)} fusion(f32[1024]{0:T(1024)S(1)} %bitcast.169, bf16[1,1408,2048]{2,1,0:T(8,128)(2,1)} %param.21, f32[1024,1408]{1,0:T(8,128)} %fusion.9, bf16[1,2048,1408]{2,1,0:T(8,128)(2,1)} %param.19, bf16[1024,2176]{0,1:T(8,128)(2,1)} %all-gather.5.cloned.1.call-done), kind=kOutput, calls=%fused_computation.1 | convolution fusion | flops 11828199424 | bytes 25694208 | tf_op jit(solution)/shard_map/enf,efd->end/dot_general | solution.py:87
  180.3 0.0 reduce-scatter.9.cloned.1.call-update
  180.3 0.3 reduce-scatter.7.cloned.1.call-start
  180.6 11.8 %fusion.11 = f32[1024,1408]{1,0:T(8,128)} fusion(bf16[1,2048,1408]{2,1,0:T(8,128)(2,1)} %param.20, bf16[1024,2176]{0,1:T(8,128)(2,1)} %all-gather.3.cloned.1.call-done), kind=kOutput, calls=%fused_computation.18 | convolution fusion | flops 5905580032 | bytes 15728640 | tf_op jit(solution)/shard_map/nd,edf->enf/dot_general | solution.py:85
  192.5 21.9 %multiply_convert_fusion.1 = bf16[1024,2048]{1,0:T(8,128)(2,1)} fusion(f32[1024]{0:T(1024)S(1)} %bitcast.170, bf16[1,1408,2048]{2,1,0:T(8,128)(2,1)} %param.21, f32[1024,1408]{1,0:T(8,128)} %fusion.11, bf16[1,2048,1408]{2,1,0:T(8,128)(2,1)} %param.19, bf16[1024,2176]{0,1:T(8,128)(2,1)} %all-gather.3.cloned.1.call-done), kind=kOutput, calls=%fused_computation.2 | convolution fusion | flops 11828199424 | bytes 25694208 | tf_op jit(solution)/shard_map/enf,efd->end/dot_general | solution.py:87
  214.3 0.0 reduce-scatter.7.cloned.1.call-update
  214.3 1.7 reduce-scatter.9.cloned.1.call-done
  216.0 2.0 copy.76
  218.1 37.1 %reduce-scatter.7.cloned.1.call-done = bf16[128,2048]{1,0:T(8,128)(2,1)} async-done(((bf16[1024,2048]{1,0:T(8,128)(2,1)}), bf16[128,2048]{1,0:T(8,128)(2,1)}) %reduce-scatter.7.cloned.1.call-update) | async-done | bytes 524304
  255.2 2.1 copy.74
  257.2 3.0 %add_convert_fusion = bf16[1,256,2048]{1,2,0:T(8,128)(2,1)} fusion(f32[256,16,128]{0,2,1:T(8,128)S(1)} %broadcast_multiply_fusion, bf16[1,256,2048]{1,2,0:T(8,128)(2,1)S(1)} %copy.60, bf16[1,128,2048]{1,2,0:T(8,128)(2,1)} %bitcast.161, bf16[1,128,2048]{1,2,0:T(8,128)(2,1)} %bitcast.162, f32[2048]{0:T(1024)S(1)} %copy-done.1), kind=kLoop, calls=%fused_computation.51 | loop fusion | flops 5767168 | bytes 5251072 | tf_op jit(solution)/shard_map/convert_element_type | solution.py:92
  260.2 2.3 copy.71
  (11 shorter events, 0.1 us)
Async XLA Ops:
  9.9 36.9 %copy-start.3 = (f32[1,256,4]{1,2,0:T(4,128)S(1)}, f32[1,256,4]{1,2,0:T(4,128)}, u32[]{:S(2)}) copy-start(f32[1,256,4]{1,2,0:T(4,128)} %param.18) | copy-start | bytes 12292
  10.0 36.9 %copy-start.4 = (s32[1,256,4]{1,2,0:T(4,128)S(1)}, s32[1,256,4]{1,2,0:T(4,128)}, u32[]{:S(2)}) copy-start(s32[1,256,4]{1,2,0:T(4,128)} %param.17) | copy-start | bytes 12292
  42.4 13.9 %all-to-all-start.1 = ((bf16[16,2,8192]{2,1,0:T(2,128)(2,1)}), bf16[16,2,8192]{2,1,0:T(2,128)(2,1)}, u32[]{:S(2)}, u32[]{:S(2)}) async-start(bf16[16,2,8192]{2,1,0:T(2,128)(2,1)} %reshape.234), calls=%async_computation.1 | async-start | bytes 1048576 | tf_op jit(solution)/shard_map/all_to_all | solution.py:20
  46.6 60.2 %all-gather.5.cloned.1.call-start = ((), (), s32[]{:S(2)}) async-start(), calls=%async_computation.5 | async-start | bytes 5013504 | tf_op jit(solution)/shard_map/all_gather | solution.py:79
  54.8 8.8 %copy-start = (bf16[32,8,16,128]{3,2,1,0:T(8,128)(2,1)S(1)}, bf16[32,8,16,128]{3,2,1,0:T(8,128)(2,1)}, u32[]{:S(2)}) copy-start(bf16[32,8,16,128]{3,2,1,0:T(8,128)(2,1)} %copy.78) | copy-start | bytes 3145732
  63.6 2.5 copy-start.1
  65.8 0.7 copy-start.2
  68.0 78.1 %all-gather.3.cloned.1.call-start = ((), (), s32[]{:S(2)}) async-start(), calls=%async_computation.4 | async-start | bytes 5013504 | tf_op jit(solution)/shard_map/all_gather | solution.py:79
  68.8 147.3 %reduce-scatter.9.cloned.1.call-start = ((), (), s32[]{:S(2)}) async-start(), calls=%async_computation.7 | async-start | bytes 4718592
  180.3 74.9 %reduce-scatter.7.cloned.1.call-start = ((), (), s32[]{:S(2)}) async-start(), calls=%async_computation.6 | async-start | bytes 4718592
Sparse Core Ops, SparseCore 0:
  68.1 38.6 all-gather.4
  108.5 37.5 all-gather.2
  180.4 35.5 reduce-scatter.8
  218.3 36.8 reduce-scatter.6

commit v4 on v3

--- a/solution.py
+++ b/solution.py
@@ -8,12 +8,12 @@
 HD = 128
 TOP = 4
 EXPERTS = 8
-CHUNKS = 2
+CHUNKS = 1
 
 
 def block_prefix(state):
     blocks = lax.axis_size("seq")
-    pieces = state.reshape(blocks, -1)
+    pieces = state if blocks == state.shape[0] else state.reshape(blocks, -1)
     gathered = lax.all_to_all(pieces, "seq", split_axis=0, concat_axis=0, tiled=True)
     shifted = jnp.concatenate([jnp.zeros_like(gathered[:1]), gathered[:-1]], axis=0)
     prefixes = lax.cumsum(shifted, axis=0).astype(jnp.bfloat16)

time: 272 us -> 229 us (0.84); the launches traced: 269 us -> 229 us
  matrix products: 73.6 us -> 61 us
  local copies, waits for them, and re-layouts: 22.1 us -> 11.2 us
  other arithmetic: 13.4 us -> 2.67 us
  waiting for transfers between devices: 117 us -> 112 us
    reduce_scatter x0 -> x1, waiting for transfers between devices: none -> 52.7 us  [on_device(): lax.psum_scatter(contrib, 'exp', scatter_dimension=0, tiled=True)]
    unnamed x6 -> x2, waiting for transfers between devices: 39.5 us -> 0.03 us
    all_gather x2 -> x1, waiting for transfers between devices: 76.3 us -> 57.3 us  [on_device(): lax.all_gather(payload[c * chunk:(c + 1) * chunk], 'exp', axis=0, tiled=T...]
    unnamed x20 -> x14, local copies, waits for them, and re-layouts: 16.7 us -> 7.27 us
    dot_general x2 -> x1, matrix products: 43.3 us -> 35.2 us  [on_device(): jnp.einsum('enf,efd->end', hidden, w_down, preferred_element_type=jnp.flo...]
    another operation x2 -> x1, other arithmetic: 5.33 us -> 0.08 us  [block_prefix(): prefixes = lax.cumsum(shifted, axis=0).astype(jnp.bfloat16)]
    dot_general x2 -> x1, matrix products: 23.7 us -> 18.9 us  [on_device(): jnp.einsum('nd,edf->enf', rows, w_gate, preferred_element_type=jnp.float32)]
    all_to_all x1 -> x0, other arithmetic: 3.94 us -> none  [block_prefix(): lax.all_to_all(prefixes, 'seq', split_axis=0, concat_axis=0, tiled=True)]
  transfers between devices with their start and end apart: 5 -> 3, of which waited for: 5 -> 3; matrix products, arithmetic and copies ran while one was open for 17% -> 3% of each run, Pallas kernels for 0% -> 0%
where the time goes in v4:
time: 229 us
  waiting for transfers between devices  112 us (49%)
  matrix products  61 us (27%)
  blocking collectives  24.3 us (11%)
  between operations  13.6 us (6%)
  local copies, waits for them, and re-layouts  11.2 us (5%)
  starting transfers between devices  4.51 us (2%)
  other arithmetic  2.67 us (1%)
    all_gather x1, waiting for transfers between devices, on_device(): lax.all_gather(payload[c * chunk:(c + 1) * chunk], 'exp', axis=0, tiled=T...  57.3 us
    reduce_scatter x1, waiting for transfers between devices, on_device(): lax.psum_scatter(contrib, 'exp', scatter_dimension=0, tiled=True)  52.7 us
    dot_general x1, matrix products, on_device(): jnp.einsum('enf,efd->end', hidden, w_down, preferred_element_type=jnp.flo...  35.2 us
    all_to_all x1, blocking collectives, block_prefix(): lax.all_to_all(pieces, 'seq', split_axis=0, concat_axis=0, tiled=True)  24.3 us
    dot_general x1, matrix products, on_device(): jnp.einsum('nd,edf->enf', rows, w_gate, preferred_element_type=jnp.float32)  18.9 us
    unnamed x14, local copies, waits for them, and re-layouts  7.27 us
  transfers between devices with their start and end apart: 3, of which 3 were waited for; matrix products, arithmetic and copies ran while one was open for 3% of the time, Pallas kernels for 0%

profile of v4, /device:TPU:1, one launch (start us, length us, event | category | flops | bytes accessed | tf_op | source)
XLA Modules:
  0.0 229.0 jit_solution(10594119964028985818)
XLA Ops:
  6.5 1.5 copy.48
  8.0 1.5 copy.50
  9.5 0.0 copy-start.3
  9.5 0.0 copy-start.4
  9.5 0.5 fusion.28
  10.0 24.3 %all_to_all.10 = f32[16,128,128]{2,1,0:T(8,128)S(1)} all-to-all(f32[16,128,128]{2,1,0:T(8,128)S(1)} %fusion.28), channel_id=1, replica_groups=mesh['seq'=16,'exp'=8] {'seq'}, dimensions={0} | all-to-all | bytes 2097152 | tf_op jit(solution)/shard_map/all_to_all | solution.py:17
  34.2 0.1 fusion.25
  34.3 1.0 copy.43
  35.3 4.2 %all-to-all-start.1 = ((bf16[16,128,128]{1,2,0:T(8,128)(2,1)}), bf16[16,128,128]{1,2,0:T(8,128)(2,1)}, u32[]{:S(2)}, u32[]{:S(2)}) async-start(bf16[16,128,128]{1,2,0:T(8,128)(2,1)} %copy.43), calls=%async_computation.1 | async-start | bytes 1048576 | tf_op jit(solution)/shard_map/all_to_all | solution.py:20
  39.6 0.0 all-gather.2.cloned.1.call-start
  39.6 0.0 copy-done.3
  39.7 0.0 copy-done.4
  39.7 1.5 copy.37
  41.2 2.4 %copy.49 = bf16[32,8,16,128]{3,2,1,0:T(8,128)(2,1)} copy(bf16[32,8,16,128]{3,1,2,0:T(8,128)(2,1)} %bitcast.85) | data formatting | bytes 2097152
  43.6 3.9 %fusion.22 = f32[16,256,128]{1,2,0:T(8,128)} fusion(bf16[256,16,128]{0,2,1:T(8,128)(2,1)S(1)} %bitcast.79, pred[256,256]{1,0:T(8,128)(4,1)S(1)} %iota_compare_fusion, bf16[256,16,128]{2,1,0:T(8,128)(2,1)S(1)} %bitcast.81, bf16[256,16,128]{2,1,0:T(8,128)(2,1)} %bitcast.82), kind=kOutput, calls=%fused_computation.29 | convolution fusion | flops 538968064 | bytes 5308416 | tf_op jit(solution)/shard_map/htu,uhd->thd/dot_general | solution.py:46
  47.6 0.0 copy-start.1
  47.6 1.7 all-to-all-done.1
  49.2 2.6 %multiply_reduce_fusion = (f32[256,16]{0,1:T(8,128)S(1)}, f32[256,16,128]{0,2,1:T(8,128)S(1)}) fusion(bf16[16,128,128]{1,2,0:T(8,128)(2,1)} %all-to-all-done.1, bf16[256,16,128]{2,1,0:T(8,128)(2,1)} %bitcast.83, f32[16,256,128]{1,2,0:T(8,128)} %fusion.22), kind=kOutput, calls=%fused_computation.28 | convolution fusion | flops 135786496 | bytes 5783552 | tf_op jit(solution)/shard_map/thd,hde->the/dot_general | solution.py:47
  51.9 0.0 copy-start.2
  51.9 0.2 broadcast_multiply_fusion
  52.0 0.0 copy-done.1
  52.0 0.5 fusion.17
  52.6 0.0 copy-done.2
  52.6 0.3 fusion.24
  53.0 0.0 copy-start
  53.0 1.0 copy-done
  54.0 0.0 all-gather.2.cloned.1.call-update
  54.0 0.2 reduce-scatter.2.cloned.1.call-start
  54.2 57.3 %all-gather.2.cloned.1.call-done = bf16[2048,2176]{0,1:T(8,128)(2,1)} async-done(((bf16[256,2176]{0,1:T(8,128)(2,1)}), bf16[2048,2176]{0,1:T(8,128)(2,1)}) %all-gather.2.cloned.1.call-update) | async-done | bytes 8912912 | tf_op jit(solution)/shard_map/all_gather | solution.py:79
  111.6 0.9 slice_bitcast_fusion
  112.5 18.9 %fusion.5 = f32[2048,1408]{1,0:T(8,128)} fusion(bf16[2048,2176]{0,1:T(8,128)(2,1)} %all-gather.2.cloned.1.call-done, bf16[1,2048,1408]{2,1,0:T(8,128)(2,1)} %param.19), kind=kOutput, calls=%fused_computation.9 | convolution fusion | flops 11811160064 | bytes 25690112 | tf_op jit(solution)/shard_map/nd,edf->enf/dot_general | solution.py:84
  131.4 35.2 %multiply_convert_fusion = bf16[2048,2048]{0,1:T(8,128)(2,1)} fusion(f32[2048]{0:T(1024)S(1)} %bitcast.86, bf16[1,1408,2048]{2,1,0:T(8,128)(2,1)} %param.21, bf16[2048,2176]{0,1:T(8,128)(2,1)} %all-gather.2.cloned.1.call-done, f32[2048,1408]{1,0:T(8,128)} %fusion.5, bf16[1,2048,1408]{2,1,0:T(8,128)(2,1)} %param.20), kind=kOutput, calls=%fused_computation | convolution fusion | flops 23656398848 | bytes 39854080 | tf_op jit(solution)/shard_map/enf,efd->end/dot_general | solution.py:87
  166.5 0.0 reduce-scatter.2.cloned.1.call-update
  166.5 52.7 %reduce-scatter.2.cloned.1.call-done = bf16[256,2048]{0,1:T(8,128)(2,1)} async-done(((bf16[2048,2048]{0,1:T(8,128)(2,1)}), bf16[256,2048]{0,1:T(8,128)(2,1)}) %reduce-scatter.2.cloned.1.call-update) | async-done | bytes 1048592 | tf_op jit(solution)/shard_map/reduce_scatter | solution.py:90
  219.2 1.5 fusion.23
  220.7 1.4 copy.46
  (10 shorter events, 0.1 us)
Async XLA Ops:
  9.5 30.2 %copy-start.3 = (f32[1,256,4]{1,2,0:T(4,128)S(1)}, f32[1,256,4]{1,2,0:T(4,128)}, u32[]{:S(2)}) copy-start(f32[1,256,4]{1,2,0:T(4,128)} %param.18) | copy-start | bytes 12292
  9.5 30.2 %copy-start.4 = (s32[1,256,4]{1,2,0:T(4,128)S(1)}, s32[1,256,4]{1,2,0:T(4,128)}, u32[]{:S(2)}) copy-start(s32[1,256,4]{1,2,0:T(4,128)} %param.17) | copy-start | bytes 12292
  35.3 13.9 %all-to-all-start.1 = ((bf16[16,128,128]{1,2,0:T(8,128)(2,1)}), bf16[16,128,128]{1,2,0:T(8,128)(2,1)}, u32[]{:S(2)}, u32[]{:S(2)}) async-start(bf16[16,128,128]{1,2,0:T(8,128)(2,1)} %copy.43), calls=%async_computation.1 | async-start | bytes 1048576 | tf_op jit(solution)/shard_map/all_to_all | solution.py:20
  39.6 72.0 %all-gather.2.cloned.1.call-start = ((), (), s32[]{:S(2)}) async-start(), calls=%async_computation.3 | async-start | bytes 10027008 | tf_op jit(solution)/shard_map/all_gather | solution.py:79
  47.6 4.5 %copy-start.1 = (f32[2048]{0:T(1024)S(1)}, f32[2048]{0:T(1024)}, u32[]{:S(2)}) copy-start(f32[2048]{0:T(1024)} %param.15) | copy-start | bytes 24580
  51.9 0.7 copy-start.2
  53.0 1.0 copy-start
  54.0 165.2 %reduce-scatter.2.cloned.1.call-start = ((), (), s32[]{:S(2)}) async-start(), calls=%async_computation.4 | async-start | bytes 9437184 | tf_op jit(solution)/shard_map/reduce_scatter | solution.py:90
Sparse Core Ops, SparseCore 0:
  54.1 57.4 all-gather.1
  166.7 52.4 reduce-scatter.1

commit v5 on v4

--- a/solution.py
+++ b/solution.py
@@ -1,14 +1,15 @@
 import jax
 import jax.numpy as jnp
 from jax import lax
+from jax.experimental.layout import Layout, with_layout_constraint
 from jax.sharding import PartitionSpec as P
+
 
 D = 2048
 HEADS = 16
 HD = 128
-TOP = 4
 EXPERTS = 8
-CHUNKS = 1
+CHUNKS = 2
 
 
 def block_prefix(state):
@@ -38,18 +39,19 @@
     queries = query_matrix[0].reshape(positions, HEADS, HD)
     key_rows = key_vectors[0].reshape(positions, HEADS, HD)
     value_rows = value_vectors[0].reshape(positions, HEADS, HD)
-    state = jnp.einsum("thd,the->hde", key_rows, value_rows, preferred_element_type=jnp.float32)
+    state = jnp.einsum("thd,the->hed", key_rows, value_rows, preferred_element_type=jnp.float32)
     prefix = block_prefix(state)
     causal = jnp.tril(jnp.ones((positions, positions), dtype=bool))
     scores = jnp.einsum("thd,uhd->htu", queries, key_rows, preferred_element_type=jnp.float32)
     weights = jnp.where(causal[None], scores, 0.0).astype(jnp.bfloat16)
     inner = jnp.einsum("htu,uhd->thd", weights, value_rows, preferred_element_type=jnp.float32)
     outer_product = jnp.einsum(
-        "thd,hde->the", queries, prefix, preferred_element_type=jnp.float32
+        "thd,hed->the", queries, prefix, preferred_element_type=jnp.float32
     )
     mixed = inner + outer_product
     mean_square = jnp.mean(mixed * mixed, axis=-1, keepdims=True)
     attn = (mixed * lax.rsqrt(mean_square + 1e-06)).reshape(positions, D) * head_gain
+    attn = with_layout_constraint(attn, Layout(major_to_minor=(0, 1)))
     resid_float = (
         (residual_in[0].astype(jnp.float32) + attn).astype(jnp.bfloat16).astype(jnp.float32)
     )
@@ -63,7 +65,6 @@
         jnp.where(route_ids[:, :, None] == experts[None, None, :], route_gates[:, :, None], 0.0),
         axis=1,
     )
-    groups = lax.axis_size("exp")
     me = lax.axis_index("exp")
     local_count = w_gate.shape[0]
     high = table.astype(jnp.bfloat16)
@@ -73,14 +74,15 @@
     pad = jnp.zeros((positions, 128 - 3 * EXPERTS), jnp.bfloat16)
     payload = jnp.concatenate([normed, high, middle, low, pad], axis=1)
 
+    columns = jnp.arange(3 * EXPERTS, dtype=jnp.int32) % EXPERTS
+    select = (columns[:, None] == me * local_count + jnp.arange(local_count)[None, :]).astype(jnp.bfloat16)
     chunk = positions // CHUNKS
     outs = []
     for c in range(CHUNKS):
         gathered = lax.all_gather(payload[c * chunk:(c + 1) * chunk], "exp", axis=0, tiled=True)
         rows = gathered[:, :D]
-        code = gathered[:, D:D + 3 * EXPERTS].astype(jnp.float32)
-        code = lax.dynamic_slice_in_dim(code.reshape(-1, 3, EXPERTS), me * local_count, local_count, axis=2)
-        weight = code[:, 0] + code[:, 1] + code[:, 2]
+        code = gathered[:, D:D + 3 * EXPERTS]
+        weight = jnp.dot(code, select, preferred_element_type=jnp.float32)
         gate_part = jnp.einsum("nd,edf->enf", rows, w_gate, preferred_element_type=jnp.float32)
         up_part = jnp.einsum("nd,edf->enf", rows, w_up, preferred_element_type=jnp.float32)
         hidden = (jax.nn.silu(gate_part) * up_part).astype(jnp.bfloat16)
@@ -107,6 +109,5 @@
         P("exp", None, None),
     )
     out_specs = P("exp", "seq", None)
-    return jax.shard_map(
-        on_device, mesh=mesh, in_specs=in_specs, out_specs=out_specs, check_vma=False
-    )
+
+    return jax.shard_map(on_device, mesh=mesh, in_specs=in_specs, out_specs=out_specs, check_vma=False)

time: 229 us -> 217 us (0.948); the launches traced: 229 us -> 214 us
  blocking collectives: 24.3 us -> 0 us
  waiting for transfers between devices: 112 us -> 97.4 us
  matrix products: 61 us -> 74.4 us
  starting transfers between devices: 4.51 us -> 13 us
  other arithmetic: 2.67 us -> 7.07 us
    all_to_all x1 -> x0, blocking collectives: 24.3 us -> none  [block_prefix(): lax.all_to_all(pieces, 'seq', split_axis=0, concat_axis=0, tiled=True)]
    all_gather x1 -> x2, waiting for transfers between devices: 57.3 us -> 33.9 us  [on_device(): lax.all_gather(payload[c * chunk:(c + 1) * chunk], 'exp', axis=0, tiled=T...]
    all_to_all x0 -> x1, waiting for transfers between devices: none -> 15.8 us  [block_prefix(): lax.all_to_all(pieces, 'seq', split_axis=0, concat_axis=0, tiled=True)]
    reduce_scatter x1 -> x2, waiting for transfers between devices: 52.7 us -> 42 us  [on_device(): lax.psum_scatter(contrib, 'exp', scatter_dimension=0, tiled=True)]
    all_to_all x0 -> x1, starting transfers between devices: none -> 8.42 us  [block_prefix(): lax.all_to_all(pieces, 'seq', split_axis=0, concat_axis=0, tiled=True)]
    dot_general x3 -> x6, matrix products: 21.9 us -> 29.4 us  [the longest x2 23.5 us: on_device(): jnp.einsum('nd,edf->enf', rows, w_up, preferred_element_type=jnp.float32)]
    dot_general x1 -> x2, matrix products: 35.2 us -> 42.3 us  [on_device(): jnp.einsum('enf,efd->end', hidden, w_down, preferred_element_type=jnp.flo...]
    unnamed x14 -> x10, local copies, waits for them, and re-layouts: 7.27 us -> 2.92 us
  transfers between devices with their start and end apart: 3 -> 6, of which waited for: 3 -> 6; matrix products, arithmetic and copies ran while one was open for 3% -> 34% of each run, Pallas kernels for 0% -> 0%
where the time goes in v5:
time: 217 us; the launch traced here: 214 us
  waiting for transfers between devices  97.4 us (45%)
  matrix products  74.4 us (34%)
  between operations  13.3 us (6%)
  starting transfers between devices  13 us (6%)
  local copies, waits for them, and re-layouts  8.97 us (4%)
  other arithmetic  7.07 us (3%)
    dot_general x2, matrix products, on_device(): jnp.einsum('enf,efd->end', hidden, w_down, preferred_element_type=jnp.flo...  42.3 us
    reduce_scatter x2, waiting for transfers between devices, on_device(): lax.psum_scatter(contrib, 'exp', scatter_dimension=0, tiled=True)  42 us
    all_gather x2, waiting for transfers between devices, on_device(): lax.all_gather(payload[c * chunk:(c + 1) * chunk], 'exp', axis=0, tiled=T...  33.9 us
    dot_general x2, matrix products, on_device(): jnp.einsum('nd,edf->enf', rows, w_up, preferred_element_type=jnp.float32)  23.5 us
    all_to_all x1, waiting for transfers between devices, block_prefix(): lax.all_to_all(pieces, 'seq', split_axis=0, concat_axis=0, tiled=True)  15.8 us
    all_to_all x1, starting transfers between devices, block_prefix(): lax.all_to_all(pieces, 'seq', split_axis=0, concat_axis=0, tiled=True)  8.42 us
    all_to_all x1, waiting for transfers between devices, block_prefix(): lax.all_to_all(prefixes, 'seq', split_axis=0, concat_axis=0, tiled=True)  4.96 us
  transfers between devices with their start and end apart: 6, of which 6 were waited for; matrix products, arithmetic and copies ran while one was open for 34% of the time, Pallas kernels for 0%

profile of v5, /device:TPU:1, one launch (start us, length us, event | category | flops | bytes accessed | tf_op | source)
XLA Modules:
  0.0 214.2 jit_solution(5185791083464020433)
XLA Ops:
  6.5 0.0 copy-start.3
  6.5 0.0 copy-start.2
  6.5 1.5 copy.34
  8.0 1.5 copy.36
  9.5 1.4 fusion.60
  10.9 8.4 %all-to-all-start = ((f32[16,128,128]{2,1,0:T(8,128)}), f32[16,128,128]{2,1,0:T(8,128)S(1)}, u32[]{:S(2)}, u32[]{:S(2)}) async-start(f32[16,128,128]{2,1,0:T(8,128)} %fusion.60), calls=%async_computation | async-start | bytes 2097152 | tf_op jit(solution)/shard_map/all_to_all | solution.py:18
  19.4 0.0 copy-done.3
  19.4 0.0 copy-done.2
  19.4 0.1 copy.30
  19.6 0.1 copy.31
  19.7 15.8 %all-to-all-done = f32[16,128,128]{2,1,0:T(8,128)S(1)} async-done(((f32[16,128,128]{2,1,0:T(8,128)}), f32[16,128,128]{2,1,0:T(8,128)S(1)}, u32[]{:S(2)}, u32[]{:S(2)}) %all-to-all-start) | async-done | bytes 1048608 | tf_op jit(solution)/shard_map/all_to_all | solution.py:18
  35.4 0.9 reduce-window_convert_fusion
  36.3 4.3 %all-to-all-start.1 = ((bf16[16,128,128]{2,1,0:T(8,128)(2,1)}), bf16[16,128,128]{2,1,0:T(8,128)(2,1)}, u32[]{:S(2)}, u32[]{:S(2)}) async-start(bf16[16,128,128]{2,1,0:T(8,128)(2,1)} %reduce-window_convert_fusion), calls=%async_computation.1 | async-start | bytes 1048576 | tf_op jit(solution)/shard_map/all_to_all | solution.py:21
  40.6 0.0 all-gather.3.cloned.1.call-start
  40.6 0.1 copy.32
  40.8 1.4 copy.35
  42.3 2.7 %fusion.57 = f32[16,256,128]{1,2,0:T(8,128)} fusion(bf16[256,16,128]{0,2,1:T(8,128)(2,1)S(1)} %bitcast.138, pred[256,256]{1,0:T(8,128)(4,1)S(1)} %iota_compare_fusion, bf16[256,16,128]{2,1,0:T(8,128)(2,1)S(1)} %bitcast.140, bf16[256,16,128]{2,1,0:T(8,128)(2,1)S(1)} %bitcast.141), kind=kOutput, calls=%fused_computation.48 | convolution fusion | flops 538968064 | bytes 5308416 | tf_op jit(solution)/shard_map/htu,uhd->thd/dot_general | solution.py:47
  45.0 5.0 %all-to-all-done.1 = bf16[16,128,128]{2,1,0:T(8,128)(2,1)} async-done(((bf16[16,128,128]{2,1,0:T(8,128)(2,1)}), bf16[16,128,128]{2,1,0:T(8,128)(2,1)}, u32[]{:S(2)}, u32[]{:S(2)}) %all-to-all-start.1) | async-done | bytes 524320 | tf_op jit(solution)/shard_map/all_to_all | solution.py:21
  49.9 2.3 %multiply_reduce_fusion = (f32[256,16]{0,1:T(8,128)S(1)}, f32[256,16,128]{0,2,1:T(8,128)S(1)}) fusion(bf16[16,128,128]{2,1,0:T(8,128)(2,1)} %all-to-all-done.1, bf16[256,16,128]{2,1,0:T(8,128)(2,1)S(1)} %bitcast.142, f32[16,256,128]{1,2,0:T(8,128)} %fusion.57), kind=kOutput, calls=%fused_computation.47 | convolution fusion | flops 135786496 | bytes 5783552 | tf_op jit(solution)/shard_map/thd,hed->the/dot_general | solution.py:48
  52.2 0.0 copy-start
  52.3 1.5 broadcast_multiply_fusion
  53.8 0.0 copy-start.1
  53.8 1.9 copy.33
  55.7 0.0 copy-done
  55.7 1.7 fusion.52
  57.5 0.0 copy-done.1
  57.5 0.3 fusion.54
  57.8 1.2 concatenate.7
  59.0 1.1 fusion.87
  60.1 0.0 all-gather.3.cloned.1.call-update
  60.1 0.0 all-gather.5.cloned.1.call-start
  60.1 0.7 all-gather.5.cloned.1.call-update
  60.9 0.0 reduce-scatter.3.cloned.1.call-start
  60.9 33.2 %all-gather.3.cloned.1.call-done = bf16[1024,2176]{1,0:T(8,128)(2,1)} async-done(((bf16[128,2176]{1,0:T(8,128)(2,1)}), bf16[1024,2176]{1,0:T(8,128)(2,1)}) %all-gather.3.cloned.1.call-update) | async-done | bytes 4456464 | tf_op jit(solution)/shard_map/all_gather | solution.py:82
  94.1 1.1 fusion.69
  95.3 11.8 %fusion.11 = f32[1024,1408]{1,0:T(8,128)} fusion(bf16[1,2048,1408]{2,1,0:T(8,128)(2,1)} %param.20, bf16[1024,2176]{1,0:T(8,128)(2,1)} %all-gather.3.cloned.1.call-done), kind=kOutput, calls=%fused_computation.17 | convolution fusion | flops 5905580032 | bytes 15728640 | tf_op jit(solution)/shard_map/nd,edf->enf/dot_general | solution.py:87
  107.0 21.0 %multiply_convert_fusion.1 = bf16[1024,2048]{1,0:T(8,128)(2,1)} fusion(f32[1024]{0:T(1024)S(1)} %bitcast.148, bf16[1,1408,2048]{2,1,0:T(8,128)(2,1)} %param.21, f32[1024,1408]{1,0:T(8,128)} %fusion.11, bf16[1,2048,1408]{2,1,0:T(8,128)(2,1)} %param.19, bf16[1024,2176]{1,0:T(8,128)(2,1)} %all-gather.3.cloned.1.call-done), kind=kOutput, calls=%fused_computation.1 | convolution fusion | flops 11828199424 | bytes 25694208 | tf_op jit(solution)/shard_map/enf,efd->end/dot_general | solution.py:89
  128.1 0.0 reduce-scatter.3.cloned.1.call-update
  128.1 0.2 reduce-scatter.5.cloned.1.call-start
  128.3 0.7 all-gather.5.cloned.1.call-done
  129.0 1.1 fusion.67
  130.1 11.8 %fusion.9 = f32[1024,1408]{1,0:T(8,128)} fusion(bf16[1,2048,1408]{2,1,0:T(8,128)(2,1)} %param.20, bf16[1024,2176]{1,0:T(8,128)(2,1)} %all-gather.5.cloned.1.call-done), kind=kOutput, calls=%fused_computation.15 | convolution fusion | flops 5905580032 | bytes 15728640 | tf_op jit(solution)/shard_map/nd,edf->enf/dot_general | solution.py:87
  141.8 21.2 %multiply_convert_fusion = bf16[1024,2048]{1,0:T(8,128)(2,1)} fusion(f32[1024]{0:T(1024)S(1)} %bitcast.147, bf16[1,1408,2048]{2,1,0:T(8,128)(2,1)} %param.21, f32[1024,1408]{1,0:T(8,128)} %fusion.9, bf16[1,2048,1408]{2,1,0:T(8,128)(2,1)} %param.19, bf16[1024,2176]{1,0:T(8,128)(2,1)} %all-gather.5.cloned.1.call-done), kind=kOutput, calls=%fused_computation | convolution fusion | flops 11828199424 | bytes 25694208 | tf_op jit(solution)/shard_map/enf,efd->end/dot_general | solution.py:89
  163.1 0.0 reduce-scatter.5.cloned.1.call-update
  163.1 2.9 %reduce-scatter.3.cloned.1.call-done = bf16[128,2048]{1,0:T(8,128)(2,1)} async-done(((bf16[1024,2048]{1,0:T(8,128)(2,1)}), bf16[128,2048]{1,0:T(8,128)(2,1)}) %reduce-scatter.3.cloned.1.call-update) | async-done | bytes 524304 | tf_op jit(solution)/shard_map/reduce_scatter | solution.py:92
  166.0 39.1 %reduce-scatter.5.cloned.1.call-done = bf16[128,2048]{1,0:T(8,128)(2,1)} async-done(((bf16[1024,2048]{1,0:T(8,128)(2,1)}), bf16[128,2048]{1,0:T(8,128)(2,1)}) %reduce-scatter.5.cloned.1.call-update) | async-done | bytes 524304 | tf_op jit(solution)/shard_map/reduce_scatter | solution.py:92
  205.1 2.6 %fusion.58 = bf16[1,256,2048]{2,1,0:T(8,128)(2,1)} fusion(bf16[256,2048]{1,0:T(8,128)(2,1)S(1)} %get-tuple-element.6, bf16[128,2048]{1,0:T(8,128)(2,1)} %reduce-scatter.5.cloned.1.call-done, bf16[128,2048]{1,0:T(8,128)(2,1)} %reduce-scatter.3.cloned.1.call-done), kind=kLoop, calls=%fused_computation.50 | loop fusion | flops 3670016 | bytes 3145728 | tf_op jit(solution)/shard_map/broadcast_in_dim | solution.py:94
  (7 shorter events, 0.1 us)
Async XLA Ops:
  6.5 12.8 %copy-start.3 = (s32[1,256,4]{1,2,0:T(4,128)S(1)}, s32[1,256,4]{1,2,0:T(4,128)}, u32[]{:S(2)}) copy-start(s32[1,256,4]{1,2,0:T(4,128)} %param.17) | copy-start | bytes 12292
  6.5 12.9 %copy-start.2 = (f32[1,256,4]{1,2,0:T(4,128)S(1)}, f32[1,256,4]{1,2,0:T(4,128)}, u32[]{:S(2)}) copy-start(f32[1,256,4]{1,2,0:T(4,128)} %param.18) | copy-start | bytes 12292
  10.9 24.5 %all-to-all-start = ((f32[16,128,128]{2,1,0:T(8,128)}), f32[16,128,128]{2,1,0:T(8,128)S(1)}, u32[]{:S(2)}, u32[]{:S(2)}) async-start(f32[16,128,128]{2,1,0:T(8,128)} %fusion.60), calls=%async_computation | async-start | bytes 2097152 | tf_op jit(solution)/shard_map/all_to_all | solution.py:18
  36.3 13.6 %all-to-all-start.1 = ((bf16[16,128,128]{2,1,0:T(8,128)(2,1)}), bf16[16,128,128]{2,1,0:T(8,128)(2,1)}, u32[]{:S(2)}, u32[]{:S(2)}) async-start(bf16[16,128,128]{2,1,0:T(8,128)(2,1)} %reduce-window_convert_fusion), calls=%async_computation.1 | async-start | bytes 1048576 | tf_op jit(solution)/shard_map/all_to_all | solution.py:21
  40.6 53.6 %all-gather.3.cloned.1.call-start = ((), (), s32[]{:S(2)}) async-start(), calls=%async_computation.4 | async-start | bytes 5013504 | tf_op jit(solution)/shard_map/all_gather | solution.py:82
  52.2 3.5 %copy-start = (f32[2048]{0:T(1024)S(1)}, f32[2048]{0:T(1024)}, u32[]{:S(2)}) copy-start(f32[2048]{0:T(1024)} %param.15) | copy-start | bytes 24580
  53.8 3.7 %copy-start.1 = (f32[2048]{0:T(1024)S(1)}, f32[2048]{0:T(1024)}, u32[]{:S(2)}) copy-start(f32[2048]{0:T(1024)} %param.16) | copy-start | bytes 24580
  60.1 68.9 %all-gather.5.cloned.1.call-start = ((), (), s32[]{:S(2)}) async-start(), calls=%async_computation.6 | async-start | bytes 5013504 | tf_op jit(solution)/shard_map/all_gather | solution.py:82
  60.9 105.2 %reduce-scatter.3.cloned.1.call-start = ((), (), s32[]{:S(2)}) async-start(), calls=%async_computation.5 | async-start | bytes 4718592 | tf_op jit(solution)/shard_map/reduce_scatter | solution.py:92
  128.1 77.0 %reduce-scatter.5.cloned.1.call-start = ((), (), s32[]{:S(2)}) async-start(), calls=%async_computation.7 | async-start | bytes 4718592 | tf_op jit(solution)/shard_map/reduce_scatter | solution.py:92
Sparse Core Ops, SparseCore 0:
  60.2 33.8 all-gather.2
  95.8 33.1 all-gather.4
  131.4 34.6 reduce-scatter.2
  168.3 36.7 reduce-scatter.4

commit v6 on v5

--- a/solution.py
+++ b/solution.py
@@ -65,7 +65,8 @@
         jnp.where(route_ids[:, :, None] == experts[None, None, :], route_gates[:, :, None], 0.0),
         axis=1,
     )
-    me = lax.axis_index("exp")
+    cores = lax.axis_size("core")
+    me = lax.axis_index("y") * cores + lax.axis_index("core")
     local_count = w_gate.shape[0]
     high = table.astype(jnp.bfloat16)
     rest = table - high.astype(jnp.float32)
@@ -73,13 +74,11 @@
     low = (rest - middle.astype(jnp.float32)).astype(jnp.bfloat16)
     pad = jnp.zeros((positions, 128 - 3 * EXPERTS), jnp.bfloat16)
     payload = jnp.concatenate([normed, high, middle, low, pad], axis=1)
-
     columns = jnp.arange(3 * EXPERTS, dtype=jnp.int32) % EXPERTS
     select = (columns[:, None] == me * local_count + jnp.arange(local_count)[None, :]).astype(jnp.bfloat16)
-    chunk = positions // CHUNKS
-    outs = []
-    for c in range(CHUNKS):
-        gathered = lax.all_gather(payload[c * chunk:(c + 1) * chunk], "exp", axis=0, tiled=True)
+    swap = [(i, (i + 1) % cores) for i in range(cores)]
+
+    def expert(gathered):
         rows = gathered[:, :D]
         code = gathered[:, D:D + 3 * EXPERTS]
         weight = jnp.dot(code, select, preferred_element_type=jnp.float32)
@@ -88,26 +87,41 @@
         hidden = (jax.nn.silu(gate_part) * up_part).astype(jnp.bfloat16)
         result = jnp.einsum("enf,efd->end", hidden, w_down, preferred_element_type=jnp.float32)
         result = result.astype(jnp.bfloat16).astype(jnp.float32)
-        contrib = jnp.sum(result * weight.T[:, :, None], axis=0).astype(jnp.bfloat16)
-        outs.append(lax.psum_scatter(contrib, "exp", scatter_dimension=0, tiled=True))
+        return jnp.sum(result * weight.T[:, :, None], axis=0).astype(jnp.bfloat16)
+
+    chunk = positions // CHUNKS
+    outs = []
+    for c in range(CHUNKS):
+        own = lax.all_gather(payload[c * chunk:(c + 1) * chunk], "y", axis=0, tiled=True)
+        other = lax.ppermute(own, "core", swap)
+        back = expert(other)
+        returned = lax.ppermute(back, "core", swap)
+        mine = expert(own)
+        total = (mine.astype(jnp.float32) + returned.astype(jnp.float32)).astype(jnp.bfloat16)
+        outs.append(lax.psum_scatter(total, "y", scatter_dimension=0, tiled=True))
     combined = jnp.concatenate(outs, axis=0)
     return (resid_float + combined.astype(jnp.float32)).astype(jnp.bfloat16)[None]
 
 
 def solution(mesh):
+    devices = mesh.devices
+    split = jax.sharding.Mesh(
+        devices.reshape(devices.shape[0], devices.shape[1] // 2, 2), ("seq", "y", "core")
+    )
+    exp = ("y", "core")
     in_specs = (
-        P("exp", "seq", None),
-        P("exp", "seq", None),
-        P("exp", "seq", None),
-        P("exp", "seq", None),
+        P(exp, "seq", None),
+        P(exp, "seq", None),
+        P(exp, "seq", None),
+        P(exp, "seq", None),
         P(),
         P(),
-        P("exp", "seq", None),
-        P("exp", "seq", None),
-        P("exp", None, None),
-        P("exp", None, None),
-        P("exp", None, None),
+        P(exp, "seq", None),
+        P(exp, "seq", None),
+        P(exp, None, None),
+        P(exp, None, None),
+        P(exp, None, None),
     )
-    out_specs = P("exp", "seq", None)
+    out_specs = P(exp, "seq", None)
 
-    return jax.shard_map(on_device, mesh=mesh, in_specs=in_specs, out_specs=out_specs, check_vma=False)
+    return jax.shard_map(on_device, mesh=split, in_specs=in_specs, out_specs=out_specs, check_vma=False)

time: 217 us -> 256 us (1.18)
  matrix products: 74.4 us -> 95.6 us
  waiting for transfers between devices: 97.4 us -> 115 us
    all_gather x2, waiting for transfers between devices: 33.9 us -> 64.1 us  [on_device(): lax.all_gather(payload[c * chunk:(c + 1) * chunk], 'y', axis=0, tiled=True)]
    dot_general x6 -> x12, matrix products: 68 us -> 89.2 us  [the longest x4 55.7 us: expert(): jnp.einsum('enf,efd->end', hidden, w_down, preferred_element_type=jnp.flo...]
    reduce_scatter x2, waiting for transfers between devices: 42 us -> 29.3 us  [on_device(): outs.append(lax.psum_scatter(total, 'y', scatter_dimension=0, tiled=True))]
  transfers between devices with their start and end apart: 6 -> 10, of which waited for: 6 -> 5; matrix products, arithmetic and copies ran while one was open for 34% -> 31% of each run, Pallas kernels for 0% -> 0%
where the time goes in v6:
time: 256 us; the launch traced here: 255 us
  waiting for transfers between devices  115 us (45%)
  matrix products  95.6 us (37%)
  starting transfers between devices  15.3 us (6%)
  between operations  13.4 us (5%)
  local copies, waits for them, and re-layouts  8.95 us (3%)
  other arithmetic  7.05 us (3%)
    all_gather x2, waiting for transfers between devices, on_device(): lax.all_gather(payload[c * chunk:(c + 1) * chunk], 'y', axis=0, tiled=True)  64.1 us
    dot_general x4, matrix products, expert(): jnp.einsum('enf,efd->end', hidden, w_down, preferred_element_type=jnp.flo...  55.7 us
    dot_general x4, matrix products, expert(): jnp.einsum('nd,edf->enf', rows, w_gate, preferred_element_type=jnp.float32)  32 us
    reduce_scatter x2, waiting for transfers between devices, on_device(): outs.append(lax.psum_scatter(total, 'y', scatter_dimension=0, tiled=True))  29.3 us
    all_to_all x1, waiting for transfers between devices, block_prefix(): lax.all_to_all(pieces, 'seq', split_axis=0, concat_axis=0, tiled=True)  15.8 us
    all_to_all x1, starting transfers between devices, block_prefix(): lax.all_to_all(pieces, 'seq', split_axis=0, concat_axis=0, tiled=True)  8.42 us
  transfers between devices with their start and end apart: 10, of which 5 were waited for; matrix products, arithmetic and copies ran while one was open for 31% of the time, Pallas kernels for 0%

profile of v6, /device:TPU:1, one launch (start us, length us, event | category | flops | bytes accessed | tf_op | source)
XLA Modules:
  0.0 255.2 jit_solution(4460677447926566586)
XLA Ops:
  6.5 1.5 copy.34
  8.0 1.5 copy.36
  9.5 0.0 copy-start.2
  9.5 0.0 copy-start.3
  9.5 1.4 fusion.148
  10.9 8.4 %all-to-all-start = ((f32[16,128,128]{2,1,0:T(8,128)}), f32[16,128,128]{2,1,0:T(8,128)S(1)}, u32[]{:S(2)}, u32[]{:S(2)}) async-start(f32[16,128,128]{2,1,0:T(8,128)} %fusion.148), calls=%async_computation | async-start | bytes 2097152 | tf_op jit(solution)/shard_map/all_to_all | solution.py:18
  19.4 0.0 copy-done.2
  19.4 0.0 copy-done.3
  19.4 0.1 copy.30
  19.5 0.1 copy.31
  19.7 15.8 %all-to-all-done = f32[16,128,128]{2,1,0:T(8,128)S(1)} async-done(((f32[16,128,128]{2,1,0:T(8,128)}), f32[16,128,128]{2,1,0:T(8,128)S(1)}, u32[]{:S(2)}, u32[]{:S(2)}) %all-to-all-start) | async-done | bytes 1048608 | tf_op jit(solution)/shard_map/all_to_all | solution.py:18
  35.4 0.9 reduce-window_convert_fusion
  36.3 4.3 %all-to-all-start.1 = ((bf16[16,128,128]{2,1,0:T(8,128)(2,1)}), bf16[16,128,128]{2,1,0:T(8,128)(2,1)}, u32[]{:S(2)}, u32[]{:S(2)}) async-start(bf16[16,128,128]{2,1,0:T(8,128)(2,1)} %reduce-window_convert_fusion), calls=%async_computation.1 | async-start | bytes 1048576 | tf_op jit(solution)/shard_map/all_to_all | solution.py:21
  40.6 0.0 all-gather.3.cloned.1.call-start
  40.6 0.1 copy.32
  40.8 1.4 copy.35
  42.2 2.7 %fusion.117 = f32[16,256,128]{1,2,0:T(8,128)} fusion(bf16[256,16,128]{0,2,1:T(8,128)(2,1)S(1)} %bitcast.236, pred[256,256]{1,0:T(8,128)(4,1)S(1)} %iota_compare_fusion, bf16[256,16,128]{2,1,0:T(8,128)(2,1)S(1)} %bitcast.238, bf16[256,16,128]{2,1,0:T(8,128)(2,1)S(1)} %bitcast.239), kind=kOutput, calls=%fused_computation.72 | convolution fusion | flops 538968064 | bytes 5308416 | tf_op jit(solution)/shard_map/htu,uhd->thd/dot_general | solution.py:47
  44.9 5.0 %all-to-all-done.1 = bf16[16,128,128]{2,1,0:T(8,128)(2,1)} async-done(((bf16[16,128,128]{2,1,0:T(8,128)(2,1)}), bf16[16,128,128]{2,1,0:T(8,128)(2,1)}, u32[]{:S(2)}, u32[]{:S(2)}) %all-to-all-start.1) | async-done | bytes 524320 | tf_op jit(solution)/shard_map/all_to_all | solution.py:21
  49.9 2.3 multiply_reduce_fusion
  52.2 1.5 broadcast_multiply_fusion
  53.7 1.9 copy.33
  55.7 0.0 copy-done
  55.7 0.0 copy-start.1
  55.7 1.7 fusion.86
  57.4 0.0 copy-done.1
  57.4 0.3 fusion.88
  57.8 1.2 concatenate.7
  59.0 1.1 fusion.178
  60.0 0.0 all-gather.3.cloned.1.call-update
  60.1 0.0 all-gather.5.cloned.1.call-start
  60.1 0.7 all-gather.5.cloned.1.call-update
  60.8 0.0 reduce-scatter.3.cloned.1.call-start
  60.9 31.4 %all-gather.3.cloned.1.call-done = bf16[512,2176]{1,0:T(8,128)(2,1)} async-done(((bf16[128,2176]{1,0:T(8,128)(2,1)}), bf16[512,2176]{1,0:T(8,128)(2,1)}) %all-gather.3.cloned.1.call-update) | async-done | bytes 2228240 | tf_op jit(solution)/shard_map/all_gather | solution.py:95
  92.3 0.8 collective-permute-start
  93.1 32.8 %all-gather.5.cloned.1.call-done = bf16[512,2176]{1,0:T(8,128)(2,1)} async-done(((bf16[128,2176]{1,0:T(8,128)(2,1)}), bf16[512,2176]{1,0:T(8,128)(2,1)}) %all-gather.5.cloned.1.call-update) | async-done | bytes 2228240 | tf_op jit(solution)/shard_map/all_gather | solution.py:95
  125.9 0.8 collective-permute-start.2
  126.7 0.0 collective-permute-done
  126.7 0.1 fusion.159
  126.8 8.3 %fusion.27 = f32[1,512,1408]{2,1,0:T(8,128)} fusion(bf16[1,2048,1408]{2,1,0:T(8,128)(2,1)} %param.19, bf16[512,2176]{1,0:T(8,128)(2,1)S(1)} %collective-permute-done), kind=kOutput, calls=%fused_computation.32 | convolution fusion | flops 2952790016 | bytes 10747904 | tf_op jit(solution)/shard_map/nd,edf->enf/dot_general | solution.py:85
  135.2 0.0 copy-done.6
  135.2 14.0 %multiply_convert_fusion.2 = bf16[512,2048]{1,0:T(8,128)(2,1)} fusion(f32[512]{0:T(512)S(1)} %bitcast.248, bf16[1,1408,2048]{2,1,0:T(8,128)(2,1)} %param.21, bf16[1,2048,1408]{2,1,0:T(8,128)(2,1)} %param.20, bf16[512,2176]{1,0:T(8,128)(2,1)} %copy-done.6, f32[1,512,1408]{2,1,0:T(8,128)} %fusion.27), kind=kOutput, calls=%fused_computation.28 | convolution fusion | flops 5914099712 | bytes 18614272 | tf_op jit(solution)/shard_map/enf,efd->end/dot_general | solution.py:88
  149.1 0.0 collective-permute-start.1
  149.1 0.0 copy-done.5
  149.1 0.1 fusion.161
  149.2 7.7 %fusion.24 = f32[1,512,1408]{2,1,0:T(8,128)} fusion(bf16[1,2048,1408]{2,1,0:T(8,128)(2,1)} %param.19, bf16[512,2176]{1,0:T(8,128)(2,1)S(1)} %copy-done.5), kind=kOutput, calls=%fused_computation.31 | convolution fusion | flops 2952790016 | bytes 10747904 | tf_op jit(solution)/shard_map/nd,edf->enf/dot_general | solution.py:85
  156.9 0.0 collective-permute-done.2
  156.9 1.0 fusion.155
  157.9 8.3 %fusion.33 = f32[1,512,1408]{2,1,0:T(8,128)} fusion(bf16[1,2048,1408]{2,1,0:T(8,128)(2,1)} %param.19, bf16[512,2176]{1,0:T(8,128)(2,1)} %collective-permute-done.2), kind=kOutput, calls=%fused_computation.34 | convolution fusion | flops 2952790016 | bytes 10747904 | tf_op jit(solution)/shard_map/nd,edf->enf/dot_general | solution.py:85
  166.2 0.0 collective-permute-done.1
  166.3 13.8 %add_convert_fusion.1 = bf16[512,2048]{1,0:T(8,128)(2,1)} fusion(bf16[512,2048]{1,0:T(8,128)(2,1)} %collective-permute-done.1, bf16[1,1408,2048]{2,1,0:T(8,128)(2,1)} %param.21, f32[512]{0:T(512)S(1)} %bitcast.246, bf16[1,2048,1408]{2,1,0:T(8,128)(2,1)} %param.20, f32[1,512,1408]{2,1,0:T(8,128)} %fusion.24, bf16[512,2176]{1,0:T(8,128)(2,1)S(1)} %copy-done.5), kind=kOutput, calls=%fused_computation.27 | convolution fusion | flops 5918294016 | bytes 20711424 | tf_op jit(solution)/shard_map/enf,efd->end/dot_general | solution.py:88
  180.1 0.0 reduce-scatter.3.cloned.1.call-update
  180.1 0.3 reduce-scatter.5.cloned.1.call-start
  180.4 0.0 copy-start.4
  180.4 14.0 %multiply_convert_fusion = bf16[512,2048]{1,0:T(8,128)(2,1)} fusion(f32[512]{0:T(512)S(1)} %bitcast.245, bf16[1,1408,2048]{2,1,0:T(8,128)(2,1)} %param.21, bf16[1,2048,1408]{2,1,0:T(8,128)(2,1)} %param.20, bf16[512,2176]{1,0:T(8,128)(2,1)} %collective-permute-done.2, f32[1,512,1408]{2,1,0:T(8,128)} %fusion.33), kind=kOutput, calls=%fused_computation.25 | convolution fusion | flops 5914099712 | bytes 18614272 | tf_op jit(solution)/shard_map/enf,efd->end/dot_general | solution.py:88
  194.4 0.5 collective-permute-start.3
  194.9 0.0 copy-done.4
  194.9 0.1 fusion.157
  195.0 7.7 %fusion.30 = f32[1,512,1408]{2,1,0:T(8,128)} fusion(bf16[1,2048,1408]{2,1,0:T(8,128)(2,1)} %param.19, bf16[512,2176]{1,0:T(8,128)(2,1)S(1)} %copy-done.4), kind=kOutput, calls=%fused_computation.33 | convolution fusion | flops 2952790016 | bytes 10747904 | tf_op jit(solution)/shard_map/nd,edf->enf/dot_general | solution.py:85
  202.7 0.0 collective-permute-done.3
  202.7 14.0 %add_convert_fusion = bf16[512,2048]{1,0:T(8,128)(2,1)} fusion(bf16[512,2048]{1,0:T(8,128)(2,1)} %collective-permute-done.3, bf16[1,1408,2048]{2,1,0:T(8,128)(2,1)} %param.21, f32[512]{0:T(512)S(1)} %bitcast.247, bf16[1,2048,1408]{2,1,0:T(8,128)(2,1)} %param.20, f32[1,512,1408]{2,1,0:T(8,128)} %fusion.30, bf16[512,2176]{1,0:T(8,128)(2,1)S(1)} %copy-done.4), kind=kOutput, calls=%fused_computation.24 | convolution fusion | flops 5918294016 | bytes 20711424 | tf_op jit(solution)/shard_map/enf,efd->end/dot_general | solution.py:88
  216.7 0.0 reduce-scatter.5.cloned.1.call-update
  216.7 0.0 reduce-scatter.3.cloned.1.call-done
  216.8 29.3 %reduce-scatter.5.cloned.1.call-done = bf16[128,2048]{1,0:T(8,128)(2,1)} async-done(((bf16[512,2048]{1,0:T(8,128)(2,1)}), bf16[128,2048]{1,0:T(8,128)(2,1)}) %reduce-scatter.5.cloned.1.call-update) | async-done | bytes 524304 | tf_op jit(solution)/shard_map/reduce_scatter | solution.py:101
  246.1 2.6 %fusion.146 = bf16[1,256,2048]{2,1,0:T(8,128)(2,1)} fusion(bf16[256,2048]{1,0:T(8,128)(2,1)S(1)} %get-tuple-element.6, bf16[128,2048]{1,0:T(8,128)(2,1)} %reduce-scatter.5.cloned.1.call-done, bf16[128,2048]{1,0:T(8,128)(2,1)} %reduce-scatter.3.cloned.1.call-done), kind=kLoop, calls=%fused_computation.74 | loop fusion | flops 3670016 | bytes 3145728 | tf_op jit(solution)/shard_map/broadcast_in_dim | solution.py:103
  (10 shorter events, 0.1 us)
Async XLA Ops:
  9.5 9.9 %copy-start.2 = (f32[1,256,4]{1,2,0:T(4,128)S(1)}, f32[1,256,4]{1,2,0:T(4,128)}, u32[]{:S(2)}) copy-start(f32[1,256,4]{1,2,0:T(4,128)} %param.18) | copy-start | bytes 12292
  9.5 9.9 %copy-start.3 = (s32[1,256,4]{1,2,0:T(4,128)S(1)}, s32[1,256,4]{1,2,0:T(4,128)}, u32[]{:S(2)}) copy-start(s32[1,256,4]{1,2,0:T(4,128)} %param.17) | copy-start | bytes 12292
  10.9 24.5 %all-to-all-start = ((f32[16,128,128]{2,1,0:T(8,128)}), f32[16,128,128]{2,1,0:T(8,128)S(1)}, u32[]{:S(2)}, u32[]{:S(2)}) async-start(f32[16,128,128]{2,1,0:T(8,128)} %fusion.148), calls=%async_computation | async-start | bytes 2097152 | tf_op jit(solution)/shard_map/all_to_all | solution.py:18
  36.3 13.6 %all-to-all-start.1 = ((bf16[16,128,128]{2,1,0:T(8,128)(2,1)}), bf16[16,128,128]{2,1,0:T(8,128)(2,1)}, u32[]{:S(2)}, u32[]{:S(2)}) async-start(bf16[16,128,128]{2,1,0:T(8,128)(2,1)} %reduce-window_convert_fusion), calls=%async_computation.1 | async-start | bytes 1048576 | tf_op jit(solution)/shard_map/all_to_all | solution.py:21
  40.6 51.7 %all-gather.3.cloned.1.call-start = ((), (), s32[]{:S(2)}) async-start(), calls=%async_computation.4 | async-start | bytes 2785280 | tf_op jit(solution)/shard_map/all_gather | solution.py:95
  53.7 1.9 copy-start
  55.7 1.8 copy-start.1
  60.1 65.8 %all-gather.5.cloned.1.call-start = ((), (), s32[]{:S(2)}) async-start(), calls=%async_computation.6 | async-start | bytes 2785280 | tf_op jit(solution)/shard_map/all_gather | solution.py:95
  60.8 155.9 %reduce-scatter.3.cloned.1.call-start = ((), (), s32[]{:S(2)}) async-start(), calls=%async_computation.5 | async-start | bytes 2621440 | tf_op jit(solution)/shard_map/reduce_scatter | solution.py:101
  92.3 34.4 %collective-permute-start = (bf16[512,2176]{1,0:T(8,128)(2,1)}, bf16[512,2176]{1,0:T(8,128)(2,1)S(1)}, u32[]{:S(2)}, u32[]{:S(2)}) collective-permute-start(bf16[512,2176]{1,0:T(8,128)(2,1)} %all-gather.3.cloned.1.call-done), channel_id=1, source_target_pairs={{0,1},{1,0},{2,3},{3,2},{4,5},{5,4},{6,7},{7,6},{8,9},{9,8},{10,11... | collective-permute-start | bytes 6684680 | tf_op jit(solution)/shard_map/ppermute | solution.py:96
  125.9 31.1 %collective-permute-start.2 = (bf16[512,2176]{1,0:T(8,128)(2,1)}, bf16[512,2176]{1,0:T(8,128)(2,1)}, u32[]{:S(2)}, u32[]{:S(2)}) collective-permute-start(bf16[512,2176]{1,0:T(8,128)(2,1)} %all-gather.5.cloned.1.call-done), channel_id=1, source_target_pairs={{0,1},{1,0},{2,3},{3,2},{4,5},{5,4},{6,7},{7,6},{8,9},{9,8},{10,11... | collective-permute-start | bytes 6684680 | tf_op jit(solution)/shard_map/ppermute | solution.py:96
  126.7 8.5 %copy-start.6 = (bf16[512,2176]{1,0:T(8,128)(2,1)}, bf16[512,2176]{1,0:T(8,128)(2,1)S(1)}, u32[]{:S(2)}) copy-start(bf16[512,2176]{1,0:T(8,128)(2,1)S(1)} %collective-permute-done) | copy-start | bytes 6684676
  135.2 14.0 %copy-start.5 = (bf16[512,2176]{1,0:T(8,128)(2,1)S(1)}, bf16[512,2176]{1,0:T(8,128)(2,1)}, u32[]{:S(2)}) copy-start(bf16[512,2176]{1,0:T(8,128)(2,1)} %all-gather.3.cloned.1.call-done) | copy-start | bytes 6684676
  149.1 17.1 %collective-permute-start.1 = (bf16[512,2048]{1,0:T(8,128)(2,1)}, bf16[512,2048]{1,0:T(8,128)(2,1)}, u32[]{:S(2)}, u32[]{:S(2)}) collective-permute-start(bf16[512,2048]{1,0:T(8,128)(2,1)} %multiply_convert_fusion.2), channel_id=1, source_target_pairs={{0,1},{1,0},{2,3},{3,2},{4,5},{5,4},{6,7},{7,6},{8,9},{9,8},{10,11... | collective-permute-start | bytes 6291464 | tf_op jit(solution)/shard_map/ppermute | solution.py:98
  180.1 66.0 %reduce-scatter.5.cloned.1.call-start = ((), (), s32[]{:S(2)}) async-start(), calls=%async_computation.7 | async-start | bytes 2621440 | tf_op jit(solution)/shard_map/reduce_scatter | solution.py:101
  180.4 14.5 %copy-start.4 = (bf16[512,2176]{1,0:T(8,128)(2,1)S(1)}, bf16[512,2176]{1,0:T(8,128)(2,1)}, u32[]{:S(2)}) copy-start(bf16[512,2176]{1,0:T(8,128)(2,1)} %all-gather.5.cloned.1.call-done) | copy-start | bytes 6684676
  194.4 8.4 %collective-permute-start.3 = (bf16[512,2048]{1,0:T(8,128)(2,1)}, bf16[512,2048]{1,0:T(8,128)(2,1)}, u32[]{:S(2)}, u32[]{:S(2)}) collective-permute-start(bf16[512,2048]{1,0:T(8,128)(2,1)} %multiply_convert_fusion), channel_id=1, source_target_pairs={{0,1},{1,0},{2,3},{3,2},{4,5},{5,4},{6,7},{7,6},{8,9},{9,8},{10,11... | collective-permute-start | bytes 6291464 | tf_op jit(solution)/shard_map/ppermute | solution.py:98
Sparse Core Ops, SparseCore 0:
  60.2 32.0 all-gather.2
  93.9 31.8 all-gather.4
  180.2 29.5 reduce-scatter.2
  216.9 29.1 reduce-scatter.4

commit v7 on v6

--- a/solution.py
+++ b/solution.py
@@ -65,8 +65,7 @@
         jnp.where(route_ids[:, :, None] == experts[None, None, :], route_gates[:, :, None], 0.0),
         axis=1,
     )
-    cores = lax.axis_size("core")
-    me = lax.axis_index("y") * cores + lax.axis_index("core")
+    me = lax.axis_index("y") * lax.axis_size("core") + lax.axis_index("core")
     local_count = w_gate.shape[0]
     high = table.astype(jnp.bfloat16)
     rest = table - high.astype(jnp.float32)
@@ -74,11 +73,35 @@
     low = (rest - middle.astype(jnp.float32)).astype(jnp.bfloat16)
     pad = jnp.zeros((positions, 128 - 3 * EXPERTS), jnp.bfloat16)
     payload = jnp.concatenate([normed, high, middle, low, pad], axis=1)
+
     columns = jnp.arange(3 * EXPERTS, dtype=jnp.int32) % EXPERTS
     select = (columns[:, None] == me * local_count + jnp.arange(local_count)[None, :]).astype(jnp.bfloat16)
-    swap = [(i, (i + 1) % cores) for i in range(cores)]
+    chips = lax.axis_size("y")
+    cores = lax.axis_size("core")
+    ring = lax.axis_index("y")
+    core = lax.axis_index("core")
 
-    def expert(gathered):
+    def shift(x, axis, step, size):
+        return lax.ppermute(x, axis, [(i, (i + step) % size) for i in range(size)])
+
+    def gather_rows(x):
+        n = x.shape[0]
+        half = n // 2
+        prev = shift(x, "y", 1, chips)
+        nxt = shift(x, "y", -1, chips)
+        far = jnp.concatenate([shift(prev[:half], "y", 1, chips), shift(nxt[half:], "y", -1, chips)], axis=0)
+        relative = jnp.stack([x, nxt, far, prev])
+        doubled = jnp.concatenate([relative, relative], axis=0)
+        same = lax.dynamic_slice_in_dim(doubled, (chips - ring) % chips, chips, axis=0)
+        other = shift(same, "core", 1, cores)
+        first = jnp.where(core == 0, same, other)
+        second = jnp.where(core == 0, other, same)
+        return jnp.stack([first, second], axis=1).reshape(chips * cores * n, x.shape[1])
+
+    chunk = positions // CHUNKS
+    outs = []
+    for c in range(CHUNKS):
+        gathered = gather_rows(payload[c * chunk:(c + 1) * chunk])
         rows = gathered[:, :D]
         code = gathered[:, D:D + 3 * EXPERTS]
         weight = jnp.dot(code, select, preferred_element_type=jnp.float32)
@@ -87,18 +110,8 @@
         hidden = (jax.nn.silu(gate_part) * up_part).astype(jnp.bfloat16)
         result = jnp.einsum("enf,efd->end", hidden, w_down, preferred_element_type=jnp.float32)
         result = result.astype(jnp.bfloat16).astype(jnp.float32)
-        return jnp.sum(result * weight.T[:, :, None], axis=0).astype(jnp.bfloat16)
-
-    chunk = positions // CHUNKS
-    outs = []
-    for c in range(CHUNKS):
-        own = lax.all_gather(payload[c * chunk:(c + 1) * chunk], "y", axis=0, tiled=True)
-        other = lax.ppermute(own, "core", swap)
-        back = expert(other)
-        returned = lax.ppermute(back, "core", swap)
-        mine = expert(own)
-        total = (mine.astype(jnp.float32) + returned.astype(jnp.float32)).astype(jnp.bfloat16)
-        outs.append(lax.psum_scatter(total, "y", scatter_dimension=0, tiled=True))
+        contrib = jnp.sum(result * weight.T[:, :, None], axis=0).astype(jnp.bfloat16)
+        outs.append(lax.psum_scatter(contrib, ("y", "core"), scatter_dimension=0, tiled=True))
     combined = jnp.concatenate(outs, axis=0)
     return (resid_float + combined.astype(jnp.float32)).astype(jnp.bfloat16)[None]
 

time: 256 us -> 233 us (0.910)
  waiting for transfers between devices: 115 us -> 83.4 us
  matrix products: 95.6 us -> 65.8 us
  local copies, waits for them, and re-layouts: 8.95 us -> 26 us
  starting transfers between devices: 15.3 us -> 28.5 us
  other arithmetic: 7.05 us -> 13 us
    all_gather x2 -> x0, waiting for transfers between devices: 64.1 us -> none  [on_device(): lax.all_gather(payload[c * chunk:(c + 1) * chunk], 'y', axis=0, tiled=True)]
    dot_general x12 -> x6, matrix products: 89.2 us -> 59.4 us  [the longest x2 42.2 us: on_device(): jnp.einsum('enf,efd->end', hidden, w_down, preferred_element_type=jnp.flo...]
    ppermute x4 -> x10, waiting for transfers between devices: 0.01 us -> 26.9 us  [shift(): return lax.ppermute(x, axis, [(i, (i + step) % size) for i in range(size)])]
    ppermute x4 -> x10, starting transfers between devices: 2.19 us -> 15.5 us  [shift(): return lax.ppermute(x, axis, [(i, (i + step) % size) for i in range(size)])]
    unnamed x16 -> x35, local copies, waits for them, and re-layouts: 2.93 us -> 14.5 us
    reduce_scatter x2, waiting for transfers between devices: 29.3 us -> 35.7 us  [on_device(): lax.psum_scatter(contrib, ('y', 'core'), scatter_dimension=0, tiled=True)]
    another operation x0 -> x4, other arithmetic: none -> 4.95 us  [gather_rows(): jnp.stack([first, second], axis=1).reshape(chips * cores * n, x.shape[1])]
    dynamic_slice x0 -> x2, local copies, waits for them, and re-layouts: none -> 4.71 us  [gather_rows(): lax.dynamic_slice_in_dim(doubled, (chips - ring) % chips, chips, axis=0)]
  transfers between devices with their start and end apart: 10 -> 14, of which waited for: 5 -> 7; matrix products, arithmetic and copies ran while one was open for 31% -> 33% of each run, Pallas kernels for 0% -> 0%
where the time goes in v7:
time: 233 us; the launch traced here: 231 us
  waiting for transfers between devices  83.4 us (36%)
  matrix products  65.8 us (28%)
  starting transfers between devices  28.5 us (12%)
  local copies, waits for them, and re-layouts  26 us (11%)
  between operations  13.9 us (6%)
  other arithmetic  13 us (6%)
    dot_general x2, matrix products, on_device(): jnp.einsum('enf,efd->end', hidden, w_down, preferred_element_type=jnp.flo...  42.2 us
    reduce_scatter x2, waiting for transfers between devices, on_device(): lax.psum_scatter(contrib, ('y', 'core'), scatter_dimension=0, tiled=True)  35.7 us
    ppermute x10, waiting for transfers between devices, shift(): return lax.ppermute(x, axis, [(i, (i + step) % size) for i in range(size)])  26.9 us
    dot_general x2, matrix products, on_device(): jnp.einsum('nd,edf->enf', rows, w_up, preferred_element_type=jnp.float32)  16.9 us
    all_to_all x1, waiting for transfers between devices, block_prefix(): lax.all_to_all(pieces, 'seq', split_axis=0, concat_axis=0, tiled=True)  15.8 us
    ppermute x10, starting transfers between devices, shift(): return lax.ppermute(x, axis, [(i, (i + step) % size) for i in range(size)])  15.5 us
    unnamed x35, local copies, waits for them, and re-layouts  14.5 us
    all_to_all x1, starting transfers between devices, block_prefix(): lax.all_to_all(pieces, 'seq', split_axis=0, concat_axis=0, tiled=True)  8.42 us
  transfers between devices with their start and end apart: 14, of which 7 were waited for; matrix products, arithmetic and copies ran while one was open for 33% of the time, Pallas kernels for 0%

profile of v7, /device:TPU:1, one launch (start us, length us, event | category | flops | bytes accessed | tf_op | source)
XLA Modules:
  0.0 230.6 jit_solution(16047537323772621715)
XLA Ops:
  6.5 1.5 copy.49
  8.0 1.5 copy.51
  9.5 1.4 fusion.60
  10.9 8.4 %all-to-all-start = ((f32[16,128,128]{2,1,0:T(8,128)}), f32[16,128,128]{2,1,0:T(8,128)S(1)}, u32[]{:S(2)}, u32[]{:S(2)}) async-start(f32[16,128,128]{2,1,0:T(8,128)} %fusion.60), calls=%async_computation | async-start | bytes 2097152 | tf_op jit(solution)/shard_map/all_to_all | solution.py:18
  19.4 0.1 copy.43
  19.6 0.1 copy.44
  19.7 15.8 %all-to-all-done = f32[16,128,128]{2,1,0:T(8,128)S(1)} async-done(((f32[16,128,128]{2,1,0:T(8,128)}), f32[16,128,128]{2,1,0:T(8,128)S(1)}, u32[]{:S(2)}, u32[]{:S(2)}) %all-to-all-start) | async-done | bytes 1048608 | tf_op jit(solution)/shard_map/all_to_all | solution.py:18
  35.4 0.9 reduce-window_convert_fusion
  36.3 4.3 %all-to-all-start.1 = ((bf16[16,128,128]{2,1,0:T(8,128)(2,1)}), bf16[16,128,128]{2,1,0:T(8,128)(2,1)}, u32[]{:S(2)}, u32[]{:S(2)}) async-start(bf16[16,128,128]{2,1,0:T(8,128)(2,1)} %reduce-window_convert_fusion), calls=%async_computation.1 | async-start | bytes 1048576 | tf_op jit(solution)/shard_map/all_to_all | solution.py:21
  40.6 0.1 copy.45
  40.8 1.5 copy.50
  42.3 2.7 %fusion.57 = f32[16,256,128]{1,2,0:T(8,128)} fusion(bf16[256,16,128]{0,2,1:T(8,128)(2,1)S(1)} %bitcast.184, pred[256,256]{1,0:T(8,128)(4,1)S(1)} %iota_compare_fusion, bf16[256,16,128]{2,1,0:T(8,128)(2,1)S(1)} %bitcast.186, bf16[256,16,128]{2,1,0:T(8,128)(2,1)S(1)} %bitcast.187), kind=kOutput, calls=%fused_computation.54 | convolution fusion | flops 538968064 | bytes 5308416 | tf_op jit(solution)/shard_map/htu,uhd->thd/dot_general | solution.py:47
  45.0 5.0 %all-to-all-done.1 = bf16[16,128,128]{2,1,0:T(8,128)(2,1)} async-done(((bf16[16,128,128]{2,1,0:T(8,128)(2,1)}), bf16[16,128,128]{2,1,0:T(8,128)(2,1)}, u32[]{:S(2)}, u32[]{:S(2)}) %all-to-all-start.1) | async-done | bytes 524320 | tf_op jit(solution)/shard_map/all_to_all | solution.py:21
  49.9 2.3 multiply_reduce_fusion
  52.3 1.5 broadcast_multiply_fusion
  53.8 1.9 copy.48
  55.7 1.7 fusion.52
  57.5 0.3 fusion.54
  57.8 1.2 concatenate.21
  59.0 0.1 fusion.89
  59.1 2.8 %collective-permute-start.5 = (bf16[128,2176]{1,0:T(8,128)(2,1)S(1)}, bf16[128,2176]{1,0:T(8,128)(2,1)S(1)}, u32[]{:S(2)}, u32[]{:S(2)}) collective-permute-start(bf16[128,2176]{1,0:T(8,128)(2,1)S(1)} %get-tuple-element.14), channel_id=1, source_target_pairs={{0,6},{2,0},{4,2},{6,4},{1,7},{3,1},{5,3},{7,5},{8,14},{10,8},{12,... | collective-permute-start | bytes 1671176 | tf_op jit(solution)/shard_map/ppermute | solution.py:85
  61.9 2.7 %collective-permute-start = (bf16[128,2176]{1,0:T(8,128)(2,1)S(1)}, bf16[128,2176]{1,0:T(8,128)(2,1)S(1)}, u32[]{:S(2)}, u32[]{:S(2)}) collective-permute-start(bf16[128,2176]{1,0:T(8,128)(2,1)S(1)} %get-tuple-element.13), channel_id=1, source_target_pairs={{0,6},{2,0},{4,2},{6,4},{1,7},{3,1},{5,3},{7,5},{8,14},{10,8},{12,... | collective-permute-start | bytes 1671176 | tf_op jit(solution)/shard_map/ppermute | solution.py:85
  64.5 0.1 bitcast_dynamic-update-slice_fusion.10
  64.6 9.0 %collective-permute-done.6 = bf16[128,2176]{1,0:T(8,128)(2,1)S(1)} collective-permute-done((bf16[128,2176]{1,0:T(8,128)(2,1)S(1)}, bf16[128,2176]{1,0:T(8,128)(2,1)S(1)}, u32[]{:S(2)}, u32[]{:S(2)}) %collective-permute-start.6) | collective-permute-done | bytes 557088 | tf_op jit(solution)/shard_map/ppermute | solution.py:85
  73.7 0.1 collective-permute-start.7
  73.8 2.7 %collective-permute-start.8 = (bf16[64,2176]{1,0:T(8,128)(2,1)S(1)}, bf16[64,2176]{1,0:T(8,128)(2,1)S(1)}, u32[]{:S(2)}, u32[]{:S(2)}) collective-permute-start(bf16[64,2176]{1,0:T(8,128)(2,1)S(1)} %slice.52), channel_id=1, source_target_pairs={{0,6},{2,0},{4,2},{6,4},{1,7},{3,1},{5,3},{7,5},{8,14},{10,8},{12,... | collective-permute-start | bytes 835592 | tf_op jit(solution)/shard_map/ppermute | solution.py:85
  76.5 9.1 %collective-permute-done.1 = bf16[128,2176]{1,0:T(8,128)(2,1)S(1)} collective-permute-done((bf16[128,2176]{1,0:T(8,128)(2,1)S(1)}, bf16[128,2176]{1,0:T(8,128)(2,1)S(1)}, u32[]{:S(2)}, u32[]{:S(2)}) %collective-permute-start.1) | collective-permute-done | bytes 557088 | tf_op jit(solution)/shard_map/ppermute | solution.py:85
  85.6 0.1 collective-permute-start.2
  85.7 2.7 %collective-permute-start.3 = (bf16[64,2176]{1,0:T(8,128)(2,1)S(1)}, bf16[64,2176]{1,0:T(8,128)(2,1)S(1)}, u32[]{:S(2)}, u32[]{:S(2)}) collective-permute-start(bf16[64,2176]{1,0:T(8,128)(2,1)S(1)} %slice.47), channel_id=1, source_target_pairs={{0,6},{2,0},{4,2},{6,4},{1,7},{3,1},{5,3},{7,5},{8,14},{10,8},{12,... | collective-permute-start | bytes 835592 | tf_op jit(solution)/shard_map/ppermute | solution.py:85
  88.4 0.1 bitcast_dynamic-update-slice_fusion.2
  88.5 0.1 bitcast_dynamic-update-slice_fusion.8
  88.6 3.0 %collective-permute-done.7 = bf16[64,2176]{1,0:T(8,128)(2,1)S(1)} collective-permute-done((bf16[64,2176]{1,0:T(8,128)(2,1)S(1)}, bf16[64,2176]{1,0:T(8,128)(2,1)S(1)}, u32[]{:S(2)}, u32[]{:S(2)}) %collective-permute-start.7) | collective-permute-done | bytes 278560 | tf_op jit(solution)/shard_map/ppermute | solution.py:85
  91.6 0.1 bitcast_dynamic-update-slice_fusion
  91.7 5.8 %collective-permute-done.2 = bf16[64,2176]{1,0:T(8,128)(2,1)S(1)} collective-permute-done((bf16[64,2176]{1,0:T(8,128)(2,1)S(1)}, bf16[64,2176]{1,0:T(8,128)(2,1)S(1)}, u32[]{:S(2)}, u32[]{:S(2)}) %collective-permute-start.2) | collective-permute-done | bytes 278560 | tf_op jit(solution)/shard_map/ppermute | solution.py:85
  97.6 0.1 bitcast_dynamic-update-slice_fusion.6
  97.6 0.1 bitcast_dynamic-update-slice_fusion.11
  97.8 0.1 bitcast_dynamic-update-slice_fusion.3
  98.0 0.1 fusion.70
  98.0 2.0 copy-done.2
  100.1 2.0 copy-done
  102.2 1.5 constant_dynamic-slice_fusion.1
  103.7 4.5 %collective-permute-start.4 = (bf16[4,128,2176]{2,1,0:T(8,128)(2,1)}, bf16[4,128,2176]{2,1,0:T(8,128)(2,1)}, u32[]{:S(2)}, u32[]{:S(2)}) collective-permute-start(bf16[4,128,2176]{2,1,0:T(8,128)(2,1)} %constant_dynamic-slice_fusion.1), channel_id=1, source_target_pairs={{0,1},{1,0},{2,3},{3,2},{4,5},{5,4},{6,7},{7,6},{8,9},{9,8},{10,11... | collective-permute-start | bytes 6684680 | tf_op jit(solution)/shard_map/ppermute | solution.py:85
  108.2 0.8 fusion.68
  109.0 0.9 bitcast_dynamic-update-slice_fusion.1
  109.9 3.2 %constant_dynamic-slice_fusion = bf16[4,128,2176]{2,1,0:T(8,128)(2,1)} fusion(bf16[8,128,2176]{2,1,0:T(8,128)(2,1)} %bitcast_dynamic-update-slice_fusion.1, s32[]{:T(128)S(6)} %select_n.56), kind=kLoop, calls=%fused_computation.98 | loop fusion | bytes 4456452 | tf_op jit(solution)/shard_map/dynamic_slice | solution.py:95
  113.1 2.0 select_bitcast_fusion.3
  115.1 0.4 pad_maximum_fusion
  115.6 0.4 copy.46
  116.0 2.3 %slice-done = s8[4194304]{0:T(1024)(128)(4,1)S(1)} async-done(((s8[5767168]{0:T(1024)(128)(4,1)}), s8[4194304]{0:T(1024)(128)(4,1)S(1)}, s32[]{:S(2)}) %slice-start) | async-done | bytes 4194328
  118.3 1.2 slice-done.1
  119.5 8.5 %fusion.11 = f32[1024,1408]{1,0:T(8,128)} fusion(bf16[1,2048,1408]{2,1,0:T(8,128)(2,1)S(1)} %bitcast.194, bf16[1024,2176]{1,0:T(8,128)(2,1)S(1)} %bitcast.180), kind=kOutput, calls=%fused_computation.17 | convolution fusion | flops 5905580032 | bytes 15728640 | tf_op jit(solution)/shard_map/nd,edf->enf/dot_general | solution.py:109
  128.0 0.2 fusion.73
  128.1 21.0 %multiply_convert_fusion.1 = bf16[1024,2048]{1,0:T(8,128)(2,1)} fusion(f32[1024]{0:T(1024)S(1)} %bitcast.198, bf16[1,1408,2048]{2,1,0:T(8,128)(2,1)} %param.21, f32[1024,1408]{1,0:T(8,128)} %fusion.11, bf16[1,2048,1408]{2,1,0:T(8,128)(2,1)} %param.19, bf16[1024,2176]{1,0:T(8,128)(2,1)} %bitcast.182), kind=kOutput, calls=%fused_computation.1 | convolution fusion | flops 11828199424 | bytes 25694208 | tf_op jit(solution)/shard_map/enf,efd->end/dot_general | solution.py:111
  149.1 0.3 reduce-scatter.5.cloned.1.call-start
  149.4 2.0 select_bitcast_fusion.1
  151.5 0.4 pad_maximum_fusion.1
  151.9 0.4 copy.47
  152.4 0.2 fusion.71
  152.5 1.9 slice-done.2
  154.5 1.4 slice-done.3
  155.9 8.4 %fusion.9 = f32[1024,1408]{1,0:T(8,128)} fusion(bf16[1,2048,1408]{2,1,0:T(8,128)(2,1)S(1)} %bitcast.196, bf16[1024,2176]{1,0:T(8,128)(2,1)S(1)} %bitcast.178), kind=kOutput, calls=%fused_computation.15 | convolution fusion | flops 5905580032 | bytes 15728640 | tf_op jit(solution)/shard_map/nd,edf->enf/dot_general | solution.py:109
  164.3 21.2 %multiply_convert_fusion = bf16[1024,2048]{1,0:T(8,128)(2,1)} fusion(f32[1024]{0:T(1024)S(1)} %bitcast.197, bf16[1,1408,2048]{2,1,0:T(8,128)(2,1)} %param.21, f32[1024,1408]{1,0:T(8,128)} %fusion.9, bf16[1,2048,1408]{2,1,0:T(8,128)(2,1)} %param.19, bf16[1024,2176]{1,0:T(8,128)(2,1)} %bitcast.179), kind=kOutput, calls=%fused_computation | convolution fusion | flops 11828199424 | bytes 25694208 | tf_op jit(solution)/shard_map/enf,efd->end/dot_general | solution.py:111
  185.5 35.7 %reduce-scatter.5.cloned.1.call-done = bf16[128,2048]{1,0:T(8,128)(2,1)} async-done(((bf16[1024,2048]{1,0:T(8,128)(2,1)}), bf16[128,2048]{1,0:T(8,128)(2,1)}) %reduce-scatter.5.cloned.1.call-update) | async-done | bytes 524304 | tf_op jit(solution)/shard_map/reduce_scatter | solution.py:114
  221.2 2.6 %fusion.58 = bf16[1,256,2048]{2,1,0:T(8,128)(2,1)} fusion(bf16[256,2048]{1,0:T(8,128)(2,1)S(1)} %get-tuple-element.6, bf16[128,2048]{1,0:T(8,128)(2,1)} %reduce-scatter.5.cloned.1.call-done, bf16[128,2048]{1,0:T(8,128)(2,1)} %reduce-scatter.3.cloned.1.call-done), kind=kLoop, calls=%fused_computation.56 | loop fusion | flops 3670016 | bytes 3145728 | tf_op jit(solution)/shard_map/broadcast_in_dim | solution.py:116
  (49 shorter events, 0.5 us)
Async XLA Ops:
  6.5 12.8 %copy-start.8 = (s32[1,256,4]{1,2,0:T(4,128)S(1)}, s32[1,256,4]{1,2,0:T(4,128)}, u32[]{:S(2)}) copy-start(s32[1,256,4]{1,2,0:T(4,128)} %param.17) | copy-start | bytes 12292
  6.5 12.9 %copy-start.7 = (f32[1,256,4]{1,2,0:T(4,128)S(1)}, f32[1,256,4]{1,2,0:T(4,128)}, u32[]{:S(2)}) copy-start(f32[1,256,4]{1,2,0:T(4,128)} %param.18) | copy-start | bytes 12292
  10.9 24.5 %all-to-all-start = ((f32[16,128,128]{2,1,0:T(8,128)}), f32[16,128,128]{2,1,0:T(8,128)S(1)}, u32[]{:S(2)}, u32[]{:S(2)}) async-start(f32[16,128,128]{2,1,0:T(8,128)} %fusion.60), calls=%async_computation | async-start | bytes 2097152 | tf_op jit(solution)/shard_map/all_to_all | solution.py:18
  36.3 13.6 %all-to-all-start.1 = ((bf16[16,128,128]{2,1,0:T(8,128)(2,1)}), bf16[16,128,128]{2,1,0:T(8,128)(2,1)}, u32[]{:S(2)}, u32[]{:S(2)}) async-start(bf16[16,128,128]{2,1,0:T(8,128)(2,1)} %reduce-window_convert_fusion), calls=%async_computation.1 | async-start | bytes 1048576 | tf_op jit(solution)/shard_map/all_to_all | solution.py:21
  40.6 145.0 %reduce-scatter.3.cloned.1.call-start = ((), (), s32[]{:S(2)}) async-start(), calls=%async_computation.4 | async-start | bytes 4718592 | tf_op jit(solution)/shard_map/reduce_scatter | solution.py:114
  52.2 3.5 %copy-start.5 = (f32[2048]{0:T(1024)S(1)}, f32[2048]{0:T(1024)}, u32[]{:S(2)}) copy-start(f32[2048]{0:T(1024)} %param.15) | copy-start | bytes 24580
  53.8 3.7 %copy-start.6 = (f32[2048]{0:T(1024)S(1)}, f32[2048]{0:T(1024)}, u32[]{:S(2)}) copy-start(f32[2048]{0:T(1024)} %param.16) | copy-start | bytes 24580
  59.1 14.7 %collective-permute-start.5 = (bf16[128,2176]{1,0:T(8,128)(2,1)S(1)}, bf16[128,2176]{1,0:T(8,128)(2,1)S(1)}, u32[]{:S(2)}, u32[]{:S(2)}) collective-permute-start(bf16[128,2176]{1,0:T(8,128)(2,1)S(1)} %get-tuple-element.14), channel_id=1, source_target_pairs={{0,6},{2,0},{4,2},{6,4},{1,7},{3,1},{5,3},{7,5},{8,14},{10,8},{12,... | collective-permute-start | bytes 1671176 | tf_op jit(solution)/shard_map/ppermute | solution.py:85
  61.8 11.8 %collective-permute-start.6 = (bf16[128,2176]{1,0:T(8,128)(2,1)S(1)}, bf16[128,2176]{1,0:T(8,128)(2,1)S(1)}, u32[]{:S(2)}, u32[]{:S(2)}) collective-permute-start(bf16[128,2176]{1,0:T(8,128)(2,1)S(1)} %get-tuple-element.14), channel_id=1, source_target_pairs={{0,2},{2,4},{4,6},{6,0},{1,3},{3,5},{5,7},{7,1},{8,10},{10,12},{12... | collective-permute-start | bytes 1671176 | tf_op jit(solution)/shard_map/ppermute | solution.py:85
  61.9 23.8 %collective-permute-start = (bf16[128,2176]{1,0:T(8,128)(2,1)S(1)}, bf16[128,2176]{1,0:T(8,128)(2,1)S(1)}, u32[]{:S(2)}, u32[]{:S(2)}) collective-permute-start(bf16[128,2176]{1,0:T(8,128)(2,1)S(1)} %get-tuple-element.13), channel_id=1, source_target_pairs={{0,6},{2,0},{4,2},{6,4},{1,7},{3,1},{5,3},{7,5},{8,14},{10,8},{12,... | collective-permute-start | bytes 1671176 | tf_op jit(solution)/shard_map/ppermute | solution.py:85
  64.5 21.1 %collective-permute-start.1 = (bf16[128,2176]{1,0:T(8,128)(2,1)S(1)}, bf16[128,2176]{1,0:T(8,128)(2,1)S(1)}, u32[]{:S(2)}, u32[]{:S(2)}) collective-permute-start(bf16[128,2176]{1,0:T(8,128)(2,1)S(1)} %get-tuple-element.13), channel_id=1, source_target_pairs={{0,2},{2,4},{4,6},{6,0},{1,3},{3,5},{5,7},{7,1},{8,10},{10,12},{12... | collective-permute-start | bytes 1671176 | tf_op jit(solution)/shard_map/ppermute | solution.py:85
  73.7 17.9 %collective-permute-start.7 = (bf16[64,2176]{1,0:T(8,128)(2,1)S(1)}, bf16[64,2176]{1,0:T(8,128)(2,1)S(1)}, u32[]{:S(2)}, u32[]{:S(2)}) collective-permute-start(bf16[64,2176]{1,0:T(8,128)(2,1)S(1)} %slice.51), channel_id=1, source_target_pairs={{0,2},{2,4},{4,6},{6,0},{1,3},{3,5},{5,7},{7,1},{8,10},{10,12},{12... | collective-permute-start | bytes 835592 | tf_op jit(solution)/shard_map/ppermute | solution.py:85
  73.8 17.8 %collective-permute-start.8 = (bf16[64,2176]{1,0:T(8,128)(2,1)S(1)}, bf16[64,2176]{1,0:T(8,128)(2,1)S(1)}, u32[]{:S(2)}, u32[]{:S(2)}) collective-permute-start(bf16[64,2176]{1,0:T(8,128)(2,1)S(1)} %slice.52), channel_id=1, source_target_pairs={{0,6},{2,0},{4,2},{6,4},{1,7},{3,1},{5,3},{7,5},{8,14},{10,8},{12,... | collective-permute-start | bytes 835592 | tf_op jit(solution)/shard_map/ppermute | solution.py:85
  85.6 11.9 %collective-permute-start.2 = (bf16[64,2176]{1,0:T(8,128)(2,1)S(1)}, bf16[64,2176]{1,0:T(8,128)(2,1)S(1)}, u32[]{:S(2)}, u32[]{:S(2)}) collective-permute-start(bf16[64,2176]{1,0:T(8,128)(2,1)S(1)} %slice.46), channel_id=1, source_target_pairs={{0,2},{2,4},{4,6},{6,0},{1,3},{3,5},{5,7},{7,1},{8,10},{10,12},{12... | collective-permute-start | bytes 835592 | tf_op jit(solution)/shard_map/ppermute | solution.py:85
  85.7 11.8 %collective-permute-start.3 = (bf16[64,2176]{1,0:T(8,128)(2,1)S(1)}, bf16[64,2176]{1,0:T(8,128)(2,1)S(1)}, u32[]{:S(2)}, u32[]{:S(2)}) collective-permute-start(bf16[64,2176]{1,0:T(8,128)(2,1)S(1)} %slice.47), channel_id=1, source_target_pairs={{0,6},{2,0},{4,2},{6,4},{1,7},{3,1},{5,3},{7,5},{8,14},{10,8},{12,... | collective-permute-start | bytes 835592 | tf_op jit(solution)/shard_map/ppermute | solution.py:85
  98.0 2.1 copy-start.2
  100.1 2.1 copy-start
  103.7 9.4 %collective-permute-start.4 = (bf16[4,128,2176]{2,1,0:T(8,128)(2,1)}, bf16[4,128,2176]{2,1,0:T(8,128)(2,1)}, u32[]{:S(2)}, u32[]{:S(2)}) collective-permute-start(bf16[4,128,2176]{2,1,0:T(8,128)(2,1)} %constant_dynamic-slice_fusion.1), channel_id=1, source_target_pairs={{0,1},{1,0},{2,3},{3,2},{4,5},{5,4},{6,7},{7,6},{8,9},{9,8},{10,11... | collective-permute-start | bytes 6684680 | tf_op jit(solution)/shard_map/ppermute | solution.py:85
  108.2 4.9 %copy-start.1 = (bf16[8,128,2176]{2,1,0:T(8,128)(2,1)S(1)}, bf16[8,128,2176]{2,1,0:T(8,128)(2,1)}, u32[]{:S(2)}) copy-start(bf16[8,128,2176]{2,1,0:T(8,128)(2,1)} %copy-done) | copy-start | bytes 13369348
  113.1 36.4 %collective-permute-start.9 = (bf16[4,128,2176]{2,1,0:T(8,128)(2,1)}, bf16[4,128,2176]{2,1,0:T(8,128)(2,1)S(1)}, u32[]{:S(2)}, u32[]{:S(2)}) collective-permute-start(bf16[4,128,2176]{2,1,0:T(8,128)(2,1)} %constant_dynamic-slice_fusion), channel_id=1, source_target_pairs={{0,1},{1,0},{2,3},{3,2},{4,5},{5,4},{6,7},{7,6},{8,9},{9,8},{10,11... | collective-permute-start | bytes 6684680 | tf_op jit(solution)/shard_map/ppermute | solution.py:85
  115.1 3.2 %slice-start = ((s8[5767168]{0:T(1024)(128)(4,1)}), s8[4194304]{0:T(1024)(128)(4,1)S(1)}, s32[]{:S(2)}) async-start(s8[5767168]{0:T(1024)(128)(4,1)} %bitcast.193), calls=%async_computation.6 | async-start | bytes 8388608
  115.6 3.9 %slice-start.1 = ((s8[5767168]{0:T(1024)(128)(4,1)}), s8[1572864]{0:T(1024)(128)(4,1)S(1)}, s32[]{:S(2)}) async-start(s8[5767168]{0:T(1024)(128)(4,1)} %bitcast.193), calls=%async_computation.7 | async-start | bytes 3145728
  116.0 12.0 %copy-start.4 = (bf16[4,2,128,2176]{3,2,1,0:T(8,128)(2,1)}, bf16[4,2,128,2176]{3,2,1,0:T(8,128)(2,1)S(1)}, u32[]{:S(2)}) copy-start(bf16[4,2,128,2176]{3,2,1,0:T(8,128)(2,1)S(1)} %copy.46) | copy-start | bytes 13369348
  149.1 72.1 %reduce-scatter.5.cloned.1.call-start = ((), (), s32[]{:S(2)}) async-start(), calls=%async_computation.5 | async-start | bytes 4718592 | tf_op jit(solution)/shard_map/reduce_scatter | solution.py:114
  151.5 3.0 %slice-start.2 = ((s8[5767168]{0:T(1024)(128)(4,1)}), s8[4194304]{0:T(1024)(128)(4,1)S(1)}, s32[]{:S(2)}) async-start(s8[5767168]{0:T(1024)(128)(4,1)} %bitcast.195), calls=%async_computation.8 | async-start | bytes 8388608
  151.9 3.9 %slice-start.3 = ((s8[5767168]{0:T(1024)(128)(4,1)}), s8[1572864]{0:T(1024)(128)(4,1)S(1)}, s32[]{:S(2)}) async-start(s8[5767168]{0:T(1024)(128)(4,1)} %bitcast.195), calls=%async_computation.9 | async-start | bytes 3145728
  152.4 11.9 %copy-start.3 = (bf16[4,2,128,2176]{3,2,1,0:T(8,128)(2,1)}, bf16[4,2,128,2176]{3,2,1,0:T(8,128)(2,1)S(1)}, u32[]{:S(2)}) copy-start(bf16[4,2,128,2176]{3,2,1,0:T(8,128)(2,1)S(1)} %copy.47) | copy-start | bytes 13369348
Sparse Core Ops, SparseCore 0:
  149.3 32.6 reduce-scatter.2
  185.6 35.5 reduce-scatter.4

commit v8 on v6

--- a/solution.py
+++ b/solution.py
@@ -65,8 +65,10 @@
         jnp.where(route_ids[:, :, None] == experts[None, None, :], route_gates[:, :, None], 0.0),
         axis=1,
     )
+    chips = lax.axis_size("y")
     cores = lax.axis_size("core")
-    me = lax.axis_index("y") * cores + lax.axis_index("core")
+    core = lax.axis_index("core")
+    me = lax.axis_index("y") * cores + core
     local_count = w_gate.shape[0]
     high = table.astype(jnp.bfloat16)
     rest = table - high.astype(jnp.float32)
@@ -74,11 +76,13 @@
     low = (rest - middle.astype(jnp.float32)).astype(jnp.bfloat16)
     pad = jnp.zeros((positions, 128 - 3 * EXPERTS), jnp.bfloat16)
     payload = jnp.concatenate([normed, high, middle, low, pad], axis=1)
+
     columns = jnp.arange(3 * EXPERTS, dtype=jnp.int32) % EXPERTS
     select = (columns[:, None] == me * local_count + jnp.arange(local_count)[None, :]).astype(jnp.bfloat16)
-    swap = [(i, (i + 1) % cores) for i in range(cores)]
-
-    def expert(gathered):
+    chunk = positions // CHUNKS
+    outs = []
+    for c in range(CHUNKS):
+        gathered = lax.all_gather(payload[c * chunk:(c + 1) * chunk], ("y", "core"), axis=0, tiled=True)
         rows = gathered[:, :D]
         code = gathered[:, D:D + 3 * EXPERTS]
         weight = jnp.dot(code, select, preferred_element_type=jnp.float32)
@@ -87,20 +91,16 @@
         hidden = (jax.nn.silu(gate_part) * up_part).astype(jnp.bfloat16)
         result = jnp.einsum("enf,efd->end", hidden, w_down, preferred_element_type=jnp.float32)
         result = result.astype(jnp.bfloat16).astype(jnp.float32)
-        return jnp.sum(result * weight.T[:, :, None], axis=0).astype(jnp.bfloat16)
-
-    chunk = positions // CHUNKS
-    outs = []
-    for c in range(CHUNKS):
-        own = lax.all_gather(payload[c * chunk:(c + 1) * chunk], "y", axis=0, tiled=True)
-        other = lax.ppermute(own, "core", swap)
-        back = expert(other)
-        returned = lax.ppermute(back, "core", swap)
-        mine = expert(own)
-        total = (mine.astype(jnp.float32) + returned.astype(jnp.float32)).astype(jnp.bfloat16)
-        outs.append(lax.psum_scatter(total, "y", scatter_dimension=0, tiled=True))
-    combined = jnp.concatenate(outs, axis=0)
-    return (resid_float + combined.astype(jnp.float32)).astype(jnp.bfloat16)[None]
+        contrib = jnp.sum(result * weight.T[:, :, None], axis=0).astype(jnp.bfloat16)
+        paired = contrib.reshape(chips, cores, chunk, D)
+        mine = lax.dynamic_index_in_dim(paired, core, axis=1, keepdims=False)
+        theirs = lax.dynamic_index_in_dim(paired, (core + 1) % cores, axis=1, keepdims=False)
+        received = lax.ppermute(theirs, "core", [(i, (i + 1) % cores) for i in range(cores)])
+        total = (mine.astype(jnp.float32) + received.astype(jnp.float32)).astype(jnp.bfloat16)
+        combined = lax.psum_scatter(total.reshape(chips * chunk, D), "y", scatter_dimension=0, tiled=True)
+        own = resid_float[c * chunk:(c + 1) * chunk]
+        outs.append((own + combined.astype(jnp.float32)).astype(jnp.bfloat16))
+    return jnp.concatenate(outs, axis=0)[None]
 
 
 def solution(mesh):

time: 256 us -> 220 us (0.86)
  waiting for transfers between devices: 115 us -> 90.8 us
  matrix products: 95.6 us -> 74.2 us
  local copies, waits for them, and re-layouts: 8.95 us -> 15.1 us
  other arithmetic: 7.05 us -> 12.7 us
    all_gather x2, waiting for transfers between devices: 64.1 us -> 33.2 us  [on_device(): lax.all_gather(payload[c * chunk:(c + 1) * chunk], ('y', 'core'), axis=0,...]
    dot_general x12 -> x6, matrix products: 89.2 us -> 67.8 us  [the longest x2 42 us: on_device(): jnp.einsum('enf,efd->end', hidden, w_down, preferred_element_type=jnp.flo...]
    convert_element_type x0 -> x3, other arithmetic: none -> 7.32 us  [the longest x2 5.84 us: on_device(): (mine.astype(jnp.float32) + received.astype(jnp.float32)).astype(jnp.bflo...]
    squeeze x0 -> x2, local copies, waits for them, and re-layouts: none -> 5.09 us  [on_device(): lax.dynamic_index_in_dim(paired, (core + 1) % cores, axis=1, keepdims=False)]
    ppermute x4 -> x2, waiting for transfers between devices: 0.01 us -> 3.87 us  [on_device(): lax.ppermute(theirs, 'core', [(i, (i + 1) % cores) for i in range(cores)])]
    reduce_scatter x2, waiting for transfers between devices: 29.3 us -> 32.2 us  [on_device(): lax.psum_scatter(total.reshape(chips * chunk, D), 'y', scatter_dimension=...]
  transfers between devices with their start and end apart: 10 -> 8, of which waited for: 5 -> 6; matrix products, arithmetic and copies ran while one was open for 31% -> 36% of each run, Pallas kernels for 0% -> 0%
where the time goes in v8:
time: 220 us
  waiting for transfers between devices  90.8 us (41%)
  matrix products  74.2 us (34%)
  local copies, waits for them, and re-layouts  15.1 us (7%)
  starting transfers between devices  13.4 us (6%)
  between operations  13.4 us (6%)
  other arithmetic  12.7 us (6%)
    dot_general x2, matrix products, on_device(): jnp.einsum('enf,efd->end', hidden, w_down, preferred_element_type=jnp.flo...  42 us
    all_gather x2, waiting for transfers between devices, on_device(): lax.all_gather(payload[c * chunk:(c + 1) * chunk], ('y', 'core'), axis=0,...  33.2 us
    reduce_scatter x2, waiting for transfers between devices, on_device(): lax.psum_scatter(total.reshape(chips * chunk, D), 'y', scatter_dimension=...  32.2 us
    dot_general x2, matrix products, on_device(): jnp.einsum('nd,edf->enf', rows, w_up, preferred_element_type=jnp.float32)  23.6 us
    all_to_all x1, waiting for transfers between devices, block_prefix(): lax.all_to_all(pieces, 'seq', split_axis=0, concat_axis=0, tiled=True)  15.8 us
    all_to_all x1, starting transfers between devices, block_prefix(): lax.all_to_all(pieces, 'seq', split_axis=0, concat_axis=0, tiled=True)  8.41 us
    convert_element_type x2, other arithmetic, on_device(): (mine.astype(jnp.float32) + received.astype(jnp.float32)).astype(jnp.bflo...  5.84 us
    squeeze x2, local copies, waits for them, and re-layouts, on_device(): lax.dynamic_index_in_dim(paired, (core + 1) % cores, axis=1, keepdims=False)  5.09 us
  transfers between devices with their start and end apart: 8, of which 6 were waited for; matrix products, arithmetic and copies ran while one was open for 36% of the time, Pallas kernels for 0%

profile of v8, /device:TPU:1, one launch (start us, length us, event | category | flops | bytes accessed | tf_op | source)
XLA Modules:
  0.0 219.7 jit_solution(1507706038520286151)
XLA Ops:
  6.5 1.5 copy.40
  8.0 0.0 copy-start.5
  8.0 0.0 copy-start.6
  8.0 1.5 copy.44
  9.5 1.4 fusion.60
  11.0 8.4 %all-to-all-start = ((f32[16,128,128]{2,1,0:T(8,128)}), f32[16,128,128]{2,1,0:T(8,128)S(1)}, u32[]{:S(2)}, u32[]{:S(2)}) async-start(f32[16,128,128]{2,1,0:T(8,128)} %fusion.60), calls=%async_computation | async-start | bytes 2097152 | tf_op jit(solution)/shard_map/all_to_all | solution.py:18
  19.4 0.0 copy-done.5
  19.4 0.0 copy-done.6
  19.4 0.1 copy.34
  19.5 0.1 copy.35
  19.7 15.8 %all-to-all-done = f32[16,128,128]{2,1,0:T(8,128)S(1)} async-done(((f32[16,128,128]{2,1,0:T(8,128)}), f32[16,128,128]{2,1,0:T(8,128)S(1)}, u32[]{:S(2)}, u32[]{:S(2)}) %all-to-all-start) | async-done | bytes 1048608 | tf_op jit(solution)/shard_map/all_to_all | solution.py:18
  35.4 0.9 reduce-window_convert_fusion
  36.3 4.3 %all-to-all-start.1 = ((bf16[16,128,128]{2,1,0:T(8,128)(2,1)}), bf16[16,128,128]{2,1,0:T(8,128)(2,1)}, u32[]{:S(2)}, u32[]{:S(2)}) async-start(bf16[16,128,128]{2,1,0:T(8,128)(2,1)} %reduce-window_convert_fusion), calls=%async_computation.1 | async-start | bytes 1048576 | tf_op jit(solution)/shard_map/all_to_all | solution.py:21
  40.6 0.0 all-gather.5.cloned.1.call-start
  40.6 0.1 copy.36
  40.8 1.4 copy.43
  42.3 2.7 %fusion.55 = f32[16,256,128]{1,2,0:T(8,128)} fusion(bf16[256,16,128]{0,2,1:T(8,128)(2,1)S(1)} %bitcast.162, pred[256,256]{1,0:T(8,128)(4,1)S(1)} %iota_compare_fusion, bf16[256,16,128]{2,1,0:T(8,128)(2,1)S(1)} %bitcast.164, bf16[256,16,128]{2,1,0:T(8,128)(2,1)S(1)} %bitcast.165), kind=kOutput, calls=%fused_computation.49 | convolution fusion | flops 538968064 | bytes 5308416 | tf_op jit(solution)/shard_map/htu,uhd->thd/dot_general | solution.py:47
  44.9 5.0 %all-to-all-done.1 = bf16[16,128,128]{2,1,0:T(8,128)(2,1)} async-done(((bf16[16,128,128]{2,1,0:T(8,128)(2,1)}), bf16[16,128,128]{2,1,0:T(8,128)(2,1)}, u32[]{:S(2)}, u32[]{:S(2)}) %all-to-all-start.1) | async-done | bytes 524320 | tf_op jit(solution)/shard_map/all_to_all | solution.py:21
  49.9 2.3 %multiply_reduce_fusion.1 = (f32[256,16]{0,1:T(8,128)S(1)}, f32[256,16,128]{0,2,1:T(8,128)S(1)}) fusion(bf16[16,128,128]{2,1,0:T(8,128)(2,1)} %all-to-all-done.1, bf16[256,16,128]{2,1,0:T(8,128)(2,1)S(1)} %bitcast.166, f32[16,256,128]{1,2,0:T(8,128)} %fusion.55), kind=kOutput, calls=%fused_computation.48 | convolution fusion | flops 135786496 | bytes 5783552 | tf_op jit(solution)/shard_map/thd,hed->the/dot_general | solution.py:48
  52.2 0.0 copy-start.2
  52.2 0.0 copy-start.3
  52.3 0.2 broadcast_multiply_fusion
  52.4 0.0 copy-start.4
  52.4 1.8 copy.39
  54.3 0.0 copy-done.2
  54.3 0.0 copy-done.3
  54.3 2.0 multiply_reduce_fusion
  56.3 0.0 copy-done.4
  56.3 1.2 multiply_convert_fusion.2
  57.5 2.4 %concatenate.7 = bf16[256,2176]{1,0:T(8,128)(2,1)S(1)} concatenate(bf16[256,2048]{1,0:T(8,128)(2,1)} %multiply_convert_fusion.2, bf16[256,8]{1,0:T(8,128)(2,1)S(1)} %copy.36, bf16[256,8]{1,0:T(8,128)(2,1)S(1)} %get-tuple-element.12, bf16[256,8]{1,0:T(8,128)(2,1)S(1)} %get-tuple-element.11, bf16[256,104]{1,0:T(8,128)(2,1)S(1)} %broadcast_in_dim.48), dimensions={1} | concatenate | bytes 2228224 | tf_op jit(solution)/shard_map/concatenate | solution.py:78
  59.9 1.1 fusion.85
  61.0 0.0 all-gather.5.cloned.1.call-update
  61.0 0.0 all-gather.3.cloned.1.call-start
  61.0 0.7 all-gather.3.cloned.1.call-update
  61.7 0.0 reduce-scatter.5.cloned.1.call-start
  61.8 33.2 %all-gather.5.cloned.1.call-done = bf16[1024,2176]{1,0:T(8,128)(2,1)} async-done(((bf16[128,2176]{1,0:T(8,128)(2,1)}), bf16[1024,2176]{1,0:T(8,128)(2,1)}) %all-gather.5.cloned.1.call-update) | async-done | bytes 4456464 | tf_op jit(solution)/shard_map/all_gather | solution.py:85
  95.1 1.1 fusion.67
  96.2 11.7 %fusion.9 = f32[1024,1408]{1,0:T(8,128)} fusion(bf16[1,2048,1408]{2,1,0:T(8,128)(2,1)} %param.20, bf16[1024,2176]{1,0:T(8,128)(2,1)} %all-gather.5.cloned.1.call-done), kind=kOutput, calls=%fused_computation.15 | convolution fusion | flops 5905580032 | bytes 15728640 | tf_op jit(solution)/shard_map/nd,edf->enf/dot_general | solution.py:90
  107.9 21.0 %multiply_convert_fusion = bf16[1024,2048]{1,0:T(8,128)(2,1)} fusion(f32[1024]{0:T(1024)S(1)} %bitcast.172, bf16[1,1408,2048]{2,1,0:T(8,128)(2,1)} %param.21, f32[1024,1408]{1,0:T(8,128)} %fusion.9, bf16[1,2048,1408]{2,1,0:T(8,128)(2,1)} %param.19, bf16[1024,2176]{1,0:T(8,128)(2,1)} %all-gather.5.cloned.1.call-done), kind=kOutput, calls=%fused_computation | convolution fusion | flops 11828199424 | bytes 25694208 | tf_op jit(solution)/shard_map/enf,efd->end/dot_general | solution.py:92
  128.9 3.2 %dynamic-slice_bitcast_fusion = bf16[4,128,2048]{2,1,0:T(8,128)(2,1)} fusion(bf16[4,2,128,2048]{3,2,1,0:T(8,128)(2,1)} %bitcast.157, s32[]{:T(128)S(6)} %select_n.42), kind=kLoop, calls=%fused_computation.44 | loop fusion | bytes 4194308 | tf_op jit(solution)/shard_map/jit(dynamic_index_in_dim)/squeeze | solution.py:97
  132.1 0.2 collective-permute-start.1
  132.4 0.0 all-gather.3.cloned.1.call-done
  132.4 1.1 fusion.69
  133.5 0.0 copy-start
  133.5 11.9 %fusion.11 = f32[1024,1408]{1,0:T(8,128)} fusion(bf16[1,2048,1408]{2,1,0:T(8,128)(2,1)} %param.20, bf16[1024,2176]{1,0:T(8,128)(2,1)} %all-gather.3.cloned.1.call-done), kind=kOutput, calls=%fused_computation.17 | convolution fusion | flops 5905580032 | bytes 15728640 | tf_op jit(solution)/shard_map/nd,edf->enf/dot_general | solution.py:90
  145.3 0.0 collective-permute-done.1
  145.4 0.0 copy-done
  145.4 3.7 %fusion.24 = bf16[4,128,2048]{2,1,0:T(8,128)(2,1)} fusion(bf16[4,128,2048]{2,1,0:T(8,128)(2,1)} %collective-permute-done.1, bf16[4,2,128,2048]{3,2,1,0:T(8,128)(2,1)S(1)} %bitcast.158, s32[]{:T(128)S(6)} %select_n.40), kind=kLoop, calls=%fused_computation.29 | loop fusion | flops 4194304 | bytes 6291460 | tf_op jit(solution)/shard_map/convert_element_type | solution.py:99
  149.1 0.0 reduce-scatter.5.cloned.1.call-update
  149.1 0.0 reduce-scatter.3.cloned.1.call-start
  149.2 21.0 %multiply_convert_fusion.1 = bf16[1024,2048]{1,0:T(8,128)(2,1)} fusion(f32[1024]{0:T(1024)S(1)} %bitcast.171, bf16[1,1408,2048]{2,1,0:T(8,128)(2,1)} %param.21, f32[1024,1408]{1,0:T(8,128)} %fusion.11, bf16[1,2048,1408]{2,1,0:T(8,128)(2,1)} %param.19, bf16[1024,2176]{1,0:T(8,128)(2,1)} %all-gather.3.cloned.1.call-done), kind=kOutput, calls=%fused_computation.1 | convolution fusion | flops 11828199424 | bytes 25694208 | tf_op jit(solution)/shard_map/enf,efd->end/dot_general | solution.py:92
  170.1 0.0 copy-start.1
  170.1 1.9 dynamic-slice_bitcast_fusion.1
  172.0 0.4 collective-permute-start
  172.4 3.9 %collective-permute-done = bf16[4,128,2048]{2,1,0:T(8,128)(2,1)S(1)} collective-permute-done((bf16[4,128,2048]{2,1,0:T(8,128)(2,1)S(1)}, bf16[4,128,2048]{2,1,0:T(8,128)(2,1)S(1)}, u32[]{:S(2)}, u32[]{:S(2)}) %collective-permute-start) | collective-permute-done | bytes 2097184 | tf_op jit(solution)/shard_map/ppermute | solution.py:98
  176.3 0.0 copy-done.1
  176.3 2.1 fusion.25
  178.4 0.0 reduce-scatter.3.cloned.1.call-update
  178.4 0.5 reduce-scatter.5.cloned.1.call-done
  178.9 31.7 %reduce-scatter.3.cloned.1.call-done = bf16[128,2048]{1,0:T(8,128)(2,1)} async-done(((bf16[512,2048]{1,0:T(8,128)(2,1)}), bf16[128,2048]{1,0:T(8,128)(2,1)}) %reduce-scatter.3.cloned.1.call-update) | async-done | bytes 524304 | tf_op jit(solution)/shard_map/reduce_scatter | solution.py:100
  210.6 1.5 fusion.58
  212.1 1.0 maximum_bitcast_fusion
  (7 shorter events, 0.1 us)
Async XLA Ops:
  8.0 11.4 %copy-start.5 = (f32[1,256,4]{1,2,0:T(4,128)S(1)}, f32[1,256,4]{1,2,0:T(4,128)}, u32[]{:S(2)}) copy-start(f32[1,256,4]{1,2,0:T(4,128)} %param.18) | copy-start | bytes 12292
  8.0 11.4 %copy-start.6 = (s32[1,256,4]{1,2,0:T(4,128)S(1)}, s32[1,256,4]{1,2,0:T(4,128)}, u32[]{:S(2)}) copy-start(s32[1,256,4]{1,2,0:T(4,128)} %param.17) | copy-start | bytes 12292
  11.0 24.5 %all-to-all-start = ((f32[16,128,128]{2,1,0:T(8,128)}), f32[16,128,128]{2,1,0:T(8,128)S(1)}, u32[]{:S(2)}, u32[]{:S(2)}) async-start(f32[16,128,128]{2,1,0:T(8,128)} %fusion.60), calls=%async_computation | async-start | bytes 2097152 | tf_op jit(solution)/shard_map/all_to_all | solution.py:18
  36.3 13.6 %all-to-all-start.1 = ((bf16[16,128,128]{2,1,0:T(8,128)(2,1)}), bf16[16,128,128]{2,1,0:T(8,128)(2,1)}, u32[]{:S(2)}, u32[]{:S(2)}) async-start(bf16[16,128,128]{2,1,0:T(8,128)(2,1)} %reduce-window_convert_fusion), calls=%async_computation.1 | async-start | bytes 1048576 | tf_op jit(solution)/shard_map/all_to_all | solution.py:21
  40.6 54.5 %all-gather.5.cloned.1.call-start = ((), (), s32[]{:S(2)}) async-start(), calls=%async_computation.6 | async-start | bytes 5013504 | tf_op jit(solution)/shard_map/all_gather | solution.py:85
  52.2 2.0 copy-start.2
  52.2 2.0 copy-start.3
  52.4 3.9 %copy-start.4 = (f32[2048]{0:T(1024)S(1)}, f32[2048]{0:T(1024)}, u32[]{:S(2)}) copy-start(f32[2048]{0:T(1024)} %param.16) | copy-start | bytes 24580
  61.0 71.4 %all-gather.3.cloned.1.call-start = ((), (), s32[]{:S(2)}) async-start(), calls=%async_computation.4 | async-start | bytes 5013504 | tf_op jit(solution)/shard_map/all_gather | solution.py:85
  61.7 117.1 %reduce-scatter.5.cloned.1.call-start = ((), (), s32[]{:S(2)}) async-start(), calls=%async_computation.7 | async-start | bytes 2621440 | tf_op jit(solution)/shard_map/reduce_scatter | solution.py:100
  132.1 13.2 %collective-permute-start.1 = (bf16[4,128,2048]{2,1,0:T(8,128)(2,1)}, bf16[4,128,2048]{2,1,0:T(8,128)(2,1)}, u32[]{:S(2)}, u32[]{:S(2)}) collective-permute-start(bf16[4,128,2048]{2,1,0:T(8,128)(2,1)} %dynamic-slice_bitcast_fusion), channel_id=1, source_target_pairs={{0,1},{1,0},{2,3},{3,2},{4,5},{5,4},{6,7},{7,6},{8,9},{9,8},{10,11... | collective-permute-start | bytes 6291464 | tf_op jit(solution)/shard_map/ppermute | solution.py:98
  133.5 11.9 %copy-start = (bf16[1024,2048]{1,0:T(8,128)(2,1)S(1)}, bf16[1024,2048]{1,0:T(8,128)(2,1)}, u32[]{:S(2)}) copy-start(bf16[1024,2048]{1,0:T(8,128)(2,1)} %multiply_convert_fusion) | copy-start | bytes 12582916
  149.1 61.5 %reduce-scatter.3.cloned.1.call-start = ((), (), s32[]{:S(2)}) async-start(), calls=%async_computation.5 | async-start | bytes 2621440 | tf_op jit(solution)/shard_map/reduce_scatter | solution.py:100
  170.1 6.1 %copy-start.1 = (bf16[1024,2048]{1,0:T(8,128)(2,1)S(1)}, bf16[1024,2048]{1,0:T(8,128)(2,1)}, u32[]{:S(2)}) copy-start(bf16[1024,2048]{1,0:T(8,128)(2,1)} %multiply_convert_fusion.1) | copy-start | bytes 12582916
  172.0 4.2 %collective-permute-start = (bf16[4,128,2048]{2,1,0:T(8,128)(2,1)S(1)}, bf16[4,128,2048]{2,1,0:T(8,128)(2,1)S(1)}, u32[]{:S(2)}, u32[]{:S(2)}) collective-permute-start(bf16[4,128,2048]{2,1,0:T(8,128)(2,1)S(1)} %dynamic-slice_bitcast_fusion.1), channel_id=1, source_target_pairs={{0,1},{1,0},{2,3},{3,2},{4,5},{5,4},{6,7},{7,6},{8,9},{9,8},{10,11... | collective-permute-start | bytes 6291464 | tf_op jit(solution)/shard_map/ppermute | solution.py:98
Sparse Core Ops, SparseCore 0:
  61.1 33.8 all-gather.4
  96.7 33.1 all-gather.2
  149.2 29.5 reduce-scatter.4
  181.1 29.4 reduce-scatter.2

commit v9 on v8

--- a/solution.py
+++ b/solution.py
@@ -81,8 +81,18 @@
     select = (columns[:, None] == me * local_count + jnp.arange(local_count)[None, :]).astype(jnp.bfloat16)
     chunk = positions // CHUNKS
     outs = []
+    pending = None
+
+    def scatter(c, total):
+        combined = lax.psum_scatter(total.reshape(chips * chunk, D), "y", scatter_dimension=0, tiled=True)
+        own = resid_float[c * chunk:(c + 1) * chunk]
+        outs.append((own + combined.astype(jnp.float32)).astype(jnp.bfloat16))
+
     for c in range(CHUNKS):
         gathered = lax.all_gather(payload[c * chunk:(c + 1) * chunk], ("y", "core"), axis=0, tiled=True)
+        if pending is not None:
+            gathered, pending = lax.optimization_barrier((gathered, pending))
+            scatter(c - 1, pending)
         rows = gathered[:, :D]
         code = gathered[:, D:D + 3 * EXPERTS]
         weight = jnp.dot(code, select, preferred_element_type=jnp.float32)
@@ -96,10 +106,8 @@
         mine = lax.dynamic_index_in_dim(paired, core, axis=1, keepdims=False)
         theirs = lax.dynamic_index_in_dim(paired, (core + 1) % cores, axis=1, keepdims=False)
         received = lax.ppermute(theirs, "core", [(i, (i + 1) % cores) for i in range(cores)])
-        total = (mine.astype(jnp.float32) + received.astype(jnp.float32)).astype(jnp.bfloat16)
-        combined = lax.psum_scatter(total.reshape(chips * chunk, D), "y", scatter_dimension=0, tiled=True)
-        own = resid_float[c * chunk:(c + 1) * chunk]
-        outs.append((own + combined.astype(jnp.float32)).astype(jnp.bfloat16))
+        pending = (mine.astype(jnp.float32) + received.astype(jnp.float32)).astype(jnp.bfloat16)
+    scatter(CHUNKS - 1, pending)
     return jnp.concatenate(outs, axis=0)[None]
 
 

time: 220 us -> 225 us (1.023)
  waiting for transfers between devices: 90.8 us -> 95.1 us
    ppermute x2, waiting for transfers between devices: 3.87 us -> 8.19 us  [on_device(): lax.ppermute(theirs, 'core', [(i, (i + 1) % cores) for i in range(cores)])]
  transfers between devices with their start and end apart: 8 -> 8, of which waited for: 6 -> 7; matrix products, arithmetic and copies ran while one was open for 36% -> 32% of each run, Pallas kernels for 0% -> 0%
where the time goes in v9:
time: 225 us; the launch traced here: 224 us
  waiting for transfers between devices  95.1 us (42%)
  matrix products  74 us (33%)
  local copies, waits for them, and re-layouts  15.1 us (7%)
  starting transfers between devices  13.4 us (6%)
  other arithmetic  13.4 us (6%)
  between operations  13.4 us (6%)
    dot_general x2, matrix products, on_device(): jnp.einsum('enf,efd->end', hidden, w_down, preferred_element_type=jnp.flo...  42 us
    all_gather x2, waiting for transfers between devices, on_device(): lax.all_gather(payload[c * chunk:(c + 1) * chunk], ('y', 'core'), axis=0,...  33.2 us
    reduce_scatter x2, waiting for transfers between devices, scatter(): lax.psum_scatter(total.reshape(chips * chunk, D), 'y', scatter_dimension=...  32.1 us
    dot_general x2, matrix products, on_device(): jnp.einsum('nd,edf->enf', rows, w_up, preferred_element_type=jnp.float32)  23.4 us
    all_to_all x1, waiting for transfers between devices, block_prefix(): lax.all_to_all(pieces, 'seq', split_axis=0, concat_axis=0, tiled=True)  15.8 us
    all_to_all x1, starting transfers between devices, block_prefix(): lax.all_to_all(pieces, 'seq', split_axis=0, concat_axis=0, tiled=True)  8.41 us
    ppermute x2, waiting for transfers between devices, on_device(): lax.ppermute(theirs, 'core', [(i, (i + 1) % cores) for i in range(cores)])  8.19 us
    convert_element_type x2, other arithmetic, on_device(): (mine.astype(jnp.float32) + received.astype(jnp.float32)).astype(jnp.bflo...  6.56 us
  transfers between devices with their start and end apart: 8, of which 7 were waited for; matrix products, arithmetic and copies ran while one was open for 32% of the time, Pallas kernels for 0%

profile of v9, /device:TPU:1, one launch (start us, length us, event | category | flops | bytes accessed | tf_op | source)
XLA Modules:
  0.0 224.4 jit_solution(11251492149349068104)
XLA Ops:
  6.5 1.5 copy.40
  8.0 0.0 copy-start.4
  8.0 0.0 copy-start.5
  8.0 1.5 copy.44
  9.5 1.4 fusion.60
  11.0 8.4 %all-to-all-start = ((f32[16,128,128]{2,1,0:T(8,128)}), f32[16,128,128]{2,1,0:T(8,128)S(1)}, u32[]{:S(2)}, u32[]{:S(2)}) async-start(f32[16,128,128]{2,1,0:T(8,128)} %fusion.60), calls=%async_computation | async-start | bytes 2097152 | tf_op jit(solution)/shard_map/all_to_all | solution.py:18
  19.4 0.0 copy-done.4
  19.4 0.0 copy-done.5
  19.4 0.1 copy.34
  19.5 0.1 copy.35
  19.7 15.8 %all-to-all-done = f32[16,128,128]{2,1,0:T(8,128)S(1)} async-done(((f32[16,128,128]{2,1,0:T(8,128)}), f32[16,128,128]{2,1,0:T(8,128)S(1)}, u32[]{:S(2)}, u32[]{:S(2)}) %all-to-all-start) | async-done | bytes 1048608 | tf_op jit(solution)/shard_map/all_to_all | solution.py:18
  35.4 0.9 reduce-window_convert_fusion
  36.3 4.3 %all-to-all-start.1 = ((bf16[16,128,128]{2,1,0:T(8,128)(2,1)}), bf16[16,128,128]{2,1,0:T(8,128)(2,1)}, u32[]{:S(2)}, u32[]{:S(2)}) async-start(bf16[16,128,128]{2,1,0:T(8,128)(2,1)} %reduce-window_convert_fusion), calls=%async_computation.1 | async-start | bytes 1048576 | tf_op jit(solution)/shard_map/all_to_all | solution.py:21
  40.6 0.0 all-gather.5.cloned.1.call-start
  40.6 0.1 copy.36
  40.8 1.4 copy.43
  42.2 2.7 %fusion.55 = f32[16,256,128]{1,2,0:T(8,128)} fusion(bf16[256,16,128]{0,2,1:T(8,128)(2,1)S(1)} %bitcast.162, pred[256,256]{1,0:T(8,128)(4,1)S(1)} %iota_compare_fusion, bf16[256,16,128]{2,1,0:T(8,128)(2,1)S(1)} %bitcast.164, bf16[256,16,128]{2,1,0:T(8,128)(2,1)S(1)} %bitcast.165), kind=kOutput, calls=%fused_computation.49 | convolution fusion | flops 538968064 | bytes 5308416 | tf_op jit(solution)/shard_map/htu,uhd->thd/dot_general | solution.py:47
  44.9 5.0 %all-to-all-done.1 = bf16[16,128,128]{2,1,0:T(8,128)(2,1)} async-done(((bf16[16,128,128]{2,1,0:T(8,128)(2,1)}), bf16[16,128,128]{2,1,0:T(8,128)(2,1)}, u32[]{:S(2)}, u32[]{:S(2)}) %all-to-all-start.1) | async-done | bytes 524320 | tf_op jit(solution)/shard_map/all_to_all | solution.py:21
  49.9 2.3 %multiply_reduce_fusion.1 = (f32[256,16]{0,1:T(8,128)S(1)}, f32[256,16,128]{0,2,1:T(8,128)S(1)}) fusion(bf16[16,128,128]{2,1,0:T(8,128)(2,1)} %all-to-all-done.1, bf16[256,16,128]{2,1,0:T(8,128)(2,1)S(1)} %bitcast.166, f32[16,256,128]{1,2,0:T(8,128)} %fusion.55), kind=kOutput, calls=%fused_computation.48 | convolution fusion | flops 135786496 | bytes 5783552 | tf_op jit(solution)/shard_map/thd,hed->the/dot_general | solution.py:48
  52.2 0.0 copy-start.1
  52.2 0.0 copy-start.2
  52.3 0.2 broadcast_multiply_fusion
  52.4 0.0 copy-start.3
  52.4 1.8 copy.39
  54.3 0.0 copy-done.1
  54.3 0.0 copy-done.2
  54.3 2.0 multiply_reduce_fusion
  56.3 0.0 copy-done.3
  56.3 1.2 multiply_convert_fusion.2
  57.5 2.4 %concatenate.7 = bf16[256,2176]{1,0:T(8,128)(2,1)S(1)} concatenate(bf16[256,2048]{1,0:T(8,128)(2,1)} %multiply_convert_fusion.2, bf16[256,8]{1,0:T(8,128)(2,1)S(1)} %copy.36, bf16[256,8]{1,0:T(8,128)(2,1)S(1)} %get-tuple-element.16, bf16[256,8]{1,0:T(8,128)(2,1)S(1)} %get-tuple-element.15, bf16[256,104]{1,0:T(8,128)(2,1)S(1)} %broadcast_in_dim.48), dimensions={1} | concatenate | bytes 2228224 | tf_op jit(solution)/shard_map/concatenate | solution.py:78
  59.9 1.1 fusion.85
  61.0 0.0 all-gather.5.cloned.1.call-update
  61.0 0.0 all-gather.3.cloned.1.call-start
  61.1 0.7 all-gather.3.cloned.1.call-update
  61.7 0.0 reduce-scatter.3.cloned.1.call-start
  61.8 33.2 %all-gather.5.cloned.1.call-done = bf16[1024,2176]{1,0:T(8,128)(2,1)} async-done(((bf16[128,2176]{1,0:T(8,128)(2,1)}), bf16[1024,2176]{1,0:T(8,128)(2,1)}) %all-gather.5.cloned.1.call-update) | async-done | bytes 4456464 | tf_op jit(solution)/shard_map/all_gather | solution.py:92
  95.0 1.1 fusion.67
  96.1 11.7 %fusion.11 = f32[1024,1408]{1,0:T(8,128)} fusion(bf16[1,2048,1408]{2,1,0:T(8,128)(2,1)} %param.20, bf16[1024,2176]{1,0:T(8,128)(2,1)} %all-gather.5.cloned.1.call-done), kind=kOutput, calls=%fused_computation.17 | convolution fusion | flops 5905580032 | bytes 15728640 | tf_op jit(solution)/shard_map/nd,edf->enf/dot_general | solution.py:100
  107.9 21.0 %multiply_convert_fusion.1 = bf16[1024,2048]{1,0:T(8,128)(2,1)} fusion(f32[1024]{0:T(1024)S(1)} %bitcast.172, bf16[1,1408,2048]{2,1,0:T(8,128)(2,1)} %param.21, f32[1024,1408]{1,0:T(8,128)} %fusion.11, bf16[1,2048,1408]{2,1,0:T(8,128)(2,1)} %param.19, bf16[1024,2176]{1,0:T(8,128)(2,1)} %all-gather.5.cloned.1.call-done), kind=kOutput, calls=%fused_computation.1 | convolution fusion | flops 11828199424 | bytes 25694208 | tf_op jit(solution)/shard_map/enf,efd->end/dot_general | solution.py:102
  128.9 3.2 %dynamic-slice_bitcast_fusion.1 = bf16[4,128,2048]{2,1,0:T(8,128)(2,1)} fusion(bf16[4,2,128,2048]{3,2,1,0:T(8,128)(2,1)} %bitcast.157, s32[]{:T(128)S(6)} %select_n.42), kind=kLoop, calls=%fused_computation.45 | loop fusion | bytes 4194308 | tf_op jit(solution)/shard_map/jit(dynamic_index_in_dim)/squeeze | solution.py:107
  132.1 0.2 collective-permute-start
  132.3 4.3 %collective-permute-done = bf16[4,128,2048]{2,1,0:T(8,128)(2,1)} collective-permute-done((bf16[4,128,2048]{2,1,0:T(8,128)(2,1)}, bf16[4,128,2048]{2,1,0:T(8,128)(2,1)}, u32[]{:S(2)}, u32[]{:S(2)}) %collective-permute-start) | collective-permute-done | bytes 2097184 | tf_op jit(solution)/shard_map/ppermute | solution.py:108
  136.6 4.4 %fusion.25 = bf16[4,128,2048]{2,1,0:T(8,128)(2,1)} fusion(bf16[4,128,2048]{2,1,0:T(8,128)(2,1)} %collective-permute-done, bf16[4,2,128,2048]{3,2,1,0:T(8,128)(2,1)} %bitcast.158, s32[]{:T(128)S(6)} %select_n.40), kind=kLoop, calls=%fused_computation.31 | loop fusion | flops 4194304 | bytes 6291460 | tf_op jit(solution)/shard_map/convert_element_type | solution.py:109
  141.0 0.0 all-gather.3.cloned.1.call-done
  141.0 11.7 %fusion.9 = f32[1024,1408]{1,0:T(8,128)} fusion(bf16[1,2048,1408]{2,1,0:T(8,128)(2,1)} %param.20, bf16[1024,2176]{1,0:T(8,128)(2,1)} %all-gather.3.cloned.1.call-done), kind=kOutput, calls=%fused_computation.15 | convolution fusion | flops 5905580032 | bytes 15728640 | tf_op jit(solution)/shard_map/nd,edf->enf/dot_general | solution.py:100
  152.7 1.1 fusion.69
  153.8 0.0 reduce-scatter.3.cloned.1.call-update
  153.9 0.0 reduce-scatter.5.cloned.1.call-start
  154.0 21.0 %multiply_convert_fusion = bf16[1024,2048]{1,0:T(8,128)(2,1)} fusion(f32[1024]{0:T(1024)S(1)} %bitcast.171, bf16[1,1408,2048]{2,1,0:T(8,128)(2,1)} %param.21, f32[1024,1408]{1,0:T(8,128)} %fusion.9, bf16[1,2048,1408]{2,1,0:T(8,128)(2,1)} %param.19, bf16[1024,2176]{1,0:T(8,128)(2,1)} %all-gather.3.cloned.1.call-done), kind=kOutput, calls=%fused_computation | convolution fusion | flops 11828199424 | bytes 25694208 | tf_op jit(solution)/shard_map/enf,efd->end/dot_general | solution.py:102
  174.9 0.0 copy-start
  174.9 1.9 dynamic-slice_bitcast_fusion
  176.8 0.3 collective-permute-start.1
  177.2 3.9 %collective-permute-done.1 = bf16[4,128,2048]{2,1,0:T(8,128)(2,1)S(1)} collective-permute-done((bf16[4,128,2048]{2,1,0:T(8,128)(2,1)S(1)}, bf16[4,128,2048]{2,1,0:T(8,128)(2,1)S(1)}, u32[]{:S(2)}, u32[]{:S(2)}) %collective-permute-start.1) | collective-permute-done | bytes 2097184 | tf_op jit(solution)/shard_map/ppermute | solution.py:108
  181.1 0.0 copy-done
  181.1 2.1 fusion.24
  183.2 0.0 reduce-scatter.5.cloned.1.call-update
  183.2 0.4 reduce-scatter.3.cloned.1.call-done
  183.6 31.7 %reduce-scatter.5.cloned.1.call-done = bf16[128,2048]{1,0:T(8,128)(2,1)} async-done(((bf16[512,2048]{1,0:T(8,128)(2,1)}), bf16[128,2048]{1,0:T(8,128)(2,1)}) %reduce-scatter.5.cloned.1.call-update) | async-done | bytes 524304 | tf_op jit(solution)/shard_map/reduce_scatter | solution.py:87
  215.4 1.5 fusion.58
  216.9 1.0 maximum_bitcast_fusion
  (7 shorter events, 0.1 us)
Async XLA Ops:
  8.0 11.4 %copy-start.4 = (f32[1,256,4]{1,2,0:T(4,128)S(1)}, f32[1,256,4]{1,2,0:T(4,128)}, u32[]{:S(2)}) copy-start(f32[1,256,4]{1,2,0:T(4,128)} %param.18) | copy-start | bytes 12292
  8.0 11.4 %copy-start.5 = (s32[1,256,4]{1,2,0:T(4,128)S(1)}, s32[1,256,4]{1,2,0:T(4,128)}, u32[]{:S(2)}) copy-start(s32[1,256,4]{1,2,0:T(4,128)} %param.17) | copy-start | bytes 12292
  11.0 24.5 %all-to-all-start = ((f32[16,128,128]{2,1,0:T(8,128)}), f32[16,128,128]{2,1,0:T(8,128)S(1)}, u32[]{:S(2)}, u32[]{:S(2)}) async-start(f32[16,128,128]{2,1,0:T(8,128)} %fusion.60), calls=%async_computation | async-start | bytes 2097152 | tf_op jit(solution)/shard_map/all_to_all | solution.py:18
  36.3 13.6 %all-to-all-start.1 = ((bf16[16,128,128]{2,1,0:T(8,128)(2,1)}), bf16[16,128,128]{2,1,0:T(8,128)(2,1)}, u32[]{:S(2)}, u32[]{:S(2)}) async-start(bf16[16,128,128]{2,1,0:T(8,128)(2,1)} %reduce-window_convert_fusion), calls=%async_computation.1 | async-start | bytes 1048576 | tf_op jit(solution)/shard_map/all_to_all | solution.py:21
  40.6 54.5 %all-gather.5.cloned.1.call-start = ((), (), s32[]{:S(2)}) async-start(), calls=%async_computation.5 | async-start | bytes 5013504 | tf_op jit(solution)/shard_map/all_gather | solution.py:92
  52.2 2.0 copy-start.1
  52.2 2.0 copy-start.2
  52.4 3.9 %copy-start.3 = (f32[2048]{0:T(1024)S(1)}, f32[2048]{0:T(1024)}, u32[]{:S(2)}) copy-start(f32[2048]{0:T(1024)} %param.16) | copy-start | bytes 24580
  61.0 80.0 %all-gather.3.cloned.1.call-start = ((), (), s32[]{:S(2)}) async-start(), calls=%async_computation.4 | async-start | bytes 5013504 | tf_op jit(solution)/shard_map/all_gather | solution.py:92
  61.7 121.9 %reduce-scatter.3.cloned.1.call-start = ((), (), s32[]{:S(2)}) async-start(), calls=%async_computation.6 | async-start | bytes 2621440 | tf_op jit(solution)/shard_map/reduce_scatter | solution.py:87
  132.1 4.5 %collective-permute-start = (bf16[4,128,2048]{2,1,0:T(8,128)(2,1)}, bf16[4,128,2048]{2,1,0:T(8,128)(2,1)}, u32[]{:S(2)}, u32[]{:S(2)}) collective-permute-start(bf16[4,128,2048]{2,1,0:T(8,128)(2,1)} %dynamic-slice_bitcast_fusion.1), channel_id=1, source_target_pairs={{0,1},{1,0},{2,3},{3,2},{4,5},{5,4},{6,7},{7,6},{8,9},{9,8},{10,11... | collective-permute-start | bytes 6291464 | tf_op jit(solution)/shard_map/ppermute | solution.py:108
  153.9 61.5 %reduce-scatter.5.cloned.1.call-start = ((), (), s32[]{:S(2)}) async-start(), calls=%async_computation.7 | async-start | bytes 2621440 | tf_op jit(solution)/shard_map/reduce_scatter | solution.py:87
  174.9 6.1 %copy-start = (bf16[1024,2048]{1,0:T(8,128)(2,1)S(1)}, bf16[1024,2048]{1,0:T(8,128)(2,1)}, u32[]{:S(2)}) copy-start(bf16[1024,2048]{1,0:T(8,128)(2,1)} %multiply_convert_fusion) | copy-start | bytes 12582916
  176.8 4.2 %collective-permute-start.1 = (bf16[4,128,2048]{2,1,0:T(8,128)(2,1)S(1)}, bf16[4,128,2048]{2,1,0:T(8,128)(2,1)S(1)}, u32[]{:S(2)}, u32[]{:S(2)}) collective-permute-start(bf16[4,128,2048]{2,1,0:T(8,128)(2,1)S(1)} %dynamic-slice_bitcast_fusion), channel_id=1, source_target_pairs={{0,1},{1,0},{2,3},{3,2},{4,5},{5,4},{6,7},{7,6},{8,9},{9,8},{10,11... | collective-permute-start | bytes 6291464 | tf_op jit(solution)/shard_map/ppermute | solution.py:108
Sparse Core Ops, SparseCore 0:
  61.1 33.8 all-gather.4
  96.7 33.1 all-gather.2
  154.0 29.5 reduce-scatter.2
  185.9 29.4 reduce-scatter.4

commit v10 on v5

--- a/solution.py
+++ b/solution.py
@@ -65,23 +65,31 @@
         jnp.where(route_ids[:, :, None] == experts[None, None, :], route_gates[:, :, None], 0.0),
         axis=1,
     )
+    groups = lax.axis_size("exp")
     me = lax.axis_index("exp")
     local_count = w_gate.shape[0]
     high = table.astype(jnp.bfloat16)
     rest = table - high.astype(jnp.float32)
     middle = rest.astype(jnp.bfloat16)
     low = (rest - middle.astype(jnp.float32)).astype(jnp.bfloat16)
-    pad = jnp.zeros((positions, 128 - 3 * EXPERTS), jnp.bfloat16)
-    payload = jnp.concatenate([normed, high, middle, low, pad], axis=1)
+    codes = jnp.concatenate([high, middle, low], axis=1)
+    width = 3 * EXPERTS * CHUNKS
+    packed = codes.reshape(positions // CHUNKS, width)
+    pad = jnp.zeros((positions // CHUNKS, 128 - width), jnp.bfloat16)
 
     columns = jnp.arange(3 * EXPERTS, dtype=jnp.int32) % EXPERTS
     select = (columns[:, None] == me * local_count + jnp.arange(local_count)[None, :]).astype(jnp.bfloat16)
     chunk = positions // CHUNKS
     outs = []
     for c in range(CHUNKS):
-        gathered = lax.all_gather(payload[c * chunk:(c + 1) * chunk], "exp", axis=0, tiled=True)
+        part = normed[c * chunk:(c + 1) * chunk]
+        if c == 0:
+            part = jnp.concatenate([part, packed, pad], axis=1)
+        gathered = lax.all_gather(part, "exp", axis=0, tiled=True)
+        if c == 0:
+            all_codes = gathered[:, D:D + width].reshape(groups, positions, 3 * EXPERTS)
         rows = gathered[:, :D]
-        code = gathered[:, D:D + 3 * EXPERTS]
+        code = all_codes[:, c * chunk:(c + 1) * chunk].reshape(groups * chunk, 3 * EXPERTS)
         weight = jnp.dot(code, select, preferred_element_type=jnp.float32)
         gate_part = jnp.einsum("nd,edf->enf", rows, w_gate, preferred_element_type=jnp.float32)
         up_part = jnp.einsum("nd,edf->enf", rows, w_up, preferred_element_type=jnp.float32)
@@ -89,9 +97,10 @@
         result = jnp.einsum("enf,efd->end", hidden, w_down, preferred_element_type=jnp.float32)
         result = result.astype(jnp.bfloat16).astype(jnp.float32)
         contrib = jnp.sum(result * weight.T[:, :, None], axis=0).astype(jnp.bfloat16)
-        outs.append(lax.psum_scatter(contrib, "exp", scatter_dimension=0, tiled=True))
-    combined = jnp.concatenate(outs, axis=0)
-    return (resid_float + combined.astype(jnp.float32)).astype(jnp.bfloat16)[None]
+        combined = lax.psum_scatter(contrib, "exp", scatter_dimension=0, tiled=True)
+        own = resid_float[c * chunk:(c + 1) * chunk]
+        outs.append((own + combined.astype(jnp.float32)).astype(jnp.bfloat16))
+    return jnp.concatenate(outs, axis=0)[None]
 
 
 def solution(mesh):

time: 217 us -> 214 us (0.986)
  transfers between devices with their start and end apart: 6 -> 6, of which waited for: 6 -> 5; matrix products, arithmetic and copies ran while one was open for 34% -> 34% of each run, Pallas kernels for 0% -> 0%
where the time goes in v10:
time: 214 us; the launch traced here: 211 us
  waiting for transfers between devices  97 us (45%)
  matrix products  72.6 us (34%)
  between operations  13.3 us (6%)
  starting transfers between devices  13 us (6%)
  local copies, waits for them, and re-layouts  9.6 us (4%)
  other arithmetic  5.87 us (3%)
    dot_general x2, matrix products, on_device(): jnp.einsum('enf,efd->end', hidden, w_down, preferred_element_type=jnp.flo...  42.4 us
    reduce_scatter x2, waiting for transfers between devices, on_device(): combined = lax.psum_scatter(contrib, 'exp', scatter_dimension=0, tiled=True)  42.1 us
    all_gather x2, waiting for transfers between devices, on_device(): gathered = lax.all_gather(part, 'exp', axis=0, tiled=True)  33.3 us
    dot_general x2, matrix products, on_device(): jnp.einsum('nd,edf->enf', rows, w_up, preferred_element_type=jnp.float32)  23.5 us
    all_to_all x1, waiting for transfers between devices, block_prefix(): lax.all_to_all(pieces, 'seq', split_axis=0, concat_axis=0, tiled=True)  16 us
    all_to_all x1, starting transfers between devices, block_prefix(): lax.all_to_all(pieces, 'seq', split_axis=0, concat_axis=0, tiled=True)  8.42 us
    all_to_all x1, waiting for transfers between devices, block_prefix(): lax.all_to_all(prefixes, 'seq', split_axis=0, concat_axis=0, tiled=True)  4.9 us
  transfers between devices with their start and end apart: 6, of which 5 were waited for; matrix products, arithmetic and copies ran while one was open for 34% of the time, Pallas kernels for 0%

profile of v10, /device:TPU:1, one launch (start us, length us, event | category | flops | bytes accessed | tf_op | source)
XLA Modules:
  0.0 211.4 jit_solution(10982386271514050562)
XLA Ops:
  6.5 0.0 copy-start.3
  6.5 0.0 copy-start.4
  6.5 1.5 copy.41
  8.0 1.5 copy.43
  9.5 1.4 fusion.52
  10.9 8.4 %all-to-all-start = ((f32[16,128,128]{2,1,0:T(8,128)}), f32[16,128,128]{2,1,0:T(8,128)S(1)}, u32[]{:S(2)}, u32[]{:S(2)}) async-start(f32[16,128,128]{2,1,0:T(8,128)} %fusion.52), calls=%async_computation | async-start | bytes 2097152 | tf_op jit(solution)/shard_map/all_to_all | solution.py:18
  19.4 0.0 copy-done.3
  19.4 0.0 copy-done.4
  19.4 16.0 %all-to-all-done = f32[16,128,128]{2,1,0:T(8,128)S(1)} async-done(((f32[16,128,128]{2,1,0:T(8,128)}), f32[16,128,128]{2,1,0:T(8,128)S(1)}, u32[]{:S(2)}, u32[]{:S(2)}) %all-to-all-start) | async-done | bytes 1048608 | tf_op jit(solution)/shard_map/all_to_all | solution.py:18
  35.4 0.9 reduce-window_convert_fusion
  36.3 4.3 %all-to-all-start.1 = ((bf16[16,128,128]{2,1,0:T(8,128)(2,1)}), bf16[16,128,128]{2,1,0:T(8,128)(2,1)}, u32[]{:S(2)}, u32[]{:S(2)}) async-start(bf16[16,128,128]{2,1,0:T(8,128)(2,1)} %reduce-window_convert_fusion), calls=%async_computation.1 | async-start | bytes 1048576 | tf_op jit(solution)/shard_map/all_to_all | solution.py:21
  40.6 0.0 all-gather.3.cloned.1.call-start
  40.6 1.5 copy.42
  42.1 0.1 copy.39
  42.2 0.1 reshape.96
  42.3 2.7 %fusion.47 = f32[16,256,128]{1,2,0:T(8,128)} fusion(bf16[256,16,128]{0,2,1:T(8,128)(2,1)S(1)} %bitcast.144, pred[256,256]{1,0:T(8,128)(4,1)S(1)} %iota_compare_fusion, bf16[256,16,128]{2,1,0:T(8,128)(2,1)S(1)} %bitcast.146, bf16[256,16,128]{2,1,0:T(8,128)(2,1)S(1)} %bitcast.147), kind=kOutput, calls=%fused_computation.41 | convolution fusion | flops 538968064 | bytes 5308416 | tf_op jit(solution)/shard_map/htu,uhd->thd/dot_general | solution.py:47
  45.0 4.9 %all-to-all-done.1 = bf16[16,128,128]{2,1,0:T(8,128)(2,1)} async-done(((bf16[16,128,128]{2,1,0:T(8,128)(2,1)}), bf16[16,128,128]{2,1,0:T(8,128)(2,1)}, u32[]{:S(2)}, u32[]{:S(2)}) %all-to-all-start.1) | async-done | bytes 524320 | tf_op jit(solution)/shard_map/all_to_all | solution.py:21
  49.9 2.3 %multiply_reduce_fusion.1 = (f32[256,16]{0,1:T(8,128)S(1)}, f32[256,16,128]{0,2,1:T(8,128)S(1)}) fusion(bf16[16,128,128]{2,1,0:T(8,128)(2,1)} %all-to-all-done.1, bf16[256,16,128]{2,1,0:T(8,128)(2,1)S(1)} %bitcast.148, f32[16,256,128]{1,2,0:T(8,128)} %fusion.47), kind=kOutput, calls=%fused_computation.40 | convolution fusion | flops 135786496 | bytes 5783552 | tf_op jit(solution)/shard_map/thd,hed->the/dot_general | solution.py:48
  52.2 0.0 copy-start
  52.2 0.0 copy-start.1
  52.3 0.2 broadcast_multiply_fusion
  52.4 0.0 copy-start.2
  52.4 1.9 copy.40
  54.3 0.0 copy-done
  54.3 0.0 copy-done.1
  54.3 2.0 multiply_reduce_fusion
  56.3 0.0 copy-done.2
  56.3 0.2 multiply_convert_fusion.2
  56.6 0.9 fusion.78
  57.5 0.9 concatenate.11
  58.4 0.0 all-gather.3.cloned.1.call-update
  58.4 0.0 all-gather.5.cloned.1.call-start
  58.5 0.7 all-gather.5.cloned.1.call-update
  59.2 0.0 reduce-scatter.3.cloned.1.call-start
  59.2 33.3 %all-gather.3.cloned.1.call-done = bf16[1024,2176]{1,0:T(8,128)(2,1)} async-done(((bf16[128,2176]{1,0:T(8,128)(2,1)}), bf16[1024,2176]{1,0:T(8,128)(2,1)}) %all-gather.3.cloned.1.call-update) | async-done | bytes 4456464 | tf_op jit(solution)/shard_map/all_gather | solution.py:88
  92.5 1.0 slice.40
  93.5 0.2 reshape.101
  93.8 0.2 fusion.62
  93.9 11.7 %fusion.11 = f32[1024,1408]{1,0:T(8,128)} fusion(bf16[1,2048,1408]{2,1,0:T(8,128)(2,1)} %param.20, bf16[1024,2176]{1,0:T(8,128)(2,1)} %all-gather.3.cloned.1.call-done), kind=kOutput, calls=%fused_computation.17 | convolution fusion | flops 5905580032 | bytes 15728640 | tf_op jit(solution)/shard_map/nd,edf->enf/dot_general | solution.py:95
  105.7 21.1 %multiply_convert_fusion.1 = bf16[1024,2048]{1,0:T(8,128)(2,1)} fusion(f32[1024]{0:T(1024)S(1)} %bitcast.154, bf16[1,1408,2048]{2,1,0:T(8,128)(2,1)} %param.21, f32[1024,1408]{1,0:T(8,128)} %fusion.11, bf16[1,2048,1408]{2,1,0:T(8,128)(2,1)} %param.19, bf16[1024,2176]{1,0:T(8,128)(2,1)} %all-gather.3.cloned.1.call-done), kind=kOutput, calls=%fused_computation.1 | convolution fusion | flops 11828199424 | bytes 25694208 | tf_op jit(solution)/shard_map/enf,efd->end/dot_general | solution.py:97
  126.8 0.0 reduce-scatter.3.cloned.1.call-update
  126.8 0.2 reduce-scatter.5.cloned.1.call-start
  127.0 0.0 all-gather.5.cloned.1.call-done
  127.0 11.7 %fusion.9 = f32[1024,1408]{1,0:T(8,128)} fusion(bf16[1024,2048]{1,0:T(8,128)(2,1)} %all-gather.5.cloned.1.call-done, bf16[1,2048,1408]{2,1,0:T(8,128)(2,1)} %param.20), kind=kOutput, calls=%fused_computation.15 | convolution fusion | flops 5905580032 | bytes 15728640 | tf_op jit(solution)/shard_map/nd,edf->enf/dot_general | solution.py:95
  138.8 0.2 fusion.60
  138.9 21.3 %multiply_convert_fusion = bf16[1024,2048]{1,0:T(8,128)(2,1)} fusion(f32[1024]{0:T(1024)S(1)} %bitcast.153, bf16[1,1408,2048]{2,1,0:T(8,128)(2,1)} %param.21, f32[1024,1408]{1,0:T(8,128)} %fusion.9, bf16[1024,2048]{1,0:T(8,128)(2,1)} %all-gather.5.cloned.1.call-done, bf16[1,2048,1408]{2,1,0:T(8,128)(2,1)} %param.19), kind=kOutput, calls=%fused_computation | convolution fusion | flops 11828199424 | bytes 25694208 | tf_op jit(solution)/shard_map/enf,efd->end/dot_general | solution.py:97
  160.2 0.0 reduce-scatter.5.cloned.1.call-update
  160.2 3.1 %reduce-scatter.3.cloned.1.call-done = bf16[128,2048]{1,0:T(8,128)(2,1)} async-done(((bf16[1024,2048]{1,0:T(8,128)(2,1)}), bf16[128,2048]{1,0:T(8,128)(2,1)}) %reduce-scatter.3.cloned.1.call-update) | async-done | bytes 524304 | tf_op jit(solution)/shard_map/reduce_scatter | solution.py:100
  163.3 39.1 %reduce-scatter.5.cloned.1.call-done = bf16[128,2048]{1,0:T(8,128)(2,1)} async-done(((bf16[1024,2048]{1,0:T(8,128)(2,1)}), bf16[128,2048]{1,0:T(8,128)(2,1)}) %reduce-scatter.5.cloned.1.call-update) | async-done | bytes 524304 | tf_op jit(solution)/shard_map/reduce_scatter | solution.py:100
  202.4 1.5 fusion.50
  203.9 1.0 maximum_bitcast_fusion
  (8 shorter events, 0.1 us)
Async XLA Ops:
  6.5 12.8 %copy-start.3 = (f32[1,256,4]{1,2,0:T(4,128)S(1)}, f32[1,256,4]{1,2,0:T(4,128)}, u32[]{:S(2)}) copy-start(f32[1,256,4]{1,2,0:T(4,128)} %param.18) | copy-start | bytes 12292
  6.5 12.8 %copy-start.4 = (s32[1,256,4]{1,2,0:T(4,128)S(1)}, s32[1,256,4]{1,2,0:T(4,128)}, u32[]{:S(2)}) copy-start(s32[1,256,4]{1,2,0:T(4,128)} %param.17) | copy-start | bytes 12292
  10.9 24.5 %all-to-all-start = ((f32[16,128,128]{2,1,0:T(8,128)}), f32[16,128,128]{2,1,0:T(8,128)S(1)}, u32[]{:S(2)}, u32[]{:S(2)}) async-start(f32[16,128,128]{2,1,0:T(8,128)} %fusion.52), calls=%async_computation | async-start | bytes 2097152 | tf_op jit(solution)/shard_map/all_to_all | solution.py:18
  36.3 13.6 %all-to-all-start.1 = ((bf16[16,128,128]{2,1,0:T(8,128)(2,1)}), bf16[16,128,128]{2,1,0:T(8,128)(2,1)}, u32[]{:S(2)}, u32[]{:S(2)}) async-start(bf16[16,128,128]{2,1,0:T(8,128)(2,1)} %reduce-window_convert_fusion), calls=%async_computation.1 | async-start | bytes 1048576 | tf_op jit(solution)/shard_map/all_to_all | solution.py:21
  40.6 51.9 %all-gather.3.cloned.1.call-start = ((), (), s32[]{:S(2)}) async-start(), calls=%async_computation.4 | async-start | bytes 5013504 | tf_op jit(solution)/shard_map/all_gather | solution.py:88
  52.2 2.1 copy-start
  52.2 2.1 copy-start.1
  52.4 3.9 %copy-start.2 = (f32[2048]{0:T(1024)S(1)}, f32[2048]{0:T(1024)}, u32[]{:S(2)}) copy-start(f32[2048]{0:T(1024)} %param.16) | copy-start | bytes 24580
  58.4 68.6 %all-gather.5.cloned.1.call-start = ((), (), s32[]{:S(2)}) async-start(), calls=%async_computation.6 | async-start | bytes 4718592 | tf_op jit(solution)/shard_map/all_gather | solution.py:88
  59.2 104.1 %reduce-scatter.3.cloned.1.call-start = ((), (), s32[]{:S(2)}) async-start(), calls=%async_computation.5 | async-start | bytes 4718592 | tf_op jit(solution)/shard_map/reduce_scatter | solution.py:100
  126.8 75.6 %reduce-scatter.5.cloned.1.call-start = ((), (), s32[]{:S(2)}) async-start(), calls=%async_computation.7 | async-start | bytes 4718592 | tf_op jit(solution)/shard_map/reduce_scatter | solution.py:100
Sparse Core Ops, SparseCore 0:
  58.6 33.8 all-gather.2
  94.2 32.0 all-gather.4
  128.7 34.5 reduce-scatter.2
  165.6 36.7 reduce-scatter.4

commit v11 on v10

--- a/solution.py
+++ b/solution.py
@@ -45,18 +45,24 @@
     scores = jnp.einsum("thd,uhd->htu", queries, key_rows, preferred_element_type=jnp.float32)
     weights = jnp.where(causal[None], scores, 0.0).astype(jnp.bfloat16)
     inner = jnp.einsum("htu,uhd->thd", weights, value_rows, preferred_element_type=jnp.float32)
-    outer_product = jnp.einsum(
-        "thd,hed->the", queries, prefix, preferred_element_type=jnp.float32
-    )
-    mixed = inner + outer_product
-    mean_square = jnp.mean(mixed * mixed, axis=-1, keepdims=True)
-    attn = (mixed * lax.rsqrt(mean_square + 1e-06)).reshape(positions, D) * head_gain
-    attn = with_layout_constraint(attn, Layout(major_to_minor=(0, 1)))
-    resid_float = (
-        (residual_in[0].astype(jnp.float32) + attn).astype(jnp.bfloat16).astype(jnp.float32)
-    )
-    row_square = jnp.mean(resid_float * resid_float, axis=-1, keepdims=True)
-    normed = (resid_float * lax.rsqrt(row_square + 1e-06) * norm_gain).astype(jnp.bfloat16)
+    def finish(t0, t1, after=None):
+        q, own_inner, state_prefix, own_resid = queries[t0:t1], inner[t0:t1], prefix, residual_in[0, t0:t1]
+        if after is not None:
+            after, q, own_inner, state_prefix, own_resid = lax.optimization_barrier(
+                (after, q, own_inner, state_prefix, own_resid))
+        outer_product = jnp.einsum(
+            "thd,hed->the", q, state_prefix, preferred_element_type=jnp.float32
+        )
+        mixed = own_inner + outer_product
+        mean_square = jnp.mean(mixed * mixed, axis=-1, keepdims=True)
+        attn = (mixed * lax.rsqrt(mean_square + 1e-06)).reshape(t1 - t0, D) * head_gain
+        attn = with_layout_constraint(attn, Layout(major_to_minor=(0, 1)))
+        resid = (
+            (own_resid.astype(jnp.float32) + attn).astype(jnp.bfloat16).astype(jnp.float32)
+        )
+        row_square = jnp.mean(resid * resid, axis=-1, keepdims=True)
+        normed = (resid * lax.rsqrt(row_square + 1e-06) * norm_gain).astype(jnp.bfloat16)
+        return resid, normed, after
 
     route_ids = expert_ids[0]
     route_gates = gate_probs[0]
@@ -80,11 +86,18 @@
     columns = jnp.arange(3 * EXPERTS, dtype=jnp.int32) % EXPERTS
     select = (columns[:, None] == me * local_count + jnp.arange(local_count)[None, :]).astype(jnp.bfloat16)
     chunk = positions // CHUNKS
+    finished = []
+    parts = []
+    for c in range(CHUNKS):
+        resid, normed, held = finish(c * chunk, (c + 1) * chunk, parts[-1] if parts else None)
+        if held is not None:
+            parts[-1] = held
+        part = normed if c else jnp.concatenate([normed, packed, pad], axis=1)
+        finished.append(resid)
+        parts.append(part)
     outs = []
     for c in range(CHUNKS):
-        part = normed[c * chunk:(c + 1) * chunk]
-        if c == 0:
-            part = jnp.concatenate([part, packed, pad], axis=1)
+        part = parts[c]
         gathered = lax.all_gather(part, "exp", axis=0, tiled=True)
         if c == 0:
             all_codes = gathered[:, D:D + width].reshape(groups, positions, 3 * EXPERTS)
@@ -98,7 +111,7 @@
         result = result.astype(jnp.bfloat16).astype(jnp.float32)
         contrib = jnp.sum(result * weight.T[:, :, None], axis=0).astype(jnp.bfloat16)
         combined = lax.psum_scatter(contrib, "exp", scatter_dimension=0, tiled=True)
-        own = resid_float[c * chunk:(c + 1) * chunk]
+        own = finished[c]
         outs.append((own + combined.astype(jnp.float32)).astype(jnp.bfloat16))
     return jnp.concatenate(outs, axis=0)[None]
 

time: 214 us -> 214 us (level)
  waiting for transfers between devices: 97 us -> 85.3 us
  local copies, waits for them, and re-layouts: 9.6 us -> 15.5 us
  other arithmetic: 5.87 us -> 10.6 us
    all_to_all x1, waiting for transfers between devices: 16 us -> 10.9 us  [block_prefix(): lax.all_to_all(pieces, 'seq', split_axis=0, concat_axis=0, tiled=True)]
    unnamed x12 -> x21, local copies, waits for them, and re-layouts: 2.93 us -> 7.65 us
    all_gather x2, waiting for transfers between devices: 33.3 us -> 28.6 us  [on_device(): gathered = lax.all_gather(part, 'exp', axis=0, tiled=True)]
  transfers between devices with their start and end apart: 6 -> 6, of which waited for: 5 -> 5; matrix products, arithmetic and copies ran while one was open for 34% -> 39% of each run, Pallas kernels for 0% -> 0%
where the time goes in v11:
time: 214 us; the launch traced here: 211 us
  waiting for transfers between devices  85.3 us (40%)
  matrix products  73.2 us (34%)
  local copies, waits for them, and re-layouts  15.5 us (7%)
  between operations  13.4 us (6%)
  starting transfers between devices  13.2 us (6%)
  other arithmetic  10.6 us (5%)
    dot_general x2, matrix products, on_device(): jnp.einsum('enf,efd->end', hidden, w_down, preferred_element_type=jnp.flo...  42.3 us
    reduce_scatter x2, waiting for transfers between devices, on_device(): combined = lax.psum_scatter(contrib, 'exp', scatter_dimension=0, tiled=True)  41 us
    all_gather x2, waiting for transfers between devices, on_device(): gathered = lax.all_gather(part, 'exp', axis=0, tiled=True)  28.6 us
    dot_general x2, matrix products, on_device(): jnp.einsum('nd,edf->enf', rows, w_up, preferred_element_type=jnp.float32)  23.4 us
    all_to_all x1, waiting for transfers between devices, block_prefix(): lax.all_to_all(pieces, 'seq', split_axis=0, concat_axis=0, tiled=True)  10.9 us
    all_to_all x1, starting transfers between devices, block_prefix(): lax.all_to_all(pieces, 'seq', split_axis=0, concat_axis=0, tiled=True)  8.47 us
    unnamed x21, local copies, waits for them, and re-layouts  7.65 us
    all_to_all x1, waiting for transfers between devices, block_prefix(): lax.all_to_all(prefixes, 'seq', split_axis=0, concat_axis=0, tiled=True)  4.73 us
  transfers between devices with their start and end apart: 6, of which 5 were waited for; matrix products, arithmetic and copies ran while one was open for 39% of the time, Pallas kernels for 0%

profile of v11, /device:TPU:1, one launch (start us, length us, event | category | flops | bytes accessed | tf_op | source)
XLA Modules:
  0.0 211.3 jit_solution(8804594870574339132)
XLA Ops:
  6.5 1.6 copy.57
  8.1 1.5 copy.60
  9.6 0.0 copy-start.1
  9.6 1.0 copy-done.1
  10.5 1.4 fusion.62
  12.0 8.5 %all-to-all-start = ((f32[16,128,128]{2,1,0:T(8,128)}), f32[16,128,128]{2,1,0:T(8,128)}, u32[]{:S(2)}, u32[]{:S(2)}) async-start(f32[16,128,128]{2,1,0:T(8,128)} %fusion.62), calls=%async_computation | async-start | bytes 2097152 | tf_op jit(solution)/shard_map/all_to_all | solution.py:18
  20.4 0.0 copy-done.7
  20.5 0.0 copy-done.6
  20.5 0.0 copy-done.2
  20.5 1.2 copy.59
  21.7 1.0 slice_bitcast_fusion.1
  22.8 2.9 %fusion.47 = f32[256,16,128]{0,2,1:T(8,128)S(1)} fusion(bf16[256,16,128]{0,2,1:T(8,128)(2,1)S(1)} %bitcast.159, pred[256,256]{1,0:T(8,128)(4,1)S(1)} %iota_compare_fusion, bf16[256,16,128]{2,1,0:T(8,128)(2,1)} %bitcast.168, bf16[256,16,128]{2,1,0:T(8,128)(2,1)} %bitcast.161), kind=kOutput, calls=%fused_computation.36 | convolution fusion | flops 538968064 | bytes 5308416 | tf_op jit(solution)/shard_map/htu,uhd->thd/dot_general | solution.py:47
  25.7 0.0 copy-start
  25.7 0.0 copy-start.3
  25.7 10.9 %all-to-all-done = f32[16,128,128]{2,1,0:T(8,128)} async-done(((f32[16,128,128]{2,1,0:T(8,128)}), f32[16,128,128]{2,1,0:T(8,128)}, u32[]{:S(2)}, u32[]{:S(2)}) %all-to-all-start) | async-done | bytes 1048608 | tf_op jit(solution)/shard_map/all_to_all | solution.py:18
  36.5 2.1 reduce-window_convert_fusion
  38.6 4.2 %all-to-all-start.1 = ((bf16[16,128,128]{2,1,0:T(8,128)(2,1)}), bf16[16,128,128]{2,1,0:T(8,128)(2,1)S(1)}, u32[]{:S(2)}, u32[]{:S(2)}) async-start(bf16[16,128,128]{2,1,0:T(8,128)(2,1)} %reduce-window_convert_fusion), calls=%async_computation.1 | async-start | bytes 1048576 | tf_op jit(solution)/shard_map/all_to_all | solution.py:21
  42.8 0.0 all-gather.3.cloned.1.call-start
  42.9 2.0 copy.58
  44.9 0.1 copy.51
  45.0 0.1 reshape.117
  45.2 0.0 copy-start.4
  45.2 0.0 copy-done.3
  45.2 0.0 copy-start.5
  45.2 0.9 copy.61
  46.1 1.9 slice_bitcast_fusion
  48.0 4.7 %all-to-all-done.1 = bf16[16,128,128]{2,1,0:T(8,128)(2,1)S(1)} async-done(((bf16[16,128,128]{2,1,0:T(8,128)(2,1)}), bf16[16,128,128]{2,1,0:T(8,128)(2,1)S(1)}, u32[]{:S(2)}, u32[]{:S(2)}) %all-to-all-start.1) | async-done | bytes 524320 | tf_op jit(solution)/shard_map/all_to_all | solution.py:21
  52.7 1.3 multiply_reduce_fusion.1
  54.1 1.1 broadcast_multiply_fusion.1
  55.2 0.0 copy-done
  55.2 1.6 copy.55
  56.8 0.0 copy-done.4
  56.8 1.3 fusion.50
  58.2 0.0 copy-done.5
  58.2 0.2 fusion.52
  58.4 0.9 concatenate.11
  59.3 0.0 all-gather.3.cloned.1.call-update
  59.3 0.0 all-gather.5.cloned.1.call-start
  59.4 0.0 slice-done
  59.4 1.5 multiply_reduce_fusion
  61.0 0.1 broadcast_multiply_fusion
  61.1 0.3 copy.56
  61.4 1.3 fusion.54
  62.7 1.1 fusion.56
  63.8 0.0 all-gather.5.cloned.1.call-update
  63.8 0.2 reduce-scatter.3.cloned.1.call-start
  64.0 28.6 %all-gather.3.cloned.1.call-done = bf16[1024,2176]{1,0:T(8,128)(2,1)} async-done(((bf16[128,2176]{1,0:T(8,128)(2,1)}), bf16[1024,2176]{1,0:T(8,128)(2,1)}) %all-gather.3.cloned.1.call-update) | async-done | bytes 4456464 | tf_op jit(solution)/shard_map/all_gather | solution.py:101
  92.6 1.0 slice.56
  93.6 0.2 reshape.122
  93.9 0.2 fusion.70
  94.1 11.7 %fusion.11 = f32[1024,1408]{1,0:T(8,128)} fusion(bf16[1,2048,1408]{2,1,0:T(8,128)(2,1)} %param.20, bf16[1024,2176]{1,0:T(8,128)(2,1)} %all-gather.3.cloned.1.call-done), kind=kOutput, calls=%fused_computation.17 | convolution fusion | flops 5905580032 | bytes 15728640 | tf_op jit(solution)/shard_map/nd,edf->enf/dot_general | solution.py:108
  105.8 21.1 %multiply_convert_fusion.1 = bf16[1024,2048]{1,0:T(8,128)(2,1)} fusion(f32[1024]{0:T(1024)S(1)} %bitcast.172, bf16[1,1408,2048]{2,1,0:T(8,128)(2,1)} %param.21, f32[1024,1408]{1,0:T(8,128)} %fusion.11, bf16[1,2048,1408]{2,1,0:T(8,128)(2,1)} %param.19, bf16[1024,2176]{1,0:T(8,128)(2,1)} %all-gather.3.cloned.1.call-done), kind=kOutput, calls=%fused_computation.1 | convolution fusion | flops 11828199424 | bytes 25694208 | tf_op jit(solution)/shard_map/enf,efd->end/dot_general | solution.py:110
  126.8 0.0 reduce-scatter.3.cloned.1.call-update
  126.8 0.3 reduce-scatter.5.cloned.1.call-start
  127.1 0.0 all-gather.5.cloned.1.call-done
  127.1 11.7 %fusion.9 = f32[1024,1408]{1,0:T(8,128)} fusion(bf16[1024,2048]{1,0:T(8,128)(2,1)} %all-gather.5.cloned.1.call-done, bf16[1,2048,1408]{2,1,0:T(8,128)(2,1)} %param.20), kind=kOutput, calls=%fused_computation.15 | convolution fusion | flops 5905580032 | bytes 15728640 | tf_op jit(solution)/shard_map/nd,edf->enf/dot_general | solution.py:108
  138.8 0.2 fusion.68
  139.0 21.3 %multiply_convert_fusion = bf16[1024,2048]{1,0:T(8,128)(2,1)} fusion(f32[1024]{0:T(1024)S(1)} %bitcast.171, bf16[1,1408,2048]{2,1,0:T(8,128)(2,1)} %param.21, f32[1024,1408]{1,0:T(8,128)} %fusion.9, bf16[1024,2048]{1,0:T(8,128)(2,1)} %all-gather.5.cloned.1.call-done, bf16[1,2048,1408]{2,1,0:T(8,128)(2,1)} %param.19), kind=kOutput, calls=%fused_computation | convolution fusion | flops 11828199424 | bytes 25694208 | tf_op jit(solution)/shard_map/enf,efd->end/dot_general | solution.py:110
  160.2 0.0 reduce-scatter.5.cloned.1.call-update
  160.3 3.2 %reduce-scatter.3.cloned.1.call-done = bf16[128,2048]{1,0:T(8,128)(2,1)} async-done(((bf16[1024,2048]{1,0:T(8,128)(2,1)}), bf16[128,2048]{1,0:T(8,128)(2,1)}) %reduce-scatter.3.cloned.1.call-update) | async-done | bytes 524304 | tf_op jit(solution)/shard_map/reduce_scatter | solution.py:113
  163.4 1.2 fusion.53
  164.6 37.9 %reduce-scatter.5.cloned.1.call-done = bf16[128,2048]{1,0:T(8,128)(2,1)} async-done(((bf16[1024,2048]{1,0:T(8,128)(2,1)}), bf16[128,2048]{1,0:T(8,128)(2,1)}) %reduce-scatter.5.cloned.1.call-update) | async-done | bytes 524304 | tf_op jit(solution)/shard_map/reduce_scatter | solution.py:113
  202.5 1.2 fusion.57
  203.7 1.1 maximum_bitcast_fusion
  (14 shorter events, 0.1 us)
Async XLA Ops:
  6.5 13.9 %copy-start.7 = (s32[1,256,4]{1,2,0:T(4,128)S(1)}, s32[1,256,4]{1,2,0:T(4,128)}, u32[]{:S(2)}) copy-start(s32[1,256,4]{1,2,0:T(4,128)} %param.17) | copy-start | bytes 12292
  6.5 13.9 %copy-start.6 = (f32[1,256,4]{1,2,0:T(4,128)S(1)}, f32[1,256,4]{1,2,0:T(4,128)}, u32[]{:S(2)}) copy-start(f32[1,256,4]{1,2,0:T(4,128)} %param.18) | copy-start | bytes 12292
  6.5 13.9 %copy-start.2 = (bf16[1,256,2048]{2,1,0:T(8,128)(2,1)S(1)}, bf16[1,256,2048]{2,1,0:T(8,128)(2,1)}, u32[]{:S(2)}) copy-start(bf16[1,256,2048]{2,1,0:T(8,128)(2,1)} %param.12) | copy-start | bytes 3145732
  9.6 1.0 copy-start.1
  12.0 24.6 %all-to-all-start = ((f32[16,128,128]{2,1,0:T(8,128)}), f32[16,128,128]{2,1,0:T(8,128)}, u32[]{:S(2)}, u32[]{:S(2)}) async-start(f32[16,128,128]{2,1,0:T(8,128)} %fusion.62), calls=%async_computation | async-start | bytes 2097152 | tf_op jit(solution)/shard_map/all_to_all | solution.py:18
  25.7 29.5 %copy-start = (f32[256,16,128]{0,2,1:T(8,128)}, f32[256,16,128]{0,2,1:T(8,128)S(1)}, u32[]{:S(2)}) copy-start(f32[256,16,128]{0,2,1:T(8,128)S(1)} %fusion.47) | copy-start | bytes 6291460
  25.7 19.5 %copy-start.3 = (bf16[16,8,16,128]{3,1,2,0:T(8,128)(2,1)S(1)}, bf16[16,8,16,128]{3,1,2,0:T(8,128)(2,1)}, u32[]{:S(2)}) copy-start(bf16[16,8,16,128]{3,1,2,0:T(8,128)(2,1)} %get-tuple-element.19) | copy-start | bytes 1572868
  38.6 14.1 %all-to-all-start.1 = ((bf16[16,128,128]{2,1,0:T(8,128)(2,1)}), bf16[16,128,128]{2,1,0:T(8,128)(2,1)S(1)}, u32[]{:S(2)}, u32[]{:S(2)}) async-start(bf16[16,128,128]{2,1,0:T(8,128)(2,1)} %reduce-window_convert_fusion), calls=%async_computation.1 | async-start | bytes 1048576 | tf_op jit(solution)/shard_map/all_to_all | solution.py:21
  42.8 49.8 %all-gather.3.cloned.1.call-start = ((), (), s32[]{:S(2)}) async-start(), calls=%async_computation.4 | async-start | bytes 5013504 | tf_op jit(solution)/shard_map/all_gather | solution.py:101
  45.2 11.7 %copy-start.4 = (f32[2048]{0:T(1024)S(1)}, f32[2048]{0:T(1024)}, u32[]{:S(2)}) copy-start(f32[2048]{0:T(1024)} %param.15) | copy-start | bytes 24580
  45.2 13.0 %copy-start.5 = (f32[2048]{0:T(1024)S(1)}, f32[2048]{0:T(1024)}, u32[]{:S(2)}) copy-start(f32[2048]{0:T(1024)} %param.16) | copy-start | bytes 24580
  55.2 4.2 %slice-start = ((f32[256,16,128]{0,2,1:T(8,128)}), f32[128,16,128]{0,2,1:T(8,128)S(1)}, s32[]{:S(2)}) async-start(f32[256,16,128]{0,2,1:T(8,128)} %copy-done), calls=%async_computation.8 | async-start | bytes 2097152 | tf_op jit(solution)/shard_map/slice | solution.py:49
  59.3 67.8 %all-gather.5.cloned.1.call-start = ((), (), s32[]{:S(2)}) async-start(), calls=%async_computation.6 | async-start | bytes 4718592 | tf_op jit(solution)/shard_map/all_gather | solution.py:101
  63.8 99.6 %reduce-scatter.3.cloned.1.call-start = ((), (), s32[]{:S(2)}) async-start(), calls=%async_computation.5 | async-start | bytes 4718592 | tf_op jit(solution)/shard_map/reduce_scatter | solution.py:113
  126.8 75.7 %reduce-scatter.5.cloned.1.call-start = ((), (), s32[]{:S(2)}) async-start(), calls=%async_computation.7 | async-start | bytes 4718592 | tf_op jit(solution)/shard_map/reduce_scatter | solution.py:113
Sparse Core Ops, SparseCore 0:
  59.5 33.1 all-gather.2
  94.3 32.0 all-gather.4
  128.8 34.5 reduce-scatter.2
  165.7 36.7 reduce-scatter.4
